TPU v7x, 256 devices: a whole 4x4x8 slice. The times are simulated.
256 devices in a mesh: seq: 64 (over y_hi, x, z), chan: 4 (over y_lo, core).
Axes of the slice: x: 4, y: 4 (y_hi: 2, y_lo: 2; y = y_hi * 2 + y_lo), z: 8, core: 2. Of those that a mesh axis runs over, the one named last changes fastest.
Arguments:
- value_in: bfloat16 [24576, 4096], P('seq', 'chan'), may hold values from -6 to 6
- gate_in: bfloat16 [24576, 4096], P('seq', 'chan'), may hold values from -6 to 6
- gate_out: bfloat16 [24576, 4096], P('seq', 'chan'), may hold values from -6 to 6
- spectral_filter: bfloat16 [24576, 4096], P('seq', 'chan'), may hold values from -6 to 6
- analysis_blocks: bfloat16 [3, 128, 128], replicated, may hold values from -0.5 to 0.5
- analysis_mix: bfloat16 [128, 3, 3], replicated, may hold values from -3.5 to 3.5
- synthesis_blocks: bfloat16 [3, 128, 128], replicated, may hold values from -0.5 to 0.5
- synthesis_mix: bfloat16 [128, 3, 3], replicated, may hold values from -3.5 to 3.5
- angles: float32 [6, 384], replicated, may hold values from -3.140625 to 3.140625
- out_weight: bfloat16 [4096, 4096], P('chan'), may hold values from -0.09375 to 0.09375
Outputs:
- projected: bfloat16 [24576, 4096], P(('seq', 'chan'))
All inputs are finite; a program needn't handle non-finite values.
Results may differ from a plain program's by a relative error of at most 0.02.
Values may be sent and summed in bfloat16 or wider, within the bound.
No kernel may reach another device: no remote copies, remote signals or barrier semaphores. Data moves between devices by JAX's collectives and lax.ppermute only.
A program may use at most 64 MiB of HBM per device.

v0:
```python
import jax
import jax.numpy as jnp
from jax import lax
from jax.sharding import PartitionSpec as P


def from_partner(value, axis, distance):
    mask = 2**distance
    pairs = [(source, source ^ mask) for source in range(lax.axis_size(axis))]
    return lax.ppermute(value, axis, pairs)


def rotate_pair(values, partner, theta, sign):
    cosine = jnp.cos(theta)[:, None]
    sine = sign * jnp.sin(theta)[:, None]
    return (cosine * values.astype(jnp.float32) + sine * partner.astype(jnp.float32)).astype(
        jnp.bfloat16
    )


def per_device(
    value_in,
    gate_in,
    gate_out,
    spectral_filter,
    analysis_blocks,
    analysis_mix,
    synthesis_blocks,
    synthesis_mix,
    angles,
    out_weight,
):
    tokens, chans = value_in.shape
    nblocks = analysis_blocks.shape[0]
    blk = analysis_blocks.shape[1]
    mixed = (
        (gate_in.astype(jnp.float32) * value_in.astype(jnp.float32))
        .astype(jnp.bfloat16)
        .reshape(nblocks, blk, chans)
    )
    inner = jnp.einsum(
        "kij,kjc->kic", analysis_blocks, mixed, preferred_element_type=jnp.float32
    ).astype(jnp.bfloat16)
    spec = jnp.einsum(
        "ikl,lic->kic", analysis_mix, inner, preferred_element_type=jnp.float32
    ).astype(jnp.bfloat16)
    spec = spec.reshape(tokens, chans)
    count = lax.axis_size("seq")
    sections = count.bit_length() - 1
    rank = lax.axis_index("seq")
    for section in range(sections):
        sign = 1.0 - 2.0 * (rank >> section & 1).astype(jnp.float32)
        partner = from_partner(spec, "seq", section)
        spec = rotate_pair(spec, partner, angles[section], sign)
    spec = (spec.astype(jnp.float32) * spectral_filter.astype(jnp.float32)).astype(jnp.bfloat16)
    for section in reversed(range(sections)):
        sign = 2.0 * (rank >> section & 1).astype(jnp.float32) - 1.0
        partner = from_partner(spec, "seq", section)
        spec = rotate_pair(spec, partner, angles[section], sign)
    grid = spec.reshape(nblocks, blk, chans)
    spread = jnp.einsum(
        "ikl,lic->kic", synthesis_mix, grid, preferred_element_type=jnp.float32
    ).astype(jnp.bfloat16)
    conv = jnp.einsum("kij,kjc->kic", synthesis_blocks, spread, preferred_element_type=jnp.float32)
    gated = (gate_out.astype(jnp.float32) * conv.reshape(tokens, chans)).astype(jnp.bfloat16)
    return lax.psum_scatter(
        jnp.dot(gated, out_weight, preferred_element_type=jnp.float32).astype(jnp.bfloat16),
        "chan",
        scatter_dimension=0,
        tiled=True,
    )


def solution(mesh):
    placed = (
        P("seq", "chan"),
        P("seq", "chan"),
        P("seq", "chan"),
        P("seq", "chan"),
        P(),
        P(),
        P(),
        P(),
        P(),
        P("chan", None),
    )
    return jax.shard_map(
        per_device, mesh=mesh, in_specs=placed, out_specs=P(("seq", "chan"), None), check_vma=False
    )
```

profile of v0, /device:TPU:1, one launch (start us, length us, event | category | flops | bytes accessed | tf_op | source)
XLA Modules:
  0.0 351.7 jit_solution(5382856138816548225)
XLA Ops:
  7.4 1.7 multiply_convert_fusion.1
  11.5 2.5 collective-permute-start
  14.6 15.6 %collective-permute-done = bf16[384,1024]{1,0:T(8,128)(2,1)S(1)} collective-permute-done((bf16[384,1024]{1,0:T(8,128)(2,1)S(1)}, bf16[384,1024]{1,0:T(8,128)(2,1)S(1)}, u32[]{:S(2)}, u32[]{:S(2)}) %collective-permute-start) | collective-permute-done | bytes 786464 | tf_op jit(solution)/shard_map/ppermute | solution.py:10
  30.6 4.0 %collective-permute-start.1 = (bf16[384,1024]{1,0:T(8,128)(2,1)S(1)}, bf16[384,1024]{1,0:T(8,128)(2,1)S(1)}, u32[]{:S(2)}, u32[]{:S(2)}) collective-permute-start(bf16[384,1024]{1,0:T(8,128)(2,1)S(1)} %add_convert_fusion.11), channel_id=1, source_target_pairs={{0,8},{4,12},{8,0},{12,4},{16,24},{20,28},{24,16},{28,20},{32,40},... | collective-permute-start | bytes 2359304 | tf_op jit(solution)/shard_map/ppermute | solution.py:10
  34.6 33.9 %collective-permute-done.1 = bf16[384,1024]{1,0:T(8,128)(2,1)S(1)} collective-permute-done((bf16[384,1024]{1,0:T(8,128)(2,1)S(1)}, bf16[384,1024]{1,0:T(8,128)(2,1)S(1)}, u32[]{:S(2)}, u32[]{:S(2)}) %collective-permute-start.1) | collective-permute-done | bytes 786464 | tf_op jit(solution)/shard_map/ppermute | solution.py:10
  68.8 6.6 %collective-permute-start.2 = (bf16[384,1024]{1,0:T(8,128)(2,1)S(1)}, bf16[384,1024]{1,0:T(8,128)(2,1)S(1)}, u32[]{:S(2)}, u32[]{:S(2)}) collective-permute-start(bf16[384,1024]{1,0:T(8,128)(2,1)S(1)} %add_convert_fusion.10), channel_id=1, source_target_pairs={{0,16},{4,20},{8,24},{12,28},{16,0},{20,4},{24,8},{28,12},{32,48},... | collective-permute-start | bytes 2359304 | tf_op jit(solution)/shard_map/ppermute | solution.py:10
  75.4 34.1 %collective-permute-done.2 = bf16[384,1024]{1,0:T(8,128)(2,1)S(1)} collective-permute-done((bf16[384,1024]{1,0:T(8,128)(2,1)S(1)}, bf16[384,1024]{1,0:T(8,128)(2,1)S(1)}, u32[]{:S(2)}, u32[]{:S(2)}) %collective-permute-start.2) | collective-permute-done | bytes 786464 | tf_op jit(solution)/shard_map/ppermute | solution.py:10
  109.9 1.3 collective-permute-start.3
  111.1 16.3 %collective-permute-done.3 = bf16[384,1024]{1,0:T(8,128)(2,1)S(1)} collective-permute-done((bf16[384,1024]{1,0:T(8,128)(2,1)S(1)}, bf16[384,1024]{1,0:T(8,128)(2,1)S(1)}, u32[]{:S(2)}, u32[]{:S(2)}) %collective-permute-start.3) | collective-permute-done | bytes 786464 | tf_op jit(solution)/shard_map/ppermute | solution.py:10
  127.8 2.8 collective-permute-start.4
  130.6 15.5 %collective-permute-done.4 = bf16[384,1024]{1,0:T(8,128)(2,1)S(1)} collective-permute-done((bf16[384,1024]{1,0:T(8,128)(2,1)S(1)}, bf16[384,1024]{1,0:T(8,128)(2,1)S(1)}, u32[]{:S(2)}, u32[]{:S(2)}) %collective-permute-start.4) | collective-permute-done | bytes 786464 | tf_op jit(solution)/shard_map/ppermute | solution.py:10
  146.5 3.0 collective-permute-start.5
  149.4 14.4 %collective-permute-done.5 = bf16[384,1024]{1,0:T(8,128)(2,1)S(1)} collective-permute-done((bf16[384,1024]{1,0:T(8,128)(2,1)S(1)}, bf16[384,1024]{1,0:T(8,128)(2,1)S(1)}, u32[]{:S(2)}, u32[]{:S(2)}) %collective-permute-start.5) | collective-permute-done | bytes 786464 | tf_op jit(solution)/shard_map/ppermute | solution.py:10
  164.3 3.0 collective-permute-start.6
  167.3 13.6 %collective-permute-done.6 = bf16[384,1024]{1,0:T(8,128)(2,1)S(1)} collective-permute-done((bf16[384,1024]{1,0:T(8,128)(2,1)S(1)}, bf16[384,1024]{1,0:T(8,128)(2,1)S(1)}, u32[]{:S(2)}, u32[]{:S(2)}) %collective-permute-start.6) | collective-permute-done | bytes 786464 | tf_op jit(solution)/shard_map/ppermute | solution.py:10
  181.2 2.7 collective-permute-start.7
  184.0 13.0 %collective-permute-done.7 = bf16[384,1024]{1,0:T(8,128)(2,1)S(1)} collective-permute-done((bf16[384,1024]{1,0:T(8,128)(2,1)S(1)}, bf16[384,1024]{1,0:T(8,128)(2,1)S(1)}, u32[]{:S(2)}, u32[]{:S(2)}) %collective-permute-start.7) | collective-permute-done | bytes 786464 | tf_op jit(solution)/shard_map/ppermute | solution.py:10
  197.3 1.2 collective-permute-start.8
  198.5 15.6 %collective-permute-done.8 = bf16[384,1024]{1,0:T(8,128)(2,1)S(1)} collective-permute-done((bf16[384,1024]{1,0:T(8,128)(2,1)S(1)}, bf16[384,1024]{1,0:T(8,128)(2,1)S(1)}, u32[]{:S(2)}, u32[]{:S(2)}) %collective-permute-start.8) | collective-permute-done | bytes 786464 | tf_op jit(solution)/shard_map/ppermute | solution.py:10
  215.5 33.2 %collective-permute-done.9 = bf16[384,1024]{1,0:T(8,128)(2,1)S(1)} collective-permute-done((bf16[384,1024]{1,0:T(8,128)(2,1)S(1)}, bf16[384,1024]{1,0:T(8,128)(2,1)S(1)}, u32[]{:S(2)}, u32[]{:S(2)}) %collective-permute-start.9) | collective-permute-done | bytes 786464 | tf_op jit(solution)/shard_map/ppermute | solution.py:10
  249.2 28.5 %collective-permute-done.10 = bf16[384,1024]{1,0:T(8,128)(2,1)S(1)} collective-permute-done((bf16[384,1024]{1,0:T(8,128)(2,1)S(1)}, bf16[384,1024]{1,0:T(8,128)(2,1)S(1)}, u32[]{:S(2)}, u32[]{:S(2)}) %collective-permute-start.10) | collective-permute-done | bytes 786464 | tf_op jit(solution)/shard_map/ppermute | solution.py:10
  278.4 18.2 %collective-permute-done.11 = bf16[384,1024]{1,0:T(8,128)(2,1)S(1)} collective-permute-done((bf16[384,1024]{1,0:T(8,128)(2,1)S(1)}, bf16[384,1024]{1,0:T(8,128)(2,1)S(1)}, u32[]{:S(2)}, u32[]{:S(2)}) %collective-permute-start.11) | collective-permute-done | bytes 786464 | tf_op jit(solution)/shard_map/ppermute | solution.py:10
  299.2 8.2 %convolution_convert_fusion = bf16[384,4096]{1,0:T(8,128)(2,1)} fusion(bf16[384,1024]{1,0:T(8,128)(2,1)S(1)} %fusion, bf16[1024,4096]{1,0:T(8,128)(2,1)} %param.19), kind=kOutput, calls=%fused_computation | convolution fusion | flops 3222798336 | bytes 12320768 | tf_op jit(solution)/shard_map/dot_general | solution.py:67
  307.4 37.5 %reduce-scatter.2.cloned.1.call-done = bf16[96,4096]{1,0:T(8,128)(2,1)} async-done(((bf16[384,4096]{1,0:T(8,128)(2,1)}), bf16[96,4096]{1,0:T(8,128)(2,1)}) %reduce-scatter.2.cloned.1.call-update) | async-done | bytes 786448 | tf_op jit(solution)/shard_map/reduce_scatter | solution.py:66
  (40 shorter events, 11.7 us)
Async XLA Ops:
  6.5 2.6 copy-start
  6.5 338.4 %reduce-scatter.2.cloned.1.call-start = ((), (), s32[]{:S(2)}) async-start(), calls=%async_computation.1 | async-start | bytes 3932160 | tf_op jit(solution)/shard_map/reduce_scatter | solution.py:66
  11.2 2.9 copy-start.4
  11.5 18.8 %collective-permute-start = (bf16[384,1024]{1,0:T(8,128)(2,1)S(1)}, bf16[384,1024]{1,0:T(8,128)(2,1)S(1)}, u32[]{:S(2)}, u32[]{:S(2)}) collective-permute-start(bf16[384,1024]{1,0:T(8,128)(2,1)S(1)} %bitcast.25), channel_id=1, source_target_pairs={{0,4},{4,0},{8,12},{12,8},{16,20},{20,16},{24,28},{28,24},{32,36},... | collective-permute-start | bytes 2359304 | tf_op jit(solution)/shard_map/ppermute | solution.py:10
  30.6 37.8 %collective-permute-start.1 = (bf16[384,1024]{1,0:T(8,128)(2,1)S(1)}, bf16[384,1024]{1,0:T(8,128)(2,1)S(1)}, u32[]{:S(2)}, u32[]{:S(2)}) collective-permute-start(bf16[384,1024]{1,0:T(8,128)(2,1)S(1)} %add_convert_fusion.11), channel_id=1, source_target_pairs={{0,8},{4,12},{8,0},{12,4},{16,24},{20,28},{24,16},{28,20},{32,40},... | collective-permute-start | bytes 2359304 | tf_op jit(solution)/shard_map/ppermute | solution.py:10
  68.8 40.7 %collective-permute-start.2 = (bf16[384,1024]{1,0:T(8,128)(2,1)S(1)}, bf16[384,1024]{1,0:T(8,128)(2,1)S(1)}, u32[]{:S(2)}, u32[]{:S(2)}) collective-permute-start(bf16[384,1024]{1,0:T(8,128)(2,1)S(1)} %add_convert_fusion.10), channel_id=1, source_target_pairs={{0,16},{4,20},{8,24},{12,28},{16,0},{20,4},{24,8},{28,12},{32,48},... | collective-permute-start | bytes 2359304 | tf_op jit(solution)/shard_map/ppermute | solution.py:10
  109.9 17.6 %collective-permute-start.3 = (bf16[384,1024]{1,0:T(8,128)(2,1)S(1)}, bf16[384,1024]{1,0:T(8,128)(2,1)S(1)}, u32[]{:S(2)}, u32[]{:S(2)}) collective-permute-start(bf16[384,1024]{1,0:T(8,128)(2,1)S(1)} %add_convert_fusion.9), channel_id=1, source_target_pairs={{0,32},{4,36},{8,40},{12,44},{16,48},{20,52},{24,56},{28,60},{32,0... | collective-permute-start | bytes 2359304 | tf_op jit(solution)/shard_map/ppermute | solution.py:10
  127.8 36.0 %copy-start.1 = (bf16[384,1024]{1,0:T(8,128)(2,1)S(1)}, bf16[384,1024]{1,0:T(8,128)(2,1)}, u32[]{:S(2)}) copy-start(bf16[384,1024]{1,0:T(8,128)(2,1)} %param.13) | copy-start | bytes 2359300
  127.8 18.3 %collective-permute-start.4 = (bf16[384,1024]{1,0:T(8,128)(2,1)S(1)}, bf16[384,1024]{1,0:T(8,128)(2,1)S(1)}, u32[]{:S(2)}, u32[]{:S(2)}) collective-permute-start(bf16[384,1024]{1,0:T(8,128)(2,1)S(1)} %add_convert_fusion.8), channel_id=1, source_target_pairs={{0,64},{4,68},{8,72},{12,76},{16,80},{20,84},{24,88},{28,92},{32,9... | collective-permute-start | bytes 2359304 | tf_op jit(solution)/shard_map/ppermute | solution.py:10
  146.5 17.4 %collective-permute-start.5 = (bf16[384,1024]{1,0:T(8,128)(2,1)S(1)}, bf16[384,1024]{1,0:T(8,128)(2,1)S(1)}, u32[]{:S(2)}, u32[]{:S(2)}) collective-permute-start(bf16[384,1024]{1,0:T(8,128)(2,1)S(1)} %add_convert_fusion.7), channel_id=1, source_target_pairs={{0,128},{4,132},{8,136},{12,140},{16,144},{20,148},{24,152},{28,15... | collective-permute-start | bytes 2359304 | tf_op jit(solution)/shard_map/ppermute | solution.py:10
  164.3 16.6 %collective-permute-start.6 = (bf16[384,1024]{1,0:T(8,128)(2,1)S(1)}, bf16[384,1024]{1,0:T(8,128)(2,1)S(1)}, u32[]{:S(2)}, u32[]{:S(2)}) collective-permute-start(bf16[384,1024]{1,0:T(8,128)(2,1)S(1)} %multiply_convert_fusion), channel_id=1, source_target_pairs={{0,128},{4,132},{8,136},{12,140},{16,144},{20,148},{24,152},{28,15... | collective-permute-start | bytes 2359304 | tf_op jit(solution)/shard_map/ppermute | solution.py:10
  181.2 15.7 %collective-permute-start.7 = (bf16[384,1024]{1,0:T(8,128)(2,1)S(1)}, bf16[384,1024]{1,0:T(8,128)(2,1)S(1)}, u32[]{:S(2)}, u32[]{:S(2)}) collective-permute-start(bf16[384,1024]{1,0:T(8,128)(2,1)S(1)} %add_convert_fusion.5), channel_id=1, source_target_pairs={{0,64},{4,68},{8,72},{12,76},{16,80},{20,84},{24,88},{28,92},{32,9... | collective-permute-start | bytes 2359304 | tf_op jit(solution)/shard_map/ppermute | solution.py:10
  197.3 16.9 %collective-permute-start.8 = (bf16[384,1024]{1,0:T(8,128)(2,1)S(1)}, bf16[384,1024]{1,0:T(8,128)(2,1)S(1)}, u32[]{:S(2)}, u32[]{:S(2)}) collective-permute-start(bf16[384,1024]{1,0:T(8,128)(2,1)S(1)} %add_convert_fusion.4), channel_id=1, source_target_pairs={{0,32},{4,36},{8,40},{12,44},{16,48},{20,52},{24,56},{28,60},{32,0... | collective-permute-start | bytes 2359304 | tf_op jit(solution)/shard_map/ppermute | solution.py:10
  214.5 34.2 %collective-permute-start.9 = (bf16[384,1024]{1,0:T(8,128)(2,1)S(1)}, bf16[384,1024]{1,0:T(8,128)(2,1)S(1)}, u32[]{:S(2)}, u32[]{:S(2)}) collective-permute-start(bf16[384,1024]{1,0:T(8,128)(2,1)S(1)} %add_convert_fusion.3), channel_id=1, source_target_pairs={{0,16},{4,20},{8,24},{12,28},{16,0},{20,4},{24,8},{28,12},{32,48},... | collective-permute-start | bytes 2359304 | tf_op jit(solution)/shard_map/ppermute | solution.py:10
  249.1 29.1 %copy-start.5 = (bf16[128,3,3]{0,2,1:T(4,128)(2,1)S(1)}, bf16[128,3,3]{0,2,1:T(4,128)(2,1)}, u32[]{:S(2)}) copy-start(bf16[128,3,3]{0,2,1:T(4,128)(2,1)} %param.17) | copy-start | bytes 6916
  249.1 28.6 %collective-permute-start.10 = (bf16[384,1024]{1,0:T(8,128)(2,1)S(1)}, bf16[384,1024]{1,0:T(8,128)(2,1)S(1)}, u32[]{:S(2)}, u32[]{:S(2)}) collective-permute-start(bf16[384,1024]{1,0:T(8,128)(2,1)S(1)} %add_convert_fusion.2), channel_id=1, source_target_pairs={{0,8},{4,12},{8,0},{12,4},{16,24},{20,28},{24,16},{28,20},{32,40},... | collective-permute-start | bytes 2359304 | tf_op jit(solution)/shard_map/ppermute | solution.py:10
  278.1 18.5 %collective-permute-start.11 = (bf16[384,1024]{1,0:T(8,128)(2,1)S(1)}, bf16[384,1024]{1,0:T(8,128)(2,1)S(1)}, u32[]{:S(2)}, u32[]{:S(2)}) collective-permute-start(bf16[384,1024]{1,0:T(8,128)(2,1)S(1)} %add_convert_fusion.1), channel_id=1, source_target_pairs={{0,4},{4,0},{8,12},{12,8},{16,20},{20,16},{24,28},{28,24},{32,36},... | collective-permute-start | bytes 2359304 | tf_op jit(solution)/shard_map/ppermute | solution.py:10
  296.9 0.9 copy-start.3
  297.8 1.1 copy-start.2
Sparse Core Ops, SparseCore 0:
  307.6 37.2 reduce-scatter.1
where the time goes:
time: 352 us
  waiting for transfers between devices  289 us (82%)
  starting transfers between devices  28.3 us (8%)
  between operations  13.6 us (4%)
  matrix products  10.9 us (3%)
  other arithmetic  6.78 us (2%)
    ppermute x12, waiting for transfers between devices, from_partner(): return lax.ppermute(value, axis, pairs)  252 us
    reduce_scatter x1, waiting for transfers between devices, per_device(): lax.psum_scatter(jnp.dot(gated, out_weight, preferred_element_type=jnp.fl...  37.5 us
    ppermute x12, starting transfers between devices, from_partner(): return lax.ppermute(value, axis, pairs)  28.3 us
    dot_general x1, matrix products, per_device(): jnp.dot(gated, out_weight, preferred_element_type=jnp.float32)  8.21 us
  transfers between devices with their start and end apart: 13, of which 13 were waited for; matrix products, arithmetic and copies ran while one was open for 0% of the time, Pallas kernels for 0%

commit v1 on v0

v1 whole, which is shorter than its diff:
```python
import jax
import jax.numpy as jnp
from jax import lax
from jax.sharding import PartitionSpec as P

ROW_SPLIT = 8


def to_columns(values, count):
    nb, blk, chans = values.shape
    cs = count // ROW_SPLIT
    parts = values.reshape(nb, ROW_SPLIT, blk // ROW_SPLIT, cs, chans // cs)
    parts = parts.transpose(1, 3, 0, 2, 4).reshape(count, nb, blk // ROW_SPLIT, chans // cs)
    return lax.all_to_all(parts, "seq", 0, 0, tiled=True)


def from_columns(values, count, blk, chans):
    nb = values.shape[1]
    cs = count // ROW_SPLIT
    back = lax.all_to_all(values, "seq", 0, 0, tiled=True)
    back = back.reshape(ROW_SPLIT, cs, nb, blk // ROW_SPLIT, chans // cs)
    return back.transpose(2, 0, 3, 1, 4).reshape(nb, blk, chans)


def rotate_bit(values, cosine, sine, bit, sections, sign):
    axis = sections - 1 - bit
    lower = lax.index_in_dim(values, 0, axis, keepdims=True)
    upper = lax.index_in_dim(values, 1, axis, keepdims=True)
    new_lower = cosine * lower + sign * sine * upper
    new_upper = cosine * upper - sign * sine * lower
    return jnp.concatenate([new_lower, new_upper], axis=axis)


def per_device(
    value_in,
    gate_in,
    gate_out,
    spectral_filter,
    analysis_blocks,
    analysis_mix,
    synthesis_blocks,
    synthesis_mix,
    angles,
    out_weight,
):
    tokens, chans = value_in.shape
    nblocks = analysis_blocks.shape[0]
    blk = analysis_blocks.shape[1]
    count = lax.axis_size("seq")
    sections = count.bit_length() - 1
    rank = lax.axis_index("seq")
    mixed = (
        (gate_in.astype(jnp.float32) * value_in.astype(jnp.float32))
        .astype(jnp.bfloat16)
        .reshape(nblocks, blk, chans)
    )
    inner = jnp.einsum(
        "kij,kjc->kic", analysis_blocks, mixed, preferred_element_type=jnp.float32
    ).astype(jnp.bfloat16)
    spec = jnp.einsum(
        "ikl,lic->kic", analysis_mix, inner, preferred_element_type=jnp.float32
    ).astype(jnp.bfloat16)

    spec_cols = to_columns(spec, count)
    filt_cols = to_columns(spectral_filter.reshape(nblocks, blk, chans), count)
    rows = blk // ROW_SPLIT
    row_part = rank // (count // ROW_SPLIT)
    theta = angles.reshape(sections, nblocks, ROW_SPLIT, rows)
    theta = lax.dynamic_index_in_dim(theta, row_part, axis=2, keepdims=False)
    cosines = jnp.cos(theta)[:, :, :, None]
    sines = jnp.sin(theta)[:, :, :, None]

    shape = (2,) * sections + spec_cols.shape[1:]
    work = spec_cols.astype(jnp.float32).reshape(shape)
    for section in range(sections):
        work = rotate_bit(work, cosines[section], sines[section], section, sections, 1.0)
    work = work * filt_cols.astype(jnp.float32).reshape(shape)
    for section in reversed(range(sections)):
        work = rotate_bit(work, cosines[section], sines[section], section, sections, -1.0)
    work = work.astype(jnp.bfloat16).reshape(spec_cols.shape)

    grid = from_columns(work, count, blk, chans)
    spread = jnp.einsum(
        "ikl,lic->kic", synthesis_mix, grid, preferred_element_type=jnp.float32
    ).astype(jnp.bfloat16)
    conv = jnp.einsum("kij,kjc->kic", synthesis_blocks, spread, preferred_element_type=jnp.float32)
    gated = (gate_out.astype(jnp.float32) * conv.reshape(tokens, chans)).astype(jnp.bfloat16)
    return lax.psum_scatter(
        jnp.dot(gated, out_weight, preferred_element_type=jnp.float32).astype(jnp.bfloat16),
        "chan",
        scatter_dimension=0,
        tiled=True,
    )


def solution(mesh):
    placed = (
        P("seq", "chan"),
        P("seq", "chan"),
        P("seq", "chan"),
        P("seq", "chan"),
        P(),
        P(),
        P(),
        P(),
        P(),
        P("chan", None),
    )
    return jax.shard_map(
        per_device, mesh=mesh, in_specs=placed, out_specs=P(("seq", "chan"), None), check_vma=False
    )
```

time: 352 us -> 168 us (0.48)
  waiting for transfers between devices: 289 us -> 100 us
    ppermute x12 -> x0, waiting for transfers between devices: 252 us -> none  [from_partner(): return lax.ppermute(value, axis, pairs)]
    all_to_all x0 -> x3, waiting for transfers between devices: none -> 61.9 us  [the longest x2 41.2 us: to_columns(): return lax.all_to_all(parts, 'seq', 0, 0, tiled=True)]
    all_to_all x0 -> x3, starting transfers between devices: none -> 30.3 us  [the longest x2 22.5 us: to_columns(): return lax.all_to_all(parts, 'seq', 0, 0, tiled=True)]
    ppermute x12 -> x0, starting transfers between devices: 28.3 us -> none  [from_partner(): return lax.ppermute(value, axis, pairs)]
    convert_element_type x12 -> x0, other arithmetic: 4.26 us -> none  [the longest x11 3.81 us: rotate_pair(): (cosine * values.astype(jnp.float32) + sine * partner.astype(jnp.float32)...]
  transfers between devices with their start and end apart: 13 -> 4, of which waited for: 13 -> 4; matrix products, arithmetic and copies ran while one was open for 0% -> 2% of each run, Pallas kernels for 0% -> 0%
where the time goes in v1:
time: 168 us; the launch traced here: 167 us
  waiting for transfers between devices  100 us (60%)
  starting transfers between devices  30.5 us (18%)
  between operations  13.8 us (8%)
  matrix products  10.7 us (6%)
  other arithmetic  6.79 us (4%)
  local copies, waits for them, and re-layouts  5.55 us (3%)
    all_to_all x2, waiting for transfers between devices, to_columns(): return lax.all_to_all(parts, 'seq', 0, 0, tiled=True)  41.2 us
    reduce_scatter x1, waiting for transfers between devices, per_device(): lax.psum_scatter(jnp.dot(gated, out_weight, preferred_element_type=jnp.fl...  38.2 us
    all_to_all x2, starting transfers between devices, to_columns(): return lax.all_to_all(parts, 'seq', 0, 0, tiled=True)  22.5 us
    all_to_all x1, waiting for transfers between devices, from_columns(): back = lax.all_to_all(values, 'seq', 0, 0, tiled=True)  20.8 us
    dot_general x1, matrix products, per_device(): jnp.dot(gated, out_weight, preferred_element_type=jnp.float32)  8.21 us
    all_to_all x1, starting transfers between devices, from_columns(): back = lax.all_to_all(values, 'seq', 0, 0, tiled=True)  7.84 us
  transfers between devices with their start and end apart: 4, of which 4 were waited for; matrix products, arithmetic and copies ran while one was open for 2% of the time, Pallas kernels for 0%

profile of v1, /device:TPU:1, one launch (start us, length us, event | category | flops | bytes accessed | tf_op | source)
XLA Modules:
  0.0 167.4 jit_solution(10900203405377798902)
XLA Ops:
  6.5 1.7 %multiply_convert_fusion = bf16[384,1024]{1,0:T(8,128)(2,1)S(1)} fusion(bf16[384,1024]{1,0:T(8,128)(2,1)} %param.10, bf16[384,1024]{1,0:T(8,128)(2,1)} %param.11), kind=kLoop, calls=%fused_computation.24 | loop fusion | flops 1572864 | bytes 2359296 | tf_op jit(solution)/shard_map/convert_element_type | solution.py:54
  8.3 0.4 fusion.3
  8.7 0.9 copy.19
  9.8 0.7 fusion.1
  10.5 0.7 reshape.207
  11.2 1.0 copy.22
  12.3 15.1 %all-to-all-start = ((bf16[64,3,16,128]{3,2,1,0:T(8,128)(2,1)}), bf16[64,3,16,128]{3,2,1,0:T(8,128)(2,1)S(1)}, u32[]{:S(2)}, u32[]{:S(2)}) async-start(bf16[64,3,16,128]{3,2,1,0:T(8,128)(2,1)} %bitcast.11), calls=%async_computation | async-start | bytes 1572864 | tf_op jit(solution)/shard_map/all_to_all | solution.py:14
  27.7 1.0 copy.23
  28.9 21.3 %all-to-all-done = bf16[64,3,16,128]{3,2,1,0:T(8,128)(2,1)S(1)} async-done(((bf16[64,3,16,128]{3,2,1,0:T(8,128)(2,1)}), bf16[64,3,16,128]{3,2,1,0:T(8,128)(2,1)S(1)}, u32[]{:S(2)}, u32[]{:S(2)}) %all-to-all-start) | async-done | bytes 786464 | tf_op jit(solution)/shard_map/all_to_all | solution.py:14
  50.2 7.4 %all-to-all-start.1 = ((bf16[64,3,16,128]{3,2,1,0:T(8,128)(2,1)}), bf16[64,3,16,128]{3,2,1,0:T(8,128)(2,1)S(1)}, u32[]{:S(2)}, u32[]{:S(2)}) async-start(bf16[64,3,16,128]{3,2,1,0:T(8,128)(2,1)} %bitcast.21), calls=%async_computation.1 | async-start | bytes 1572864 | tf_op jit(solution)/shard_map/all_to_all | solution.py:14
  57.8 0.3 multiply_add_fusion.10
  58.6 0.3 multiply_add_fusion.7
  59.5 19.8 %all-to-all-done.1 = bf16[64,3,16,128]{3,2,1,0:T(8,128)(2,1)S(1)} async-done(((bf16[64,3,16,128]{3,2,1,0:T(8,128)(2,1)}), bf16[64,3,16,128]{3,2,1,0:T(8,128)(2,1)S(1)}, u32[]{:S(2)}, u32[]{:S(2)}) %all-to-all-start.1) | async-done | bytes 786464 | tf_op jit(solution)/shard_map/all_to_all | solution.py:14
  79.6 0.3 multiply_add_fusion.4
  79.9 0.3 multiply_add_fusion.3
  80.8 0.3 multiply_add_fusion
  81.4 0.9 pad_maximum_fusion.10
  82.4 7.8 %all-to-all-start.2 = ((bf16[64,3,16,128]{3,2,1,0:T(8,128)(2,1)}), bf16[64,3,16,128]{3,2,1,0:T(8,128)(2,1)S(1)}, u32[]{:S(2)}, u32[]{:S(2)}) async-start(bf16[64,3,16,128]{3,2,1,0:T(8,128)(2,1)} %bitcast.23), calls=%async_computation.2 | async-start | bytes 1572864 | tf_op jit(solution)/shard_map/all_to_all | solution.py:20
  90.6 20.8 %all-to-all-done.2 = bf16[64,3,16,128]{3,2,1,0:T(8,128)(2,1)S(1)} async-done(((bf16[64,3,16,128]{3,2,1,0:T(8,128)(2,1)}), bf16[64,3,16,128]{3,2,1,0:T(8,128)(2,1)S(1)}, u32[]{:S(2)}, u32[]{:S(2)}) %all-to-all-start.2) | async-done | bytes 786464 | tf_op jit(solution)/shard_map/all_to_all | solution.py:20
  111.9 0.7 fusion.2
  112.8 0.7 fusion.14
  113.4 0.5 copy-done.2
  114.2 8.2 %convolution_convert_fusion = bf16[384,4096]{1,0:T(8,128)(2,1)} fusion(bf16[384,1024]{1,0:T(8,128)(2,1)S(1)} %fusion, bf16[1024,4096]{1,0:T(8,128)(2,1)} %param.19), kind=kOutput, calls=%fused_computation | convolution fusion | flops 3222798336 | bytes 12320768 | tf_op jit(solution)/shard_map/dot_general | solution.py:89
  122.4 38.2 %reduce-scatter.2.cloned.1.call-done = bf16[96,4096]{1,0:T(8,128)(2,1)} async-done(((bf16[384,4096]{1,0:T(8,128)(2,1)}), bf16[96,4096]{1,0:T(8,128)(2,1)}) %reduce-scatter.2.cloned.1.call-update) | async-done | bytes 786448 | tf_op jit(solution)/shard_map/reduce_scatter | solution.py:88
  (36 shorter events, 4.3 us)
Async XLA Ops:
  6.5 1.7 %copy-start = (bf16[3,128,128]{2,1,0:T(8,128)(2,1)S(1)}, bf16[3,128,128]{2,1,0:T(8,128)(2,1)}, u32[]{:S(2)}) copy-start(bf16[3,128,128]{2,1,0:T(8,128)(2,1)} %param.14) | copy-start | bytes 294916
  8.3 1.4 copy-start.5
  11.2 16.2 %copy-start.4 = (f32[6,384]{1,0:T(8,128)S(1)}, f32[6,384]{1,0:T(8,128)}, u32[]{:S(2)}) copy-start(f32[6,384]{1,0:T(8,128)} %param.18) | copy-start | bytes 27652
  11.2 16.3 %copy-start.1 = (bf16[384,1024]{1,0:T(8,128)(2,1)S(1)}, bf16[384,1024]{1,0:T(8,128)(2,1)}, u32[]{:S(2)}) copy-start(bf16[384,1024]{1,0:T(8,128)(2,1)} %param.13) | copy-start | bytes 2359300
  12.3 38.0 %all-to-all-start = ((bf16[64,3,16,128]{3,2,1,0:T(8,128)(2,1)}), bf16[64,3,16,128]{3,2,1,0:T(8,128)(2,1)S(1)}, u32[]{:S(2)}, u32[]{:S(2)}) async-start(bf16[64,3,16,128]{3,2,1,0:T(8,128)(2,1)} %bitcast.11), calls=%async_computation | async-start | bytes 1572864 | tf_op jit(solution)/shard_map/all_to_all | solution.py:14
  50.2 29.1 %all-to-all-start.1 = ((bf16[64,3,16,128]{3,2,1,0:T(8,128)(2,1)}), bf16[64,3,16,128]{3,2,1,0:T(8,128)(2,1)S(1)}, u32[]{:S(2)}, u32[]{:S(2)}) async-start(bf16[64,3,16,128]{3,2,1,0:T(8,128)(2,1)} %bitcast.21), calls=%async_computation.1 | async-start | bytes 1572864 | tf_op jit(solution)/shard_map/all_to_all | solution.py:14
  81.4 9.0 %copy-start.6 = (bf16[128,3,3]{0,2,1:T(4,128)(2,1)S(1)}, bf16[128,3,3]{0,2,1:T(4,128)(2,1)}, u32[]{:S(2)}) copy-start(bf16[128,3,3]{0,2,1:T(4,128)(2,1)} %param.17) | copy-start | bytes 6916
  82.4 29.1 %all-to-all-start.2 = ((bf16[64,3,16,128]{3,2,1,0:T(8,128)(2,1)}), bf16[64,3,16,128]{3,2,1,0:T(8,128)(2,1)S(1)}, u32[]{:S(2)}, u32[]{:S(2)}) async-start(bf16[64,3,16,128]{3,2,1,0:T(8,128)(2,1)} %bitcast.23), calls=%async_computation.2 | async-start | bytes 1572864 | tf_op jit(solution)/shard_map/all_to_all | solution.py:20
  90.2 70.4 %reduce-scatter.2.cloned.1.call-start = ((), (), s32[]{:S(2)}) async-start(), calls=%async_computation.4 | async-start | bytes 3932160 | tf_op jit(solution)/shard_map/reduce_scatter | solution.py:88
  111.9 0.9 copy-start.3
  112.8 1.1 copy-start.2
Sparse Core Ops, SparseCore 0:
  122.5 38.0 reduce-scatter.1

commit v2 on v1

--- a/solution.py
+++ b/solution.py
@@ -85,12 +85,28 @@
     ).astype(jnp.bfloat16)
     conv = jnp.einsum("kij,kjc->kic", synthesis_blocks, spread, preferred_element_type=jnp.float32)
     gated = (gate_out.astype(jnp.float32) * conv.reshape(tokens, chans)).astype(jnp.bfloat16)
-    return lax.psum_scatter(
-        jnp.dot(gated, out_weight, preferred_element_type=jnp.float32).astype(jnp.bfloat16),
-        "chan",
-        scatter_dimension=0,
-        tiled=True,
-    )
+    product = jnp.dot(gated, out_weight, preferred_element_type=jnp.float32)
+    return scatter_sum(product)
+
+
+def exchange(value, distance):
+    pairs = [(source, source ^ distance) for source in range(lax.axis_size("chan"))]
+    return lax.ppermute(value, "chan", pairs)
+
+
+def scatter_sum(product):
+    me = lax.axis_index("chan")
+    core = me % 2
+    chip = me // 2
+    rows, width = product.shape
+    quarters = product.reshape(2, 2, rows // 4, width)
+    keep = lax.dynamic_index_in_dim(quarters, core, axis=1, keepdims=False)
+    send = lax.dynamic_index_in_dim(quarters, 1 - core, axis=1, keepdims=False)
+    half = keep + exchange(send.astype(jnp.bfloat16), 1).astype(jnp.float32)
+    keep = lax.dynamic_index_in_dim(half, chip, axis=0, keepdims=False)
+    send = lax.dynamic_index_in_dim(half, 1 - chip, axis=0, keepdims=False)
+    total = keep + exchange(send.astype(jnp.bfloat16), 2).astype(jnp.float32)
+    return total.astype(jnp.bfloat16)
 
 
 def solution(mesh):

time: 168 us -> 150 us (0.89)
  waiting for transfers between devices: 100 us -> 83.6 us
  between operations: 13.8 us -> 0.41 us
  starting transfers between devices: 30.5 us -> 35.7 us
  other arithmetic: 6.79 us -> 11.6 us
  local copies, waits for them, and re-layouts: 5.55 us -> 10.1 us
  matrix products: 10.7 us -> 8.28 us
    reduce_scatter x1 -> x0, waiting for transfers between devices: 38.2 us -> none  [per_device(): lax.psum_scatter(jnp.dot(gated, out_weight, preferred_element_type=jnp.fl...]
    ppermute x0 -> x2, waiting for transfers between devices: none -> 21.7 us  [exchange(): return lax.ppermute(value, 'chan', pairs)]
    ppermute x0 -> x2, starting transfers between devices: none -> 5.24 us  [exchange(): return lax.ppermute(value, 'chan', pairs)]
    unnamed x17, local copies, waits for them, and re-layouts: 1.23 us -> 4.56 us
    add x0 -> x1, other arithmetic: none -> 2.69 us  [scatter_sum(): half = keep + exchange(send.astype(jnp.bfloat16), 1).astype(jnp.float32)]
    dot_general x1, matrix products: 8.21 us -> 5.81 us  [per_device(): product = jnp.dot(gated, out_weight, preferred_element_type=jnp.float32)]
    convert_element_type x0 -> x1, other arithmetic: none -> 2.17 us  [scatter_sum(): return total.astype(jnp.bfloat16)]
  transfers between devices with their start and end apart: 4 -> 5, of which waited for: 4 -> 5; matrix products, arithmetic and copies ran while one was open for 2% -> 2% of each run, Pallas kernels for 0% -> 0%
where the time goes in v2:
time: 150 us
  waiting for transfers between devices  83.6 us (56%)
  starting transfers between devices  35.7 us (24%)
  other arithmetic  11.6 us (8%)
  local copies, waits for them, and re-layouts  10.1 us (7%)
  matrix products  8.28 us (6%)
    all_to_all x2, waiting for transfers between devices, to_columns(): return lax.all_to_all(parts, 'seq', 0, 0, tiled=True)  41.1 us
    all_to_all x2, starting transfers between devices, to_columns(): return lax.all_to_all(parts, 'seq', 0, 0, tiled=True)  22.5 us
    ppermute x2, waiting for transfers between devices, exchange(): return lax.ppermute(value, 'chan', pairs)  21.7 us
    all_to_all x1, waiting for transfers between devices, from_columns(): back = lax.all_to_all(values, 'seq', 0, 0, tiled=True)  20.8 us
    all_to_all x1, starting transfers between devices, from_columns(): back = lax.all_to_all(values, 'seq', 0, 0, tiled=True)  8.02 us
    dot_general x1, matrix products, per_device(): product = jnp.dot(gated, out_weight, preferred_element_type=jnp.float32)  5.81 us
    ppermute x2, starting transfers between devices, exchange(): return lax.ppermute(value, 'chan', pairs)  5.24 us
    unnamed x17, local copies, waits for them, and re-layouts  4.56 us
  transfers between devices with their start and end apart: 5, of which 5 were waited for; matrix products, arithmetic and copies ran while one was open for 2% of the time, Pallas kernels for 0%

profile of v2, /device:TPU:1, one launch (start us, length us, event | category | flops | bytes accessed | tf_op | source)
XLA Modules:
  0.0 149.7 jit_solution(14930026149450687906)
XLA Ops:
  0.0 0.9 copy.22
  0.9 1.7 %multiply_convert_fusion = bf16[384,1024]{1,0:T(8,128)(2,1)S(1)} fusion(bf16[384,1024]{1,0:T(8,128)(2,1)} %param.10, bf16[384,1024]{1,0:T(8,128)(2,1)} %param.11), kind=kLoop, calls=%fused_computation.29 | loop fusion | flops 1572864 | bytes 2359296 | tf_op jit(solution)/shard_map/convert_element_type | solution.py:54
  3.0 0.9 copy.21
  3.9 0.7 fusion.3
  4.6 0.7 reshape.213
  5.4 1.0 copy.24
  6.4 15.1 %all-to-all-start = ((bf16[64,3,16,128]{3,2,1,0:T(8,128)(2,1)}), bf16[64,3,16,128]{3,2,1,0:T(8,128)(2,1)S(1)}, u32[]{:S(2)}, u32[]{:S(2)}) async-start(bf16[64,3,16,128]{3,2,1,0:T(8,128)(2,1)} %bitcast.11), calls=%async_computation | async-start | bytes 1572864 | tf_op jit(solution)/shard_map/all_to_all | solution.py:14
  21.8 1.0 copy.25
  23.0 21.3 %all-to-all-done = bf16[64,3,16,128]{3,2,1,0:T(8,128)(2,1)S(1)} async-done(((bf16[64,3,16,128]{3,2,1,0:T(8,128)(2,1)}), bf16[64,3,16,128]{3,2,1,0:T(8,128)(2,1)S(1)}, u32[]{:S(2)}, u32[]{:S(2)}) %all-to-all-start) | async-done | bytes 786464 | tf_op jit(solution)/shard_map/all_to_all | solution.py:14
  44.3 7.4 %all-to-all-start.1 = ((bf16[64,3,16,128]{3,2,1,0:T(8,128)(2,1)}), bf16[64,3,16,128]{3,2,1,0:T(8,128)(2,1)S(1)}, u32[]{:S(2)}, u32[]{:S(2)}) async-start(bf16[64,3,16,128]{3,2,1,0:T(8,128)(2,1)} %bitcast.21), calls=%async_computation.1 | async-start | bytes 1572864 | tf_op jit(solution)/shard_map/all_to_all | solution.py:14
  53.6 19.8 %all-to-all-done.1 = bf16[64,3,16,128]{3,2,1,0:T(8,128)(2,1)S(1)} async-done(((bf16[64,3,16,128]{3,2,1,0:T(8,128)(2,1)}), bf16[64,3,16,128]{3,2,1,0:T(8,128)(2,1)S(1)}, u32[]{:S(2)}, u32[]{:S(2)}) %all-to-all-start.1) | async-done | bytes 786464 | tf_op jit(solution)/shard_map/all_to_all | solution.py:14
  75.5 0.9 pad_maximum_fusion.10
  76.5 8.0 %all-to-all-start.2 = ((bf16[64,3,16,128]{3,2,1,0:T(8,128)(2,1)}), bf16[64,3,16,128]{3,2,1,0:T(8,128)(2,1)S(1)}, u32[]{:S(2)}, u32[]{:S(2)}) async-start(bf16[64,3,16,128]{3,2,1,0:T(8,128)(2,1)} %bitcast.23), calls=%async_computation.2 | async-start | bytes 1572864 | tf_op jit(solution)/shard_map/all_to_all | solution.py:20
  84.7 20.8 %all-to-all-done.2 = bf16[64,3,16,128]{3,2,1,0:T(8,128)(2,1)S(1)} async-done(((bf16[64,3,16,128]{3,2,1,0:T(8,128)(2,1)}), bf16[64,3,16,128]{3,2,1,0:T(8,128)(2,1)S(1)}, u32[]{:S(2)}, u32[]{:S(2)}) %all-to-all-start.2) | async-done | bytes 786464 | tf_op jit(solution)/shard_map/all_to_all | solution.py:20
  106.0 0.7 fusion.4
  106.9 0.7 fusion.17
  108.3 5.8 %fusion.19 = f32[384,4096]{1,0:T(8,128)S(1)} fusion(bf16[384,1024]{1,0:T(8,128)(2,1)S(1)} %fusion.1, bf16[1024,4096]{1,0:T(8,128)(2,1)} %param.19), kind=kOutput, calls=%fused_computation.105 | convolution fusion | flops 3221225472 | bytes 15466496 | tf_op jit(solution)/shard_map/dot_general | solution.py:88
  114.1 2.6 %copy-done.1 = f32[384,4096]{1,0:T(8,128)} copy-done((f32[384,4096]{1,0:T(8,128)}, f32[384,4096]{1,0:T(8,128)S(1)}, u32[]{:S(2)}) %copy-start.1) | copy-done | bytes 6291480
  116.9 4.7 %collective-permute-start = (bf16[2,96,4096]{2,1,0:T(8,128)(2,1)S(1)}, bf16[2,96,4096]{2,1,0:T(8,128)(2,1)}, u32[]{:S(2)}, u32[]{:S(2)}) collective-permute-start(bf16[2,96,4096]{2,1,0:T(8,128)(2,1)S(1)} %fusion), channel_id=1, source_target_pairs={{0,1},{1,0},{2,3},{3,2},{4,5},{5,4},{6,7},{7,6},{8,9},{9,8},{10,11... | collective-permute-start | bytes 4718600 | tf_op jit(solution)/shard_map/ppermute | solution.py:94
  121.6 3.2 %collective-permute-done = bf16[2,96,4096]{2,1,0:T(8,128)(2,1)} collective-permute-done((bf16[2,96,4096]{2,1,0:T(8,128)(2,1)S(1)}, bf16[2,96,4096]{2,1,0:T(8,128)(2,1)}, u32[]{:S(2)}, u32[]{:S(2)}) %collective-permute-start) | collective-permute-done | bytes 1572896 | tf_op jit(solution)/shard_map/ppermute | solution.py:94
  124.8 2.7 %bitcast_add_fusion = f32[2,96,4096]{2,1,0:T(8,128)S(1)} fusion(bf16[2,96,4096]{2,1,0:T(8,128)(2,1)} %collective-permute-done, f32[2,2,96,4096]{3,2,1,0:T(8,128)} %bitcast.97, s32[]{:T(128)S(6)} %select_n.35), kind=kLoop, calls=%fused_computation.1 | loop fusion | flops 1572864 | bytes 7864324 | tf_op jit(solution)/shard_map/add | solution.py:105
  127.5 1.0 fusion.6
  129.0 18.5 %collective-permute-done.1 = bf16[96,4096]{1,0:T(8,128)(2,1)} collective-permute-done((bf16[96,4096]{1,0:T(8,128)(2,1)}, bf16[96,4096]{1,0:T(8,128)(2,1)}, u32[]{:S(2)}, u32[]{:S(2)}) %collective-permute-start.1) | collective-permute-done | bytes 786464 | tf_op jit(solution)/shard_map/ppermute | solution.py:94
  147.5 2.2 %fusion.2 = bf16[96,4096]{1,0:T(8,128)(2,1)} fusion(bf16[96,4096]{1,0:T(8,128)(2,1)} %collective-permute-done.1, f32[2,96,4096]{2,1,0:T(8,128)S(1)} %bitcast_add_fusion, s32[]{:T(128)S(6)} %select_n.38), kind=kLoop, calls=%fused_computation.27 | loop fusion | flops 1179648 | bytes 3145732 | tf_op jit(solution)/shard_map/convert_element_type | solution.py:109
  (41 shorter events, 7.0 us)
Async XLA Ops:
  0.0 2.6 %copy-start = (bf16[3,128,128]{2,1,0:T(8,128)(2,1)S(1)}, bf16[3,128,128]{2,1,0:T(8,128)(2,1)}, u32[]{:S(2)}) copy-start(bf16[3,128,128]{2,1,0:T(8,128)(2,1)} %param.14) | copy-start | bytes 294916
  5.3 16.2 %copy-start.5 = (f32[6,384]{1,0:T(8,128)S(1)}, f32[6,384]{1,0:T(8,128)}, u32[]{:S(2)}) copy-start(f32[6,384]{1,0:T(8,128)} %param.18) | copy-start | bytes 27652
  5.4 16.3 %copy-start.2 = (bf16[384,1024]{1,0:T(8,128)(2,1)S(1)}, bf16[384,1024]{1,0:T(8,128)(2,1)}, u32[]{:S(2)}) copy-start(bf16[384,1024]{1,0:T(8,128)(2,1)} %param.13) | copy-start | bytes 2359300
  6.4 37.9 %all-to-all-start = ((bf16[64,3,16,128]{3,2,1,0:T(8,128)(2,1)}), bf16[64,3,16,128]{3,2,1,0:T(8,128)(2,1)S(1)}, u32[]{:S(2)}, u32[]{:S(2)}) async-start(bf16[64,3,16,128]{3,2,1,0:T(8,128)(2,1)} %bitcast.11), calls=%async_computation | async-start | bytes 1572864 | tf_op jit(solution)/shard_map/all_to_all | solution.py:14
  44.3 29.1 %all-to-all-start.1 = ((bf16[64,3,16,128]{3,2,1,0:T(8,128)(2,1)}), bf16[64,3,16,128]{3,2,1,0:T(8,128)(2,1)S(1)}, u32[]{:S(2)}, u32[]{:S(2)}) async-start(bf16[64,3,16,128]{3,2,1,0:T(8,128)(2,1)} %bitcast.21), calls=%async_computation.1 | async-start | bytes 1572864 | tf_op jit(solution)/shard_map/all_to_all | solution.py:14
  75.5 9.0 %copy-start.6 = (bf16[128,3,3]{0,2,1:T(4,128)(2,1)S(1)}, bf16[128,3,3]{0,2,1:T(4,128)(2,1)}, u32[]{:S(2)}) copy-start(bf16[128,3,3]{0,2,1:T(4,128)(2,1)} %param.17) | copy-start | bytes 6916
  76.5 29.1 %all-to-all-start.2 = ((bf16[64,3,16,128]{3,2,1,0:T(8,128)(2,1)}), bf16[64,3,16,128]{3,2,1,0:T(8,128)(2,1)S(1)}, u32[]{:S(2)}, u32[]{:S(2)}) async-start(bf16[64,3,16,128]{3,2,1,0:T(8,128)(2,1)} %bitcast.23), calls=%async_computation.2 | async-start | bytes 1572864 | tf_op jit(solution)/shard_map/all_to_all | solution.py:20
  106.0 0.9 copy-start.4
  106.9 1.1 copy-start.3
  114.1 2.6 %copy-start.1 = (f32[384,4096]{1,0:T(8,128)}, f32[384,4096]{1,0:T(8,128)S(1)}, u32[]{:S(2)}) copy-start(f32[384,4096]{1,0:T(8,128)S(1)} %fusion.19) | copy-start | bytes 18874372
  116.9 7.9 %collective-permute-start = (bf16[2,96,4096]{2,1,0:T(8,128)(2,1)S(1)}, bf16[2,96,4096]{2,1,0:T(8,128)(2,1)}, u32[]{:S(2)}, u32[]{:S(2)}) collective-permute-start(bf16[2,96,4096]{2,1,0:T(8,128)(2,1)S(1)} %fusion), channel_id=1, source_target_pairs={{0,1},{1,0},{2,3},{3,2},{4,5},{5,4},{6,7},{7,6},{8,9},{9,8},{10,11... | collective-permute-start | bytes 4718600 | tf_op jit(solution)/shard_map/ppermute | solution.py:94
  128.5 19.0 %collective-permute-start.1 = (bf16[96,4096]{1,0:T(8,128)(2,1)}, bf16[96,4096]{1,0:T(8,128)(2,1)}, u32[]{:S(2)}, u32[]{:S(2)}) collective-permute-start(bf16[96,4096]{1,0:T(8,128)(2,1)} %fusion.6), channel_id=1, source_target_pairs={{0,2},{1,3},{2,0},{3,1},{4,6},{5,7},{6,4},{7,5},{8,10},{9,11},{10,... | collective-permute-start | bytes 2359304 | tf_op jit(solution)/shard_map/ppermute | solution.py:94

commit v3 on v2

--- a/solution.py
+++ b/solution.py
@@ -7,10 +7,10 @@
 
 
 def to_columns(values, count):
-    nb, blk, chans = values.shape
+    n, nb, blk, chans = values.shape
     cs = count // ROW_SPLIT
-    parts = values.reshape(nb, ROW_SPLIT, blk // ROW_SPLIT, cs, chans // cs)
-    parts = parts.transpose(1, 3, 0, 2, 4).reshape(count, nb, blk // ROW_SPLIT, chans // cs)
+    parts = values.reshape(n, nb, ROW_SPLIT, blk // ROW_SPLIT, cs, chans // cs)
+    parts = parts.transpose(2, 4, 0, 1, 3, 5).reshape(count, n, nb, blk // ROW_SPLIT, chans // cs)
     return lax.all_to_all(parts, "seq", 0, 0, tiled=True)
 
 
@@ -61,8 +61,10 @@
         "ikl,lic->kic", analysis_mix, inner, preferred_element_type=jnp.float32
     ).astype(jnp.bfloat16)
 
-    spec_cols = to_columns(spec, count)
-    filt_cols = to_columns(spectral_filter.reshape(nblocks, blk, chans), count)
+    both = jnp.stack([spec, spectral_filter.reshape(nblocks, blk, chans)])
+    both_cols = to_columns(both, count)
+    spec_cols = both_cols[:, 0]
+    filt_cols = both_cols[:, 1]
     rows = blk // ROW_SPLIT
     row_part = rank // (count // ROW_SPLIT)
     theta = angles.reshape(sections, nblocks, ROW_SPLIT, rows)
@@ -85,7 +87,7 @@
     ).astype(jnp.bfloat16)
     conv = jnp.einsum("kij,kjc->kic", synthesis_blocks, spread, preferred_element_type=jnp.float32)
     gated = (gate_out.astype(jnp.float32) * conv.reshape(tokens, chans)).astype(jnp.bfloat16)
-    product = jnp.dot(gated, out_weight, preferred_element_type=jnp.float32)
+    product = jnp.dot(gated, out_weight, preferred_element_type=jnp.float32).astype(jnp.bfloat16)
     return scatter_sum(product)
 
 
@@ -102,7 +104,7 @@
     quarters = product.reshape(2, 2, rows // 4, width)
     keep = lax.dynamic_index_in_dim(quarters, core, axis=1, keepdims=False)
     send = lax.dynamic_index_in_dim(quarters, 1 - core, axis=1, keepdims=False)
-    half = keep + exchange(send.astype(jnp.bfloat16), 1).astype(jnp.float32)
+    half = keep.astype(jnp.float32) + exchange(send, 1).astype(jnp.float32)
     keep = lax.dynamic_index_in_dim(half, chip, axis=0, keepdims=False)
     send = lax.dynamic_index_in_dim(half, 1 - chip, axis=0, keepdims=False)
     total = keep + exchange(send.astype(jnp.bfloat16), 2).astype(jnp.float32)

time: 150 us -> 141 us (0.940)
  starting transfers between devices: 35.7 us -> 28.9 us
  waiting for transfers between devices: 83.6 us -> 80.6 us
    all_to_all x2 -> x1, starting transfers between devices: 22.5 us -> 15.2 us  [to_columns(): return lax.all_to_all(parts, 'seq', 0, 0, tiled=True)]
    all_to_all x2 -> x1, waiting for transfers between devices: 41.1 us -> 37.7 us  [to_columns(): return lax.all_to_all(parts, 'seq', 0, 0, tiled=True)]
  transfers between devices with their start and end apart: 5 -> 4, of which waited for: 5 -> 4; matrix products, arithmetic and copies ran while one was open for 2% -> 0% of each run, Pallas kernels for 0% -> 0%
where the time goes in v3:
time: 141 us; the launch traced here: 140 us
  waiting for transfers between devices  80.6 us (57%)
  starting transfers between devices  28.9 us (20%)
  other arithmetic  11.8 us (8%)
  matrix products  9.54 us (7%)
  local copies, waits for them, and re-layouts  8.97 us (6%)
    all_to_all x1, waiting for transfers between devices, to_columns(): return lax.all_to_all(parts, 'seq', 0, 0, tiled=True)  37.7 us
    ppermute x2, waiting for transfers between devices, exchange(): return lax.ppermute(value, 'chan', pairs)  21.8 us
    all_to_all x1, waiting for transfers between devices, from_columns(): back = lax.all_to_all(values, 'seq', 0, 0, tiled=True)  21.1 us
    all_to_all x1, starting transfers between devices, to_columns(): return lax.all_to_all(parts, 'seq', 0, 0, tiled=True)  15.2 us
    all_to_all x1, starting transfers between devices, from_columns(): back = lax.all_to_all(values, 'seq', 0, 0, tiled=True)  8.74 us
    dot_general x1, matrix products, per_device(): jnp.dot(gated, out_weight, preferred_element_type=jnp.float32)  7.07 us
    ppermute x2, starting transfers between devices, exchange(): return lax.ppermute(value, 'chan', pairs)  4.89 us
    unnamed x17, local copies, waits for them, and re-layouts  3.85 us
  transfers between devices with their start and end apart: 4, of which 4 were waited for; matrix products, arithmetic and copies ran while one was open for 0% of the time, Pallas kernels for 0%

profile of v3, /device:TPU:1, one launch (start us, length us, event | category | flops | bytes accessed | tf_op | source)
XLA Modules:
  0.0 140.2 jit_solution(4854997023771135747)
XLA Ops:
  0.0 0.9 copy.23
  0.9 1.7 %multiply_convert_fusion = bf16[384,1024]{1,0:T(8,128)(2,1)S(1)} fusion(bf16[384,1024]{1,0:T(8,128)(2,1)} %param.10, bf16[384,1024]{1,0:T(8,128)(2,1)} %param.11), kind=kLoop, calls=%fused_computation.30 | loop fusion | flops 1572864 | bytes 2359296 | tf_op jit(solution)/shard_map/convert_element_type | solution.py:54
  2.6 0.4 fusion.4
  3.0 0.9 copy.22
  3.9 0.7 fusion.2
  4.6 0.7 reshape.202
  5.4 0.4 copy-done.2
  6.3 1.5 %copy.25 = bf16[8,8,2,3,16,128]{5,4,3,2,1,0:T(8,128)(2,1)} copy(bf16[8,8,2,3,16,128]{5,1,4,0,3,2:T(8,128)(2,1)S(1)} %maximum_bitcast_fusion) | data formatting | bytes 3145728 | tf_op jit(solution)/shard_map/transpose | solution.py:13
  7.8 15.2 %all-to-all-start = ((bf16[64,2,3,16,128]{4,3,2,1,0:T(8,128)(2,1)}), bf16[64,2,3,16,128]{4,3,2,1,0:T(8,128)(2,1)S(1)}, u32[]{:S(2)}, u32[]{:S(2)}) async-start(bf16[64,2,3,16,128]{4,3,2,1,0:T(8,128)(2,1)} %bitcast.10), calls=%async_computation | async-start | bytes 3145728 | tf_op jit(solution)/shard_map/all_to_all | solution.py:14
  23.3 37.7 %all-to-all-done = bf16[64,2,3,16,128]{4,3,2,1,0:T(8,128)(2,1)S(1)} async-done(((bf16[64,2,3,16,128]{4,3,2,1,0:T(8,128)(2,1)}), bf16[64,2,3,16,128]{4,3,2,1,0:T(8,128)(2,1)S(1)}, u32[]{:S(2)}, u32[]{:S(2)}) %all-to-all-start) | async-done | bytes 1572896 | tf_op jit(solution)/shard_map/all_to_all | solution.py:14
  65.5 0.9 pad_maximum_fusion.10
  66.4 8.7 %all-to-all-start.1 = ((bf16[64,3,16,128]{3,2,1,0:T(8,128)(2,1)}), bf16[64,3,16,128]{3,2,1,0:T(8,128)(2,1)S(1)}, u32[]{:S(2)}, u32[]{:S(2)}) async-start(bf16[64,3,16,128]{3,2,1,0:T(8,128)(2,1)} %bitcast.20), calls=%async_computation.1 | async-start | bytes 1572864 | tf_op jit(solution)/shard_map/all_to_all | solution.py:20
  75.4 21.1 %all-to-all-done.1 = bf16[64,3,16,128]{3,2,1,0:T(8,128)(2,1)S(1)} async-done(((bf16[64,3,16,128]{3,2,1,0:T(8,128)(2,1)}), bf16[64,3,16,128]{3,2,1,0:T(8,128)(2,1)S(1)}, u32[]{:S(2)}, u32[]{:S(2)}) %all-to-all-start.1) | async-done | bytes 786464 | tf_op jit(solution)/shard_map/all_to_all | solution.py:20
  97.0 0.7 fusion.3
  97.9 0.7 fusion.16
  98.5 0.5 copy-done.3
  99.3 7.1 %convolution_convert_fusion = bf16[384,4096]{1,0:T(8,128)(2,1)S(1)} fusion(bf16[384,1024]{1,0:T(8,128)(2,1)S(1)} %fusion, bf16[1024,4096]{1,0:T(8,128)(2,1)} %param.19), kind=kOutput, calls=%fused_computation | convolution fusion | flops 3222798336 | bytes 12320768 | tf_op jit(solution)/shard_map/dot_general | solution.py:90
  106.5 1.5 %copy-done.1 = bf16[384,4096]{1,0:T(8,128)(2,1)} copy-done((bf16[384,4096]{1,0:T(8,128)(2,1)}, bf16[384,4096]{1,0:T(8,128)(2,1)S(1)}, u32[]{:S(2)}) %copy-start.1) | copy-done | bytes 3145752
  108.0 4.5 %collective-permute-start = (bf16[2,96,4096]{2,1,0:T(8,128)(2,1)S(1)}, bf16[2,96,4096]{2,1,0:T(8,128)(2,1)}, u32[]{:S(2)}, u32[]{:S(2)}) collective-permute-start(bf16[2,96,4096]{2,1,0:T(8,128)(2,1)S(1)} %dynamic-slice_bitcast_fusion), channel_id=1, source_target_pairs={{0,1},{1,0},{2,3},{3,2},{4,5},{5,4},{6,7},{7,6},{8,9},{9,8},{10,11... | collective-permute-start | bytes 4718600 | tf_op jit(solution)/shard_map/ppermute | solution.py:96
  112.5 3.2 %collective-permute-done = bf16[2,96,4096]{2,1,0:T(8,128)(2,1)} collective-permute-done((bf16[2,96,4096]{2,1,0:T(8,128)(2,1)S(1)}, bf16[2,96,4096]{2,1,0:T(8,128)(2,1)}, u32[]{:S(2)}, u32[]{:S(2)}) %collective-permute-start) | collective-permute-done | bytes 1572896 | tf_op jit(solution)/shard_map/ppermute | solution.py:96
  115.7 2.3 %convert_add_fusion = f32[2,96,4096]{2,1,0:T(8,128)S(1)} fusion(bf16[2,96,4096]{2,1,0:T(8,128)(2,1)} %collective-permute-done, bf16[2,2,96,4096]{3,2,1,0:T(8,128)(2,1)} %bitcast.96, s32[]{:T(128)S(6)} %select_n.35), kind=kLoop, calls=%fused_computation.1 | loop fusion | flops 2359296 | bytes 6291460 | tf_op jit(solution)/shard_map/add | solution.py:107
  118.0 1.0 fusion.5
  119.4 18.6 %collective-permute-done.1 = bf16[96,4096]{1,0:T(8,128)(2,1)} collective-permute-done((bf16[96,4096]{1,0:T(8,128)(2,1)}, bf16[96,4096]{1,0:T(8,128)(2,1)}, u32[]{:S(2)}, u32[]{:S(2)}) %collective-permute-start.1) | collective-permute-done | bytes 786464 | tf_op jit(solution)/shard_map/ppermute | solution.py:96
  138.0 2.2 %fusion.1 = bf16[96,4096]{1,0:T(8,128)(2,1)} fusion(bf16[96,4096]{1,0:T(8,128)(2,1)} %collective-permute-done.1, f32[2,96,4096]{2,1,0:T(8,128)S(1)} %convert_add_fusion, s32[]{:T(128)S(6)} %select_n.38), kind=kLoop, calls=%fused_computation.27 | loop fusion | flops 1179648 | bytes 3145732 | tf_op jit(solution)/shard_map/convert_element_type | solution.py:111
  (39 shorter events, 6.7 us)
Async XLA Ops:
  0.0 2.6 %copy-start = (bf16[3,128,128]{2,1,0:T(8,128)(2,1)S(1)}, bf16[3,128,128]{2,1,0:T(8,128)(2,1)}, u32[]{:S(2)}) copy-start(bf16[3,128,128]{2,1,0:T(8,128)(2,1)} %param.14) | copy-start | bytes 294916
  4.6 1.1 copy-start.2
  7.8 15.3 %copy-start.5 = (f32[6,384]{1,0:T(8,128)S(1)}, f32[6,384]{1,0:T(8,128)}, u32[]{:S(2)}) copy-start(f32[6,384]{1,0:T(8,128)} %param.18) | copy-start | bytes 27652
  7.8 53.2 %all-to-all-start = ((bf16[64,2,3,16,128]{4,3,2,1,0:T(8,128)(2,1)}), bf16[64,2,3,16,128]{4,3,2,1,0:T(8,128)(2,1)S(1)}, u32[]{:S(2)}, u32[]{:S(2)}) async-start(bf16[64,2,3,16,128]{4,3,2,1,0:T(8,128)(2,1)} %bitcast.10), calls=%async_computation | async-start | bytes 3145728 | tf_op jit(solution)/shard_map/all_to_all | solution.py:14
  65.5 9.7 %copy-start.6 = (bf16[128,3,3]{0,2,1:T(4,128)(2,1)S(1)}, bf16[128,3,3]{0,2,1:T(4,128)(2,1)}, u32[]{:S(2)}) copy-start(bf16[128,3,3]{0,2,1:T(4,128)(2,1)} %param.17) | copy-start | bytes 6916
  66.4 30.1 %all-to-all-start.1 = ((bf16[64,3,16,128]{3,2,1,0:T(8,128)(2,1)}), bf16[64,3,16,128]{3,2,1,0:T(8,128)(2,1)S(1)}, u32[]{:S(2)}, u32[]{:S(2)}) async-start(bf16[64,3,16,128]{3,2,1,0:T(8,128)(2,1)} %bitcast.20), calls=%async_computation.1 | async-start | bytes 1572864 | tf_op jit(solution)/shard_map/all_to_all | solution.py:20
  97.0 0.9 copy-start.4
  97.9 1.1 copy-start.3
  106.4 1.6 %copy-start.1 = (bf16[384,4096]{1,0:T(8,128)(2,1)}, bf16[384,4096]{1,0:T(8,128)(2,1)S(1)}, u32[]{:S(2)}) copy-start(bf16[384,4096]{1,0:T(8,128)(2,1)S(1)} %convolution_convert_fusion) | copy-start | bytes 9437188
  108.0 7.7 %collective-permute-start = (bf16[2,96,4096]{2,1,0:T(8,128)(2,1)S(1)}, bf16[2,96,4096]{2,1,0:T(8,128)(2,1)}, u32[]{:S(2)}, u32[]{:S(2)}) collective-permute-start(bf16[2,96,4096]{2,1,0:T(8,128)(2,1)S(1)} %dynamic-slice_bitcast_fusion), channel_id=1, source_target_pairs={{0,1},{1,0},{2,3},{3,2},{4,5},{5,4},{6,7},{7,6},{8,9},{9,8},{10,11... | collective-permute-start | bytes 4718600 | tf_op jit(solution)/shard_map/ppermute | solution.py:96
  119.0 19.0 %collective-permute-start.1 = (bf16[96,4096]{1,0:T(8,128)(2,1)}, bf16[96,4096]{1,0:T(8,128)(2,1)}, u32[]{:S(2)}, u32[]{:S(2)}) collective-permute-start(bf16[96,4096]{1,0:T(8,128)(2,1)} %fusion.5), channel_id=1, source_target_pairs={{0,2},{1,3},{2,0},{3,1},{4,6},{5,7},{6,4},{7,5},{8,10},{9,11},{10,... | collective-permute-start | bytes 2359304 | tf_op jit(solution)/shard_map/ppermute | solution.py:96

commit v4 on v3

--- a/solution.py
+++ b/solution.py
@@ -87,8 +87,7 @@
     ).astype(jnp.bfloat16)
     conv = jnp.einsum("kij,kjc->kic", synthesis_blocks, spread, preferred_element_type=jnp.float32)
     gated = (gate_out.astype(jnp.float32) * conv.reshape(tokens, chans)).astype(jnp.bfloat16)
-    product = jnp.dot(gated, out_weight, preferred_element_type=jnp.float32).astype(jnp.bfloat16)
-    return scatter_sum(product)
+    return scatter_sum(gated, out_weight)
 
 
 def exchange(value, distance):
@@ -96,19 +95,23 @@
     return lax.ppermute(value, "chan", pairs)
 
 
-def scatter_sum(product):
+def scatter_sum(gated, out_weight):
     me = lax.axis_index("chan")
     core = me % 2
     chip = me // 2
-    rows, width = product.shape
-    quarters = product.reshape(2, 2, rows // 4, width)
-    keep = lax.dynamic_index_in_dim(quarters, core, axis=1, keepdims=False)
-    send = lax.dynamic_index_in_dim(quarters, 1 - core, axis=1, keepdims=False)
-    half = keep.astype(jnp.float32) + exchange(send, 1).astype(jnp.float32)
-    keep = lax.dynamic_index_in_dim(half, chip, axis=0, keepdims=False)
-    send = lax.dynamic_index_in_dim(half, 1 - chip, axis=0, keepdims=False)
-    total = keep + exchange(send.astype(jnp.bfloat16), 2).astype(jnp.float32)
-    return total.astype(jnp.bfloat16)
+    rows, chans = gated.shape
+    quarters = gated.reshape(2, 2, rows // 4, chans)
+    sent_rows = lax.dynamic_index_in_dim(quarters, 1 - core, axis=1, keepdims=False)
+    kept_rows = lax.dynamic_index_in_dim(quarters, core, axis=1, keepdims=False)
+    sent = jnp.einsum("yrc,cw->yrw", sent_rows, out_weight, preferred_element_type=jnp.float32)
+    half = exchange(sent.astype(jnp.bfloat16), 1)
+    kept = jnp.einsum("yrc,cw->yrw", kept_rows, out_weight, preferred_element_type=jnp.float32)
+    other = lax.dynamic_index_in_dim(kept, 1 - chip, axis=0, keepdims=False)
+    other = other + lax.dynamic_index_in_dim(half, 1 - chip, axis=0, keepdims=False).astype(jnp.float32)
+    quarter = exchange(other.astype(jnp.bfloat16), 2)
+    mine = lax.dynamic_index_in_dim(kept, chip, axis=0, keepdims=False)
+    mine = mine + lax.dynamic_index_in_dim(half, chip, axis=0, keepdims=False).astype(jnp.float32)
+    return (mine + quarter.astype(jnp.float32)).astype(jnp.bfloat16)
 
 
 def solution(mesh):

time: 141 us -> 140 us (level)
  matrix products: 9.54 us -> 14.4 us
  waiting for transfers between devices: 80.6 us -> 77.8 us
  local copies, waits for them, and re-layouts: 8.97 us -> 6.37 us
    dot_general x1 -> x2, matrix products: 7.07 us -> 11.9 us  [the longest x1 6.62 us: scatter_sum(): jnp.einsum('yrc,cw->yrw', sent_rows, out_weight, preferred_element_type=j...]
    ppermute x2, waiting for transfers between devices: 21.8 us -> 19 us  [exchange(): return lax.ppermute(value, 'chan', pairs)]
    convert_element_type x1 -> x2, other arithmetic: 2.17 us -> 4.66 us  [the longest x1 2.49 us: scatter_sum(): return (mine + quarter.astype(jnp.float32)).astype(jnp.bfloat16)]
    add x1 -> x0, other arithmetic: 2.31 us -> none  [scatter_sum(): half = keep.astype(jnp.float32) + exchange(send, 1).astype(jnp.float32)]
    unnamed x17, local copies, waits for them, and re-layouts: 3.85 us -> 2.34 us
  transfers between devices with their start and end apart: 4 -> 4, of which waited for: 4 -> 3; matrix products, arithmetic and copies ran while one was open for 0% -> 4% of each run, Pallas kernels for 0% -> 0%
where the time goes in v4:
time: 140 us
  waiting for transfers between devices  77.8 us (56%)
  starting transfers between devices  28.9 us (21%)
  matrix products  14.4 us (10%)
  other arithmetic  12 us (9%)
  local copies, waits for them, and re-layouts  6.37 us (5%)
    all_to_all x1, waiting for transfers between devices, to_columns(): return lax.all_to_all(parts, 'seq', 0, 0, tiled=True)  37.7 us
    all_to_all x1, waiting for transfers between devices, from_columns(): back = lax.all_to_all(values, 'seq', 0, 0, tiled=True)  21.1 us
    ppermute x2, waiting for transfers between devices, exchange(): return lax.ppermute(value, 'chan', pairs)  19 us
    all_to_all x1, starting transfers between devices, to_columns(): return lax.all_to_all(parts, 'seq', 0, 0, tiled=True)  15.2 us
    all_to_all x1, starting transfers between devices, from_columns(): back = lax.all_to_all(values, 'seq', 0, 0, tiled=True)  8.74 us
    dot_general x1, matrix products, scatter_sum(): jnp.einsum('yrc,cw->yrw', sent_rows, out_weight, preferred_element_type=j...  6.62 us
    dot_general x1, matrix products, scatter_sum(): jnp.einsum('yrc,cw->yrw', kept_rows, out_weight, preferred_element_type=j...  5.33 us
    ppermute x2, starting transfers between devices, exchange(): return lax.ppermute(value, 'chan', pairs)  4.89 us
  transfers between devices with their start and end apart: 4, of which 3 were waited for; matrix products, arithmetic and copies ran while one was open for 4% of the time, Pallas kernels for 0%

profile of v4, /device:TPU:1, one launch (start us, length us, event | category | flops | bytes accessed | tf_op | source)
XLA Modules:
  0.0 139.8 jit_solution(15778580899856707137)
XLA Ops:
  0.0 0.9 copy.25
  0.9 1.7 %multiply_convert_fusion = bf16[384,1024]{1,0:T(8,128)(2,1)S(1)} fusion(bf16[384,1024]{1,0:T(8,128)(2,1)} %param.10, bf16[384,1024]{1,0:T(8,128)(2,1)} %param.11), kind=kLoop, calls=%fused_computation.32 | loop fusion | flops 1572864 | bytes 2359296 | tf_op jit(solution)/shard_map/convert_element_type | solution.py:54
  2.6 0.4 fusion.11
  3.0 0.9 copy.24
  3.9 0.7 fusion.9
  4.6 0.7 reshape.204
  5.4 0.4 copy-done.2
  5.9 0.3 maximum_bitcast_fusion
  6.3 1.5 %copy.27 = bf16[8,8,2,3,16,128]{5,4,3,2,1,0:T(8,128)(2,1)} copy(bf16[8,8,2,3,16,128]{5,1,4,0,3,2:T(8,128)(2,1)S(1)} %maximum_bitcast_fusion) | data formatting | bytes 3145728 | tf_op jit(solution)/shard_map/transpose | solution.py:13
  7.8 15.2 %all-to-all-start = ((bf16[64,2,3,16,128]{4,3,2,1,0:T(8,128)(2,1)}), bf16[64,2,3,16,128]{4,3,2,1,0:T(8,128)(2,1)S(1)}, u32[]{:S(2)}, u32[]{:S(2)}) async-start(bf16[64,2,3,16,128]{4,3,2,1,0:T(8,128)(2,1)} %bitcast.10), calls=%async_computation | async-start | bytes 3145728 | tf_op jit(solution)/shard_map/all_to_all | solution.py:14
  23.3 37.7 %all-to-all-done = bf16[64,2,3,16,128]{4,3,2,1,0:T(8,128)(2,1)S(1)} async-done(((bf16[64,2,3,16,128]{4,3,2,1,0:T(8,128)(2,1)}), bf16[64,2,3,16,128]{4,3,2,1,0:T(8,128)(2,1)S(1)}, u32[]{:S(2)}, u32[]{:S(2)}) %all-to-all-start) | async-done | bytes 1572896 | tf_op jit(solution)/shard_map/all_to_all | solution.py:14
  65.5 0.9 pad_maximum_fusion.10
  66.4 8.7 %all-to-all-start.1 = ((bf16[64,3,16,128]{3,2,1,0:T(8,128)(2,1)}), bf16[64,3,16,128]{3,2,1,0:T(8,128)(2,1)S(1)}, u32[]{:S(2)}, u32[]{:S(2)}) async-start(bf16[64,3,16,128]{3,2,1,0:T(8,128)(2,1)} %bitcast.20), calls=%async_computation.1 | async-start | bytes 1572864 | tf_op jit(solution)/shard_map/all_to_all | solution.py:20
  75.4 21.1 %all-to-all-done.1 = bf16[64,3,16,128]{3,2,1,0:T(8,128)(2,1)S(1)} async-done(((bf16[64,3,16,128]{3,2,1,0:T(8,128)(2,1)}), bf16[64,3,16,128]{3,2,1,0:T(8,128)(2,1)S(1)}, u32[]{:S(2)}, u32[]{:S(2)}) %all-to-all-start.1) | async-done | bytes 786464 | tf_op jit(solution)/shard_map/all_to_all | solution.py:20
  97.0 0.7 fusion.10
  97.9 0.7 fusion.23
  98.6 0.5 copy-done.3
  99.3 6.6 %fusion.4 = bf16[2,96,4096]{2,1,0:T(8,128)(2,1)} fusion(bf16[1024,4096]{1,0:T(8,128)(2,1)} %param.19, bf16[2,2,96,1024]{3,2,1,0:T(8,128)(2,1)S(1)} %bitcast.105, s32[]{:T(128)S(6)} %select_n.41), kind=kOutput, calls=%fused_computation.4 | convolution fusion | flops 1611399168 | bytes 10354692 | tf_op jit(solution)/shard_map/yrc,cw->yrw/dot_general | solution.py:106
  105.9 4.5 %collective-permute-start = (bf16[2,96,4096]{2,1,0:T(8,128)(2,1)}, bf16[2,96,4096]{2,1,0:T(8,128)(2,1)}, u32[]{:S(2)}, u32[]{:S(2)}) collective-permute-start(bf16[2,96,4096]{2,1,0:T(8,128)(2,1)} %fusion.4), channel_id=1, source_target_pairs={{0,1},{1,0},{2,3},{3,2},{4,5},{5,4},{6,7},{7,6},{8,9},{9,8},{10,11... | collective-permute-start | bytes 4718600 | tf_op jit(solution)/shard_map/ppermute | solution.py:95
  110.4 5.3 %fusion.2 = f32[2,96,4096]{2,1,0:T(8,128)S(1)} fusion(bf16[1024,4096]{1,0:T(8,128)(2,1)} %param.19, bf16[2,2,96,1024]{3,2,1,0:T(8,128)(2,1)} %bitcast.106, s32[]{:T(128)S(6)} %select_n.38), kind=kOutput, calls=%fused_computation.2 | convolution fusion | flops 1610612736 | bytes 11927556 | tf_op jit(solution)/shard_map/yrc,cw->yrw/dot_general | solution.py:108
  115.8 2.2 %fusion.12 = bf16[96,4096]{1,0:T(8,128)(2,1)} fusion(f32[2,96,4096]{2,1,0:T(8,128)S(1)} %fusion.2, s32[]{:T(128)S(6)} %select_n.42, bf16[2,96,4096]{2,1,0:T(8,128)(2,1)} %collective-permute-done), kind=kLoop, calls=%fused_computation.39 | loop fusion | flops 1179648 | bytes 3145732 | tf_op jit(solution)/shard_map/convert_element_type | solution.py:111
  117.9 0.4 collective-permute-start.1
  118.3 19.0 %collective-permute-done.1 = bf16[96,4096]{1,0:T(8,128)(2,1)} collective-permute-done((bf16[96,4096]{1,0:T(8,128)(2,1)}, bf16[96,4096]{1,0:T(8,128)(2,1)}, u32[]{:S(2)}, u32[]{:S(2)}) %collective-permute-start.1) | collective-permute-done | bytes 786464 | tf_op jit(solution)/shard_map/ppermute | solution.py:95
  137.3 2.5 %fusion.8 = bf16[96,4096]{1,0:T(8,128)(2,1)} fusion(bf16[96,4096]{1,0:T(8,128)(2,1)} %collective-permute-done.1, f32[2,96,4096]{2,1,0:T(8,128)S(1)} %fusion.2, s32[]{:T(128)S(6)} %select_n.40, bf16[2,96,4096]{2,1,0:T(8,128)(2,1)} %collective-permute-done), kind=kLoop, calls=%fused_computation.30 | loop fusion | flops 1966080 | bytes 3932164 | tf_op jit(solution)/shard_map/convert_element_type | solution.py:114
  (38 shorter events, 5.8 us)
Async XLA Ops:
  0.0 2.6 %copy-start = (bf16[3,128,128]{2,1,0:T(8,128)(2,1)S(1)}, bf16[3,128,128]{2,1,0:T(8,128)(2,1)}, u32[]{:S(2)}) copy-start(bf16[3,128,128]{2,1,0:T(8,128)(2,1)} %param.14) | copy-start | bytes 294916
  4.6 1.1 copy-start.2
  7.8 15.3 %copy-start.5 = (f32[6,384]{1,0:T(8,128)S(1)}, f32[6,384]{1,0:T(8,128)}, u32[]{:S(2)}) copy-start(f32[6,384]{1,0:T(8,128)} %param.18) | copy-start | bytes 27652
  7.8 53.2 %all-to-all-start = ((bf16[64,2,3,16,128]{4,3,2,1,0:T(8,128)(2,1)}), bf16[64,2,3,16,128]{4,3,2,1,0:T(8,128)(2,1)S(1)}, u32[]{:S(2)}, u32[]{:S(2)}) async-start(bf16[64,2,3,16,128]{4,3,2,1,0:T(8,128)(2,1)} %bitcast.10), calls=%async_computation | async-start | bytes 3145728 | tf_op jit(solution)/shard_map/all_to_all | solution.py:14
  65.5 9.7 %copy-start.6 = (bf16[128,3,3]{0,2,1:T(4,128)(2,1)S(1)}, bf16[128,3,3]{0,2,1:T(4,128)(2,1)}, u32[]{:S(2)}) copy-start(bf16[128,3,3]{0,2,1:T(4,128)(2,1)} %param.17) | copy-start | bytes 6916
  66.4 30.1 %all-to-all-start.1 = ((bf16[64,3,16,128]{3,2,1,0:T(8,128)(2,1)}), bf16[64,3,16,128]{3,2,1,0:T(8,128)(2,1)S(1)}, u32[]{:S(2)}, u32[]{:S(2)}) async-start(bf16[64,3,16,128]{3,2,1,0:T(8,128)(2,1)} %bitcast.20), calls=%async_computation.1 | async-start | bytes 1572864 | tf_op jit(solution)/shard_map/all_to_all | solution.py:20
  97.0 0.9 copy-start.4
  97.9 1.1 copy-start.3
  99.3 6.6 %copy-start.1 = (bf16[384,1024]{1,0:T(8,128)(2,1)}, bf16[384,1024]{1,0:T(8,128)(2,1)S(1)}, u32[]{:S(2)}) copy-start(bf16[384,1024]{1,0:T(8,128)(2,1)S(1)} %fusion.7) | copy-start | bytes 2359300
  105.9 9.8 %collective-permute-start = (bf16[2,96,4096]{2,1,0:T(8,128)(2,1)}, bf16[2,96,4096]{2,1,0:T(8,128)(2,1)}, u32[]{:S(2)}, u32[]{:S(2)}) collective-permute-start(bf16[2,96,4096]{2,1,0:T(8,128)(2,1)} %fusion.4), channel_id=1, source_target_pairs={{0,1},{1,0},{2,3},{3,2},{4,5},{5,4},{6,7},{7,6},{8,9},{9,8},{10,11... | collective-permute-start | bytes 4718600 | tf_op jit(solution)/shard_map/ppermute | solution.py:95
  117.9 19.4 %collective-permute-start.1 = (bf16[96,4096]{1,0:T(8,128)(2,1)}, bf16[96,4096]{1,0:T(8,128)(2,1)}, u32[]{:S(2)}, u32[]{:S(2)}) collective-permute-start(bf16[96,4096]{1,0:T(8,128)(2,1)} %fusion.12), channel_id=1, source_target_pairs={{0,2},{1,3},{2,0},{3,1},{4,6},{5,7},{6,4},{7,5},{8,10},{9,11},{10,... | collective-permute-start | bytes 2359304 | tf_op jit(solution)/shard_map/ppermute | solution.py:95

commit v5 on v4

--- a/solution.py
+++ b/solution.py
@@ -20,15 +20,6 @@
     back = lax.all_to_all(values, "seq", 0, 0, tiled=True)
     back = back.reshape(ROW_SPLIT, cs, nb, blk // ROW_SPLIT, chans // cs)
     return back.transpose(2, 0, 3, 1, 4).reshape(nb, blk, chans)
-
-
-def rotate_bit(values, cosine, sine, bit, sections, sign):
-    axis = sections - 1 - bit
-    lower = lax.index_in_dim(values, 0, axis, keepdims=True)
-    upper = lax.index_in_dim(values, 1, axis, keepdims=True)
-    new_lower = cosine * lower + sign * sine * upper
-    new_upper = cosine * upper - sign * sine * lower
-    return jnp.concatenate([new_lower, new_upper], axis=axis)
 
 
 def per_device(
@@ -72,14 +63,20 @@
     cosines = jnp.cos(theta)[:, :, :, None]
     sines = jnp.sin(theta)[:, :, :, None]
 
-    shape = (2,) * sections + spec_cols.shape[1:]
-    work = spec_cols.astype(jnp.float32).reshape(shape)
-    for section in range(sections):
-        work = rotate_bit(work, cosines[section], sines[section], section, sections, 1.0)
-    work = work * filt_cols.astype(jnp.float32).reshape(shape)
-    for section in reversed(range(sections)):
-        work = rotate_bit(work, cosines[section], sines[section], section, sections, -1.0)
-    work = work.astype(jnp.bfloat16).reshape(spec_cols.shape)
+    bits = (jnp.arange(count)[:, None] >> jnp.arange(sections)[None, :]) & 1
+    same = bits[:, None, :] == bits[None, :, :]
+    below = (bits[:, None, :] == 0) & (bits[None, :, :] == 1)
+    factor = jnp.where(
+        same[None, None],
+        cosines[..., 0].transpose(1, 2, 0)[:, :, None, None, :],
+        jnp.where(below[None, None], 1.0, -1.0) * sines[..., 0].transpose(1, 2, 0)[:, :, None, None, :],
+    )
+    matrix = jnp.prod(factor, axis=-1)
+    hi = lax.Precision.HIGHEST
+    work = jnp.einsum("kide,ekic->dkic", matrix, spec_cols.astype(jnp.float32), precision=hi)
+    work = work * filt_cols.astype(jnp.float32)
+    work = jnp.einsum("kied,ekic->dkic", matrix, work, precision=hi)
+    work = work.astype(jnp.bfloat16)
 
     grid = from_columns(work, count, blk, chans)
     spread = jnp.einsum(

time: 140 us -> 140 us (level)
  matrix products: 14.4 us -> 18.3 us
  other arithmetic: 12 us -> 8.98 us
  waiting for transfers between devices: 77.8 us -> 75.5 us
  local copies, waits for them, and re-layouts: 6.37 us -> 7.8 us
    dot_general x0 -> x2, matrix products: none -> 3.73 us  [the longest x1 2.72 us: per_device(): work = jnp.einsum('kied,ekic->dkic', matrix, work, precision=hi)]
    add x11 -> x0, other arithmetic: 3.32 us -> none  [rotate_bit(): new_lower = cosine * lower + sign * sine * upper]
    all_to_all x1, waiting for transfers between devices: 37.7 us -> 35.6 us  [to_columns(): return lax.all_to_all(parts, 'seq', 0, 0, tiled=True)]
    reduce_prod x0 -> x1, other arithmetic: none -> 1.81 us  [per_device(): matrix = jnp.prod(factor, axis=-1)]
  transfers between devices with their start and end apart: 4 -> 4, of which waited for: 3 -> 3; matrix products, arithmetic and copies ran while one was open for 4% -> 6% of each run, Pallas kernels for 0% -> 0%
where the time goes in v5:
time: 140 us
  waiting for transfers between devices  75.5 us (54%)
  starting transfers between devices  29 us (21%)
  matrix products  18.3 us (13%)
  other arithmetic  8.98 us (6%)
  local copies, waits for them, and re-layouts  7.8 us (6%)
    all_to_all x1, waiting for transfers between devices, to_columns(): return lax.all_to_all(parts, 'seq', 0, 0, tiled=True)  35.6 us
    all_to_all x1, waiting for transfers between devices, from_columns(): back = lax.all_to_all(values, 'seq', 0, 0, tiled=True)  20.9 us
    ppermute x2, waiting for transfers between devices, exchange(): return lax.ppermute(value, 'chan', pairs)  19 us
    all_to_all x1, starting transfers between devices, to_columns(): return lax.all_to_all(parts, 'seq', 0, 0, tiled=True)  15.2 us
    all_to_all x1, starting transfers between devices, from_columns(): back = lax.all_to_all(values, 'seq', 0, 0, tiled=True)  8.92 us
    dot_general x1, matrix products, scatter_sum(): jnp.einsum('yrc,cw->yrw', sent_rows, out_weight, preferred_element_type=j...  6.62 us
    dot_general x1, matrix products, scatter_sum(): jnp.einsum('yrc,cw->yrw', kept_rows, out_weight, preferred_element_type=j...  5.33 us
    ppermute x2, starting transfers between devices, exchange(): return lax.ppermute(value, 'chan', pairs)  4.89 us
  transfers between devices with their start and end apart: 4, of which 3 were waited for; matrix products, arithmetic and copies ran while one was open for 6% of the time, Pallas kernels for 0%

profile of v5, /device:TPU:1, one launch (start us, length us, event | category | flops | bytes accessed | tf_op | source)
XLA Modules:
  0.0 139.9 jit_solution(7209160183548446214)
XLA Ops:
  0.0 0.9 copy.59
  0.9 1.7 %multiply_convert_fusion = bf16[384,1024]{1,0:T(8,128)(2,1)S(1)} fusion(bf16[384,1024]{1,0:T(8,128)(2,1)} %param.10, bf16[384,1024]{1,0:T(8,128)(2,1)} %param.11), kind=kLoop, calls=%fused_computation.15 | loop fusion | flops 1572864 | bytes 2359296 | tf_op jit(solution)/shard_map/convert_element_type | solution.py:45
  2.6 0.4 fusion.14
  3.0 0.9 copy.58
  3.9 0.7 fusion.12
  4.6 0.7 reshape.96
  6.3 1.5 %copy.61 = bf16[8,8,2,3,16,128]{5,4,3,2,1,0:T(8,128)(2,1)} copy(bf16[8,8,2,3,16,128]{5,1,4,0,3,2:T(8,128)(2,1)S(1)} %maximum_bitcast_fusion) | data formatting | bytes 3145728 | tf_op jit(solution)/shard_map/transpose | solution.py:13
  7.8 15.2 %all-to-all-start = ((bf16[64,2,3,16,128]{4,3,2,1,0:T(8,128)(2,1)}), bf16[64,2,3,16,128]{4,3,2,1,0:T(8,128)(2,1)S(1)}, u32[]{:S(2)}, u32[]{:S(2)}) async-start(bf16[64,2,3,16,128]{4,3,2,1,0:T(8,128)(2,1)} %bitcast.4), calls=%async_computation | async-start | bytes 3145728 | tf_op jit(solution)/shard_map/all_to_all | solution.py:14
  23.6 1.8 %select_reduce_fusion = f32[3,16,64,64]{3,2,1,0:T(8,128)S(1)} fusion(f32[3,16,6]{2,1,0:T(8,128)S(1)} %get-tuple-element.8, f32[64,64,6]{1,0,2:T(8,128)S(1)} %and_select_fusion, f32[3,16,6]{2,1,0:T(8,128)S(1)} %get-tuple-element.7, pred[64,64,6]{1,0,2:T(8,128)(4,1)S(1)} %broadcast_compare_fusion), kind=kLoop, calls=%fused_computation | loop fusion | flops 3342336 | bytes 911616 | tf_op jit(solution)/shard_map/reduce_prod | solution.py:74
  25.5 35.6 %all-to-all-done = bf16[64,2,3,16,128]{4,3,2,1,0:T(8,128)(2,1)S(1)} async-done(((bf16[64,2,3,16,128]{4,3,2,1,0:T(8,128)(2,1)}), bf16[64,2,3,16,128]{4,3,2,1,0:T(8,128)(2,1)S(1)}, u32[]{:S(2)}, u32[]{:S(2)}) %all-to-all-start) | async-done | bytes 1572896 | tf_op jit(solution)/shard_map/all_to_all | solution.py:14
  61.3 1.0 fusion.18
  62.3 2.7 %fusion.15 = bf16[64,3,16,128]{3,0,2,1:T(8,128)(2,1)S(1)} fusion(f32[3,16,64,64]{3,2,1,0:T(8,128)S(1)} %select_reduce_fusion, f32[3,16,128,64]{2,3,1,0:T(8,128)S(1)} %fusion.18, bf16[64,1,3,16,128]{4,3,2,1,0:T(8,128)(2,1)S(1)} %get-tuple-element.5), kind=kOutput, calls=%fused_computation.23 | convolution fusion | flops 303169536 | bytes 3932160 | tf_op jit(solution)/shard_map/kied,ekic->dkic/dot_general | solution.py:78
  65.0 1.4 copy.66
  66.4 8.9 %all-to-all-start.1 = ((bf16[64,3,16,128]{3,2,1,0:T(8,128)(2,1)}), bf16[64,3,16,128]{3,2,1,0:T(8,128)(2,1)S(1)}, u32[]{:S(2)}, u32[]{:S(2)}) async-start(bf16[64,3,16,128]{3,2,1,0:T(8,128)(2,1)} %copy.66), calls=%async_computation.1 | async-start | bytes 1572864 | tf_op jit(solution)/shard_map/all_to_all | solution.py:20
  75.6 20.9 %all-to-all-done.1 = bf16[64,3,16,128]{3,2,1,0:T(8,128)(2,1)S(1)} async-done(((bf16[64,3,16,128]{3,2,1,0:T(8,128)(2,1)}), bf16[64,3,16,128]{3,2,1,0:T(8,128)(2,1)S(1)}, u32[]{:S(2)}, u32[]{:S(2)}) %all-to-all-start.1) | async-done | bytes 786464 | tf_op jit(solution)/shard_map/all_to_all | solution.py:20
  97.1 0.8 fusion.13
  98.0 0.7 fusion.19
  98.6 0.5 copy-done.3
  99.4 6.6 %fusion.4 = bf16[2,96,4096]{2,1,0:T(8,128)(2,1)} fusion(bf16[1024,4096]{1,0:T(8,128)(2,1)} %param.19, bf16[2,2,96,1024]{3,2,1,0:T(8,128)(2,1)S(1)} %bitcast.91, s32[]{:T(128)S(6)} %select_n.56), kind=kOutput, calls=%fused_computation.5 | convolution fusion | flops 1611399168 | bytes 10354692 | tf_op jit(solution)/shard_map/yrc,cw->yrw/dot_general | solution.py:103
  106.0 4.5 %collective-permute-start = (bf16[2,96,4096]{2,1,0:T(8,128)(2,1)}, bf16[2,96,4096]{2,1,0:T(8,128)(2,1)}, u32[]{:S(2)}, u32[]{:S(2)}) collective-permute-start(bf16[2,96,4096]{2,1,0:T(8,128)(2,1)} %fusion.4), channel_id=1, source_target_pairs={{0,1},{1,0},{2,3},{3,2},{4,5},{5,4},{6,7},{7,6},{8,9},{9,8},{10,11... | collective-permute-start | bytes 4718600 | tf_op jit(solution)/shard_map/ppermute | solution.py:92
  110.5 5.3 %fusion.2 = f32[2,96,4096]{2,1,0:T(8,128)S(1)} fusion(bf16[1024,4096]{1,0:T(8,128)(2,1)} %param.19, bf16[2,2,96,1024]{3,2,1,0:T(8,128)(2,1)} %bitcast.92, s32[]{:T(128)S(6)} %select_n.53), kind=kOutput, calls=%fused_computation.3 | convolution fusion | flops 1610612736 | bytes 11927556 | tf_op jit(solution)/shard_map/yrc,cw->yrw/dot_general | solution.py:105
  115.8 2.2 %fusion.17 = bf16[96,4096]{1,0:T(8,128)(2,1)} fusion(f32[2,96,4096]{2,1,0:T(8,128)S(1)} %fusion.2, s32[]{:T(128)S(6)} %select_n.57, bf16[2,96,4096]{2,1,0:T(8,128)(2,1)} %collective-permute-done), kind=kLoop, calls=%fused_computation.25 | loop fusion | flops 1179648 | bytes 3145732 | tf_op jit(solution)/shard_map/convert_element_type | solution.py:108
  118.4 19.0 %collective-permute-done.1 = bf16[96,4096]{1,0:T(8,128)(2,1)} collective-permute-done((bf16[96,4096]{1,0:T(8,128)(2,1)}, bf16[96,4096]{1,0:T(8,128)(2,1)}, u32[]{:S(2)}, u32[]{:S(2)}) %collective-permute-start.1) | collective-permute-done | bytes 786464 | tf_op jit(solution)/shard_map/ppermute | solution.py:92
  137.4 2.5 %fusion.9 = bf16[96,4096]{1,0:T(8,128)(2,1)} fusion(bf16[96,4096]{1,0:T(8,128)(2,1)} %collective-permute-done.1, f32[2,96,4096]{2,1,0:T(8,128)S(1)} %fusion.2, s32[]{:T(128)S(6)} %select_n.55, bf16[2,96,4096]{2,1,0:T(8,128)(2,1)} %collective-permute-done), kind=kLoop, calls=%fused_computation.12 | loop fusion | flops 1966080 | bytes 3932164 | tf_op jit(solution)/shard_map/convert_element_type | solution.py:111
  (30 shorter events, 3.2 us)
Async XLA Ops:
  0.0 2.6 %copy-start = (bf16[3,128,128]{2,1,0:T(8,128)(2,1)S(1)}, bf16[3,128,128]{2,1,0:T(8,128)(2,1)}, u32[]{:S(2)}) copy-start(bf16[3,128,128]{2,1,0:T(8,128)(2,1)} %param.14) | copy-start | bytes 294916
  4.6 1.1 copy-start.2
  7.8 15.3 %copy-start.5 = (f32[6,384]{1,0:T(8,128)S(1)}, f32[6,384]{1,0:T(8,128)}, u32[]{:S(2)}) copy-start(f32[6,384]{1,0:T(8,128)} %param.18) | copy-start | bytes 27652
  7.8 53.2 %all-to-all-start = ((bf16[64,2,3,16,128]{4,3,2,1,0:T(8,128)(2,1)}), bf16[64,2,3,16,128]{4,3,2,1,0:T(8,128)(2,1)S(1)}, u32[]{:S(2)}, u32[]{:S(2)}) async-start(bf16[64,2,3,16,128]{4,3,2,1,0:T(8,128)(2,1)} %bitcast.4), calls=%async_computation | async-start | bytes 3145728 | tf_op jit(solution)/shard_map/all_to_all | solution.py:14
  65.0 10.4 %copy-start.6 = (bf16[128,3,3]{0,2,1:T(4,128)(2,1)S(1)}, bf16[128,3,3]{0,2,1:T(4,128)(2,1)}, u32[]{:S(2)}) copy-start(bf16[128,3,3]{0,2,1:T(4,128)(2,1)} %param.17) | copy-start | bytes 6916
  66.4 30.1 %all-to-all-start.1 = ((bf16[64,3,16,128]{3,2,1,0:T(8,128)(2,1)}), bf16[64,3,16,128]{3,2,1,0:T(8,128)(2,1)S(1)}, u32[]{:S(2)}, u32[]{:S(2)}) async-start(bf16[64,3,16,128]{3,2,1,0:T(8,128)(2,1)} %copy.66), calls=%async_computation.1 | async-start | bytes 1572864 | tf_op jit(solution)/shard_map/all_to_all | solution.py:20
  97.1 0.9 copy-start.4
  98.0 1.1 copy-start.3
  99.4 6.6 %copy-start.1 = (bf16[384,1024]{1,0:T(8,128)(2,1)}, bf16[384,1024]{1,0:T(8,128)(2,1)S(1)}, u32[]{:S(2)}) copy-start(bf16[384,1024]{1,0:T(8,128)(2,1)S(1)} %fusion.7) | copy-start | bytes 2359300
  106.0 9.8 %collective-permute-start = (bf16[2,96,4096]{2,1,0:T(8,128)(2,1)}, bf16[2,96,4096]{2,1,0:T(8,128)(2,1)}, u32[]{:S(2)}, u32[]{:S(2)}) collective-permute-start(bf16[2,96,4096]{2,1,0:T(8,128)(2,1)} %fusion.4), channel_id=1, source_target_pairs={{0,1},{1,0},{2,3},{3,2},{4,5},{5,4},{6,7},{7,6},{8,9},{9,8},{10,11... | collective-permute-start | bytes 4718600 | tf_op jit(solution)/shard_map/ppermute | solution.py:92
  118.0 19.4 %collective-permute-start.1 = (bf16[96,4096]{1,0:T(8,128)(2,1)}, bf16[96,4096]{1,0:T(8,128)(2,1)}, u32[]{:S(2)}, u32[]{:S(2)}) collective-permute-start(bf16[96,4096]{1,0:T(8,128)(2,1)} %fusion.17), channel_id=1, source_target_pairs={{0,2},{1,3},{2,0},{3,1},{4,6},{5,7},{6,4},{7,5},{8,10},{9,11},{10,... | collective-permute-start | bytes 2359304 | tf_op jit(solution)/shard_map/ppermute | solution.py:92

commit v6 on v5

--- a/solution.py
+++ b/solution.py
@@ -92,23 +92,28 @@
     return lax.ppermute(value, "chan", pairs)
 
 
-def scatter_sum(gated, out_weight):
+def scatter_sum(gated, out_weight, blocks=4):
     me = lax.axis_index("chan")
     core = me % 2
     chip = me // 2
     rows, chans = gated.shape
-    quarters = gated.reshape(2, 2, rows // 4, chans)
-    sent_rows = lax.dynamic_index_in_dim(quarters, 1 - core, axis=1, keepdims=False)
-    kept_rows = lax.dynamic_index_in_dim(quarters, core, axis=1, keepdims=False)
-    sent = jnp.einsum("yrc,cw->yrw", sent_rows, out_weight, preferred_element_type=jnp.float32)
-    half = exchange(sent.astype(jnp.bfloat16), 1)
-    kept = jnp.einsum("yrc,cw->yrw", kept_rows, out_weight, preferred_element_type=jnp.float32)
-    other = lax.dynamic_index_in_dim(kept, 1 - chip, axis=0, keepdims=False)
-    other = other + lax.dynamic_index_in_dim(half, 1 - chip, axis=0, keepdims=False).astype(jnp.float32)
-    quarter = exchange(other.astype(jnp.bfloat16), 2)
-    mine = lax.dynamic_index_in_dim(kept, chip, axis=0, keepdims=False)
-    mine = mine + lax.dynamic_index_in_dim(half, chip, axis=0, keepdims=False).astype(jnp.float32)
-    return (mine + quarter.astype(jnp.float32)).astype(jnp.bfloat16)
+    width = out_weight.shape[1] // blocks
+    pieces = []
+    for block in range(blocks):
+        weight = out_weight[:, block * width : (block + 1) * width]
+        product = jnp.dot(gated, weight, preferred_element_type=jnp.float32)
+        quarters = product.reshape(2, 2, rows // 4, width)
+        sent = lax.dynamic_index_in_dim(quarters, 1 - core, axis=1, keepdims=False)
+        kept = lax.dynamic_index_in_dim(quarters, core, axis=1, keepdims=False)
+        half = exchange(sent.astype(jnp.bfloat16), 1)
+        gated, half = lax.optimization_barrier((gated, half))
+        other = lax.dynamic_index_in_dim(kept, 1 - chip, axis=0, keepdims=False)
+        other = other + lax.dynamic_index_in_dim(half, 1 - chip, axis=0, keepdims=False).astype(jnp.float32)
+        quarter = exchange(other.astype(jnp.bfloat16), 2)
+        mine = lax.dynamic_index_in_dim(kept, chip, axis=0, keepdims=False)
+        mine = mine + lax.dynamic_index_in_dim(half, chip, axis=0, keepdims=False).astype(jnp.float32)
+        pieces.append((mine + quarter.astype(jnp.float32)).astype(jnp.bfloat16))
+    return jnp.concatenate(pieces, axis=1)
 
 
 def solution(mesh):

time: 140 us -> 138 us (0.986)
  waiting for transfers between devices: 75.5 us -> 66.8 us
  starting transfers between devices: 29 us -> 33 us
  other arithmetic: 8.98 us -> 11.6 us
    ppermute x2 -> x8, waiting for transfers between devices: 19 us -> 10.4 us  [exchange(): return lax.ppermute(value, 'chan', pairs)]
    ppermute x2 -> x8, starting transfers between devices: 4.89 us -> 8.8 us  [exchange(): return lax.ppermute(value, 'chan', pairs)]
    dot_general x2 -> x4, matrix products: 11.9 us -> 10.7 us  [scatter_sum(): product = jnp.dot(gated, weight, preferred_element_type=jnp.float32)]
    convert_element_type x1 -> x4, other arithmetic: 2.17 us -> 3.16 us  [scatter_sum(): quarter = exchange(other.astype(jnp.bfloat16), 2)]
    convert_element_type x1 -> x4, other arithmetic: 2.49 us -> 3.15 us  [scatter_sum(): pieces.append((mine + quarter.astype(jnp.float32)).astype(jnp.bfloat16))]
  transfers between devices with their start and end apart: 4 -> 10, of which waited for: 3 -> 8; matrix products, arithmetic and copies ran while one was open for 6% -> 8% of each run, Pallas kernels for 0% -> 0%
where the time goes in v6:
time: 138 us; the launch traced here: 137 us
  waiting for transfers between devices  66.8 us (48%)
  starting transfers between devices  33 us (24%)
  matrix products  17.1 us (12%)
  other arithmetic  11.6 us (8%)
  local copies, waits for them, and re-layouts  7.69 us (6%)
    all_to_all x1, waiting for transfers between devices, to_columns(): return lax.all_to_all(parts, 'seq', 0, 0, tiled=True)  35.5 us
    all_to_all x1, waiting for transfers between devices, from_columns(): back = lax.all_to_all(values, 'seq', 0, 0, tiled=True)  20.9 us
    all_to_all x1, starting transfers between devices, to_columns(): return lax.all_to_all(parts, 'seq', 0, 0, tiled=True)  15.2 us
    dot_general x4, matrix products, scatter_sum(): product = jnp.dot(gated, weight, preferred_element_type=jnp.float32)  10.7 us
    ppermute x8, waiting for transfers between devices, exchange(): return lax.ppermute(value, 'chan', pairs)  10.4 us
    all_to_all x1, starting transfers between devices, from_columns(): back = lax.all_to_all(values, 'seq', 0, 0, tiled=True)  8.97 us
    ppermute x8, starting transfers between devices, exchange(): return lax.ppermute(value, 'chan', pairs)  8.8 us
    convert_element_type x4, other arithmetic, scatter_sum(): quarter = exchange(other.astype(jnp.bfloat16), 2)  3.16 us
  transfers between devices with their start and end apart: 10, of which 8 were waited for; matrix products, arithmetic and copies ran while one was open for 8% of the time, Pallas kernels for 0%

profile of v6, /device:TPU:1, one launch (start us, length us, event | category | flops | bytes accessed | tf_op | source)
XLA Modules:
  0.0 136.6 jit_solution(13390879731137477840)
XLA Ops:
  0.0 1.7 %multiply_convert_fusion = bf16[384,1024]{1,0:T(8,128)(2,1)S(1)} fusion(bf16[384,1024]{1,0:T(8,128)(2,1)} %param.10, bf16[384,1024]{1,0:T(8,128)(2,1)} %param.11), kind=kLoop, calls=%fused_computation.15 | loop fusion | flops 1572864 | bytes 2359296 | tf_op jit(solution)/shard_map/convert_element_type | solution.py:45
  5.2 1.5 %copy.69 = bf16[8,8,2,3,16,128]{5,4,3,2,1,0:T(8,128)(2,1)} copy(bf16[8,8,2,3,16,128]{5,1,4,0,3,2:T(8,128)(2,1)S(1)} %maximum_bitcast_fusion) | data formatting | bytes 3145728 | tf_op jit(solution)/shard_map/transpose | solution.py:13
  6.7 15.2 %all-to-all-start = ((bf16[64,2,3,16,128]{4,3,2,1,0:T(8,128)(2,1)}), bf16[64,2,3,16,128]{4,3,2,1,0:T(8,128)(2,1)S(1)}, u32[]{:S(2)}, u32[]{:S(2)}) async-start(bf16[64,2,3,16,128]{4,3,2,1,0:T(8,128)(2,1)} %bitcast.4), calls=%async_computation | async-start | bytes 3145728 | tf_op jit(solution)/shard_map/all_to_all | solution.py:14
  22.6 1.8 %select_reduce_fusion = f32[3,16,64,64]{3,2,1,0:T(8,128)S(1)} fusion(f32[3,16,6]{2,1,0:T(8,128)S(1)} %get-tuple-element.22, f32[64,64,6]{1,0,2:T(8,128)S(1)} %and_select_fusion, f32[3,16,6]{2,1,0:T(8,128)S(1)} %get-tuple-element.21, pred[64,64,6]{1,0,2:T(8,128)(4,1)S(1)} %broadcast_compare_fusion), kind=kLoop, calls=%fused_computation | loop fusion | flops 3342336 | bytes 911616 | tf_op jit(solution)/shard_map/reduce_prod | solution.py:74
  24.4 35.5 %all-to-all-done = bf16[64,2,3,16,128]{4,3,2,1,0:T(8,128)(2,1)S(1)} async-done(((bf16[64,2,3,16,128]{4,3,2,1,0:T(8,128)(2,1)}), bf16[64,2,3,16,128]{4,3,2,1,0:T(8,128)(2,1)S(1)}, u32[]{:S(2)}, u32[]{:S(2)}) %all-to-all-start) | async-done | bytes 1572896 | tf_op jit(solution)/shard_map/all_to_all | solution.py:14
  60.2 1.0 fusion.17
  61.2 2.7 %fusion.15 = bf16[64,3,16,128]{3,0,2,1:T(8,128)(2,1)S(1)} fusion(f32[3,16,64,64]{3,2,1,0:T(8,128)S(1)} %select_reduce_fusion, f32[3,16,128,64]{2,3,1,0:T(8,128)S(1)} %fusion.17, bf16[64,1,3,16,128]{4,3,2,1,0:T(8,128)(2,1)S(1)} %get-tuple-element.19), kind=kOutput, calls=%fused_computation.23 | convolution fusion | flops 303169536 | bytes 3932160 | tf_op jit(solution)/shard_map/kied,ekic->dkic/dot_general | solution.py:78
  63.9 1.4 %copy.74 = bf16[64,3,16,128]{3,2,1,0:T(8,128)(2,1)} copy(bf16[64,3,16,128]{3,0,2,1:T(8,128)(2,1)S(1)} %fusion.15) | data formatting | bytes 1572864 | tf_op jit(solution)/shard_map/convert_element_type | solution.py:79
  65.3 9.0 %all-to-all-start.1 = ((bf16[64,3,16,128]{3,2,1,0:T(8,128)(2,1)}), bf16[64,3,16,128]{3,2,1,0:T(8,128)(2,1)S(1)}, u32[]{:S(2)}, u32[]{:S(2)}) async-start(bf16[64,3,16,128]{3,2,1,0:T(8,128)(2,1)} %copy.74), calls=%async_computation.1 | async-start | bytes 1572864 | tf_op jit(solution)/shard_map/all_to_all | solution.py:20
  74.5 20.9 %all-to-all-done.1 = bf16[64,3,16,128]{3,2,1,0:T(8,128)(2,1)S(1)} async-done(((bf16[64,3,16,128]{3,2,1,0:T(8,128)(2,1)}), bf16[64,3,16,128]{3,2,1,0:T(8,128)(2,1)S(1)}, u32[]{:S(2)}, u32[]{:S(2)}) %all-to-all-start.1) | async-done | bytes 786464 | tf_op jit(solution)/shard_map/all_to_all | solution.py:20
  98.3 2.9 %fusion.6 = f32[384,1024]{1,0:T(8,128)S(1)} fusion(bf16[384,1024]{1,0:T(8,128)(2,1)S(1)} %fusion.8, bf16[1024,4096]{1,0:T(8,128)(2,1)} %param.19), kind=kOutput, calls=%fused_computation.7 | convolution fusion | flops 805306368 | bytes 4456448 | tf_op jit(solution)/shard_map/dot_general | solution.py:104
  101.3 4.6 %collective-permute-start = (bf16[2,96,1024]{2,1,0:T(8,128)(2,1)S(1)}, bf16[2,96,1024]{2,1,0:T(8,128)(2,1)S(1)}, u32[]{:S(2)}, u32[]{:S(2)}) collective-permute-start(bf16[2,96,1024]{2,1,0:T(8,128)(2,1)S(1)} %fusion.20), channel_id=1, source_target_pairs={{0,1},{1,0},{2,3},{3,2},{4,5},{5,4},{6,7},{7,6},{8,9},{9,8},{10,11... | collective-permute-start | bytes 1179656 | tf_op jit(solution)/shard_map/ppermute | solution.py:92
  105.8 1.3 collective-permute-done
  107.2 2.7 %fusion.4 = f32[384,1024]{1,0:T(8,128)S(1)} fusion(bf16[384,1024]{1,0:T(8,128)(2,1)S(1)} %fusion.8, bf16[1024,4096]{1,0:T(8,128)(2,1)} %param.19), kind=kOutput, calls=%fused_computation.5 | convolution fusion | flops 805306368 | bytes 4456448 | tf_op jit(solution)/shard_map/dot_general | solution.py:104
  110.4 1.5 %collective-permute-done.2 = bf16[2,96,1024]{2,1,0:T(8,128)(2,1)} collective-permute-done((bf16[2,96,1024]{2,1,0:T(8,128)(2,1)S(1)}, bf16[2,96,1024]{2,1,0:T(8,128)(2,1)}, u32[]{:S(2)}, u32[]{:S(2)}) %collective-permute-start.2) | collective-permute-done | bytes 393248 | tf_op jit(solution)/shard_map/ppermute | solution.py:92
  111.9 2.6 %fusion.2 = f32[384,1024]{1,0:T(8,128)S(1)} fusion(bf16[384,1024]{1,0:T(8,128)(2,1)S(1)} %fusion.8, bf16[1024,4096]{1,0:T(8,128)(2,1)} %param.19), kind=kOutput, calls=%fused_computation.3 | convolution fusion | flops 805306368 | bytes 4456448 | tf_op jit(solution)/shard_map/dot_general | solution.py:104
  115.7 1.2 fusion.33
  118.4 1.2 collective-permute-start.3
  119.5 2.6 %fusion = f32[384,1024]{1,0:T(8,128)S(1)} fusion(bf16[384,1024]{1,0:T(8,128)(2,1)S(1)} %copy-done.5, bf16[1024,4096]{1,0:T(8,128)(2,1)} %param.19), kind=kOutput, calls=%fused_computation.1 | convolution fusion | flops 805306368 | bytes 4456448 | tf_op jit(solution)/shard_map/dot_general | solution.py:104
  123.3 1.1 fusion.35
  125.8 1.7 %collective-permute-done.3 = bf16[96,1024]{1,0:T(8,128)(2,1)S(1)} collective-permute-done((bf16[96,1024]{1,0:T(8,128)(2,1)S(1)}, bf16[96,1024]{1,0:T(8,128)(2,1)S(1)}, u32[]{:S(2)}, u32[]{:S(2)}) %collective-permute-start.3) | collective-permute-done | bytes 196640 | tf_op jit(solution)/shard_map/ppermute | solution.py:92
  127.5 1.0 fusion.32
  129.1 1.2 collective-permute-done.5
  131.3 4.3 %collective-permute-done.7 = bf16[96,1024]{1,0:T(8,128)(2,1)S(1)} collective-permute-done((bf16[96,1024]{1,0:T(8,128)(2,1)S(1)}, bf16[96,1024]{1,0:T(8,128)(2,1)S(1)}, u32[]{:S(2)}, u32[]{:S(2)}) %collective-permute-start.7) | collective-permute-done | bytes 196640 | tf_op jit(solution)/shard_map/ppermute | solution.py:92
  (65 shorter events, 15.7 us)
Async XLA Ops:
  0.0 1.7 %copy-start = (bf16[3,128,128]{2,1,0:T(8,128)(2,1)S(1)}, bf16[3,128,128]{2,1,0:T(8,128)(2,1)}, u32[]{:S(2)}) copy-start(bf16[3,128,128]{2,1,0:T(8,128)(2,1)} %param.14) | copy-start | bytes 294916
  1.7 1.4 copy-start.10
  3.3 1.4 %copy-start.2 = (bf16[384,1024]{1,0:T(8,128)(2,1)S(1)}, bf16[384,1024]{1,0:T(8,128)(2,1)}, u32[]{:S(2)}) copy-start(bf16[384,1024]{1,0:T(8,128)(2,1)} %param.13) | copy-start | bytes 2359300
  6.7 15.3 %copy-start.9 = (f32[6,384]{1,0:T(8,128)S(1)}, f32[6,384]{1,0:T(8,128)}, u32[]{:S(2)}) copy-start(f32[6,384]{1,0:T(8,128)} %param.18) | copy-start | bytes 27652
  6.7 53.2 %all-to-all-start = ((bf16[64,2,3,16,128]{4,3,2,1,0:T(8,128)(2,1)}), bf16[64,2,3,16,128]{4,3,2,1,0:T(8,128)(2,1)S(1)}, u32[]{:S(2)}, u32[]{:S(2)}) async-start(bf16[64,2,3,16,128]{4,3,2,1,0:T(8,128)(2,1)} %bitcast.4), calls=%async_computation | async-start | bytes 3145728 | tf_op jit(solution)/shard_map/all_to_all | solution.py:14
  63.9 10.4 %copy-start.11 = (bf16[128,3,3]{0,2,1:T(4,128)(2,1)S(1)}, bf16[128,3,3]{0,2,1:T(4,128)(2,1)}, u32[]{:S(2)}) copy-start(bf16[128,3,3]{0,2,1:T(4,128)(2,1)} %param.17) | copy-start | bytes 6916
  65.3 30.1 %all-to-all-start.1 = ((bf16[64,3,16,128]{3,2,1,0:T(8,128)(2,1)}), bf16[64,3,16,128]{3,2,1,0:T(8,128)(2,1)S(1)}, u32[]{:S(2)}, u32[]{:S(2)}) async-start(bf16[64,3,16,128]{3,2,1,0:T(8,128)(2,1)} %copy.74), calls=%async_computation.1 | async-start | bytes 1572864 | tf_op jit(solution)/shard_map/all_to_all | solution.py:20
  96.0 0.9 copy-start.8
  96.9 1.1 copy-start.3
  98.3 13.6 %copy-start.4 = (bf16[384,1024]{1,0:T(8,128)(2,1)}, bf16[384,1024]{1,0:T(8,128)(2,1)S(1)}, u32[]{:S(2)}) copy-start(bf16[384,1024]{1,0:T(8,128)(2,1)S(1)} %fusion.8) | copy-start | bytes 2359300
  101.2 8.7 %copy-start.1 = (f32[384,1024]{1,0:T(8,128)}, f32[384,1024]{1,0:T(8,128)S(1)}, u32[]{:S(2)}) copy-start(f32[384,1024]{1,0:T(8,128)S(1)} %fusion.6) | copy-start | bytes 4718596
  101.3 5.9 %collective-permute-start = (bf16[2,96,1024]{2,1,0:T(8,128)(2,1)S(1)}, bf16[2,96,1024]{2,1,0:T(8,128)(2,1)S(1)}, u32[]{:S(2)}, u32[]{:S(2)}) collective-permute-start(bf16[2,96,1024]{2,1,0:T(8,128)(2,1)S(1)} %fusion.20), channel_id=1, source_target_pairs={{0,1},{1,0},{2,3},{3,2},{4,5},{5,4},{6,7},{7,6},{8,9},{9,8},{10,11... | collective-permute-start | bytes 1179656 | tf_op jit(solution)/shard_map/ppermute | solution.py:92
  107.2 7.3 %copy-start.6 = (bf16[2,96,1024]{2,1,0:T(8,128)(2,1)}, bf16[2,96,1024]{2,1,0:T(8,128)(2,1)S(1)}, u32[]{:S(2)}) copy-start(bf16[2,96,1024]{2,1,0:T(8,128)(2,1)S(1)} %collective-permute-done) | copy-start | bytes 1179652
  110.0 1.9 %collective-permute-start.2 = (bf16[2,96,1024]{2,1,0:T(8,128)(2,1)S(1)}, bf16[2,96,1024]{2,1,0:T(8,128)(2,1)}, u32[]{:S(2)}, u32[]{:S(2)}) collective-permute-start(bf16[2,96,1024]{2,1,0:T(8,128)(2,1)S(1)} %fusion.21), channel_id=1, source_target_pairs={{0,1},{1,0},{2,3},{3,2},{4,5},{5,4},{6,7},{7,6},{8,9},{9,8},{10,11... | collective-permute-start | bytes 1179656 | tf_op jit(solution)/shard_map/ppermute | solution.py:92
  115.3 4.2 %collective-permute-start.4 = (bf16[2,96,1024]{2,1,0:T(8,128)(2,1)}, bf16[2,96,1024]{2,1,0:T(8,128)(2,1)}, u32[]{:S(2)}, u32[]{:S(2)}) collective-permute-start(bf16[2,96,1024]{2,1,0:T(8,128)(2,1)} %fusion.22), channel_id=1, source_target_pairs={{0,1},{1,0},{2,3},{3,2},{4,5},{5,4},{6,7},{7,6},{8,9},{9,8},{10,11... | collective-permute-start | bytes 1179656 | tf_op jit(solution)/shard_map/ppermute | solution.py:92
  115.7 3.8 %copy-start.5 = (bf16[384,1024]{1,0:T(8,128)(2,1)S(1)}, bf16[384,1024]{1,0:T(8,128)(2,1)}, u32[]{:S(2)}) copy-start(bf16[384,1024]{1,0:T(8,128)(2,1)} %copy-done.4) | copy-start | bytes 2359300
  116.9 6.4 %collective-permute-start.1 = (bf16[96,1024]{1,0:T(8,128)(2,1)S(1)}, bf16[96,1024]{1,0:T(8,128)(2,1)S(1)}, u32[]{:S(2)}, u32[]{:S(2)}) collective-permute-start(bf16[96,1024]{1,0:T(8,128)(2,1)S(1)} %fusion.33), channel_id=1, source_target_pairs={{0,2},{1,3},{2,0},{3,1},{4,6},{5,7},{6,4},{7,5},{8,10},{9,11},{10,... | collective-permute-start | bytes 589832 | tf_op jit(solution)/shard_map/ppermute | solution.py:92
  118.3 5.0 %copy-start.7 = (bf16[2,96,1024]{2,1,0:T(8,128)(2,1)S(1)}, bf16[2,96,1024]{2,1,0:T(8,128)(2,1)}, u32[]{:S(2)}) copy-start(bf16[2,96,1024]{2,1,0:T(8,128)(2,1)} %copy-done.6) | copy-start | bytes 1179652
  118.4 9.2 %collective-permute-start.3 = (bf16[96,1024]{1,0:T(8,128)(2,1)S(1)}, bf16[96,1024]{1,0:T(8,128)(2,1)S(1)}, u32[]{:S(2)}, u32[]{:S(2)}) collective-permute-start(bf16[96,1024]{1,0:T(8,128)(2,1)S(1)} %fusion.30), channel_id=1, source_target_pairs={{0,2},{1,3},{2,0},{3,1},{4,6},{5,7},{6,4},{7,5},{8,10},{9,11},{10,... | collective-permute-start | bytes 589832 | tf_op jit(solution)/shard_map/ppermute | solution.py:92
  122.2 6.3 %collective-permute-start.6 = (bf16[2,96,1024]{2,1,0:T(8,128)(2,1)S(1)}, bf16[2,96,1024]{2,1,0:T(8,128)(2,1)S(1)}, u32[]{:S(2)}, u32[]{:S(2)}) collective-permute-start(bf16[2,96,1024]{2,1,0:T(8,128)(2,1)S(1)} %fusion.23), channel_id=1, source_target_pairs={{0,1},{1,0},{2,3},{3,2},{4,5},{5,4},{6,7},{7,6},{8,9},{9,8},{10,11... | collective-permute-start | bytes 1179656 | tf_op jit(solution)/shard_map/ppermute | solution.py:92
  125.4 5.0 %collective-permute-start.5 = (bf16[96,1024]{1,0:T(8,128)(2,1)S(1)}, bf16[96,1024]{1,0:T(8,128)(2,1)S(1)}, u32[]{:S(2)}, u32[]{:S(2)}) collective-permute-start(bf16[96,1024]{1,0:T(8,128)(2,1)S(1)} %fusion.27), channel_id=1, source_target_pairs={{0,2},{1,3},{2,0},{3,1},{4,6},{5,7},{6,4},{7,5},{8,10},{9,11},{10,... | collective-permute-start | bytes 589832 | tf_op jit(solution)/shard_map/ppermute | solution.py:92
  128.6 7.0 %collective-permute-start.7 = (bf16[96,1024]{1,0:T(8,128)(2,1)S(1)}, bf16[96,1024]{1,0:T(8,128)(2,1)S(1)}, u32[]{:S(2)}, u32[]{:S(2)}) collective-permute-start(bf16[96,1024]{1,0:T(8,128)(2,1)S(1)} %fusion.24), channel_id=1, source_target_pairs={{0,2},{1,3},{2,0},{3,1},{4,6},{5,7},{6,4},{7,5},{8,10},{9,11},{10,... | collective-permute-start | bytes 589832 | tf_op jit(solution)/shard_map/ppermute | solution.py:92

commit v7 on v5

--- a/solution.py
+++ b/solution.py
@@ -2,6 +2,7 @@
 import jax.numpy as jnp
 from jax import lax
 from jax.sharding import PartitionSpec as P
+
 
 ROW_SPLIT = 8
 
@@ -92,23 +93,33 @@
     return lax.ppermute(value, "chan", pairs)
 
 
-def scatter_sum(gated, out_weight):
+def scatter_sum(gated, out_weight, blocks=4):
     me = lax.axis_index("chan")
     core = me % 2
     chip = me // 2
-    rows, chans = gated.shape
-    quarters = gated.reshape(2, 2, rows // 4, chans)
-    sent_rows = lax.dynamic_index_in_dim(quarters, 1 - core, axis=1, keepdims=False)
-    kept_rows = lax.dynamic_index_in_dim(quarters, core, axis=1, keepdims=False)
-    sent = jnp.einsum("yrc,cw->yrw", sent_rows, out_weight, preferred_element_type=jnp.float32)
+    width = out_weight.shape[1] // blocks
+    pieces = []
+    for block in range(blocks):
+        pieces.append(scatter_block(gated, out_weight, block, width, core, chip))
+        gated = pieces[-1][1]
+    return jnp.concatenate([piece for piece, _ in pieces], axis=1)
+
+
+def scatter_block(gated, out_weight, block, width, core, chip):
+    rows = gated.shape[0]
+    weight = out_weight[:, block * width : (block + 1) * width]
+    product = jnp.dot(gated, weight, preferred_element_type=jnp.float32)
+    quarters = product.reshape(2, 2, rows // 4, width)
+    sent = lax.dynamic_index_in_dim(quarters, 1 - core, axis=1, keepdims=False)
+    kept = lax.dynamic_index_in_dim(quarters, core, axis=1, keepdims=False)
     half = exchange(sent.astype(jnp.bfloat16), 1)
-    kept = jnp.einsum("yrc,cw->yrw", kept_rows, out_weight, preferred_element_type=jnp.float32)
     other = lax.dynamic_index_in_dim(kept, 1 - chip, axis=0, keepdims=False)
     other = other + lax.dynamic_index_in_dim(half, 1 - chip, axis=0, keepdims=False).astype(jnp.float32)
-    quarter = exchange(other.astype(jnp.bfloat16), 2)
+    gated, other = lax.optimization_barrier((gated, other.astype(jnp.bfloat16)))
+    quarter = exchange(other, 2)
     mine = lax.dynamic_index_in_dim(kept, chip, axis=0, keepdims=False)
     mine = mine + lax.dynamic_index_in_dim(half, chip, axis=0, keepdims=False).astype(jnp.float32)
-    return (mine + quarter.astype(jnp.float32)).astype(jnp.bfloat16)
+    return (mine + quarter.astype(jnp.float32)).astype(jnp.bfloat16), gated
 
 
 def solution(mesh):

time: 140 us -> 138 us (0.986)
  waiting for transfers between devices: 75.5 us -> 68.6 us
  starting transfers between devices: 29 us -> 32.6 us
    ppermute x2 -> x8, waiting for transfers between devices: 19 us -> 12.1 us  [exchange(): return lax.ppermute(value, 'chan', pairs)]
    ppermute x2 -> x8, starting transfers between devices: 4.89 us -> 8.4 us  [exchange(): return lax.ppermute(value, 'chan', pairs)]
    dot_general x2 -> x4, matrix products: 11.9 us -> 10.9 us  [scatter_block(): product = jnp.dot(gated, weight, preferred_element_type=jnp.float32)]
    convert_element_type x2 -> x8, other arithmetic: 4.66 us -> 4.12 us  [the longest x4 2.23 us: scatter_block(): return ((mine + quarter.astype(jnp.float32)).astype(jnp.bfloat16), gated)]
  transfers between devices with their start and end apart: 4 -> 10, of which waited for: 3 -> 9; matrix products, arithmetic and copies ran while one was open for 6% -> 6% of each run, Pallas kernels for 0% -> 0%
where the time goes in v7:
time: 138 us; the launch traced here: 137 us
  waiting for transfers between devices  68.6 us (50%)
  starting transfers between devices  32.6 us (24%)
  matrix products  17.2 us (12%)
  other arithmetic  9.41 us (7%)
  local copies, waits for them, and re-layouts  8.86 us (6%)
    all_to_all x1, waiting for transfers between devices, to_columns(): return lax.all_to_all(parts, 'seq', 0, 0, tiled=True)  35.6 us
    all_to_all x1, waiting for transfers between devices, from_columns(): back = lax.all_to_all(values, 'seq', 0, 0, tiled=True)  20.9 us
    all_to_all x1, starting transfers between devices, to_columns(): return lax.all_to_all(parts, 'seq', 0, 0, tiled=True)  15.2 us
    ppermute x8, waiting for transfers between devices, exchange(): return lax.ppermute(value, 'chan', pairs)  12.1 us
    dot_general x4, matrix products, scatter_block(): product = jnp.dot(gated, weight, preferred_element_type=jnp.float32)  10.9 us
    all_to_all x1, starting transfers between devices, from_columns(): back = lax.all_to_all(values, 'seq', 0, 0, tiled=True)  8.93 us
    ppermute x8, starting transfers between devices, exchange(): return lax.ppermute(value, 'chan', pairs)  8.4 us
  transfers between devices with their start and end apart: 10, of which 9 were waited for; matrix products, arithmetic and copies ran while one was open for 6% of the time, Pallas kernels for 0%

profile of v7, /device:TPU:1, one launch (start us, length us, event | category | flops | bytes accessed | tf_op | source)
XLA Modules:
  0.0 137.1 jit_solution(15526365110025426507)
XLA Ops:
  0.0 1.7 %multiply_convert_fusion = bf16[384,1024]{1,0:T(8,128)(2,1)S(1)} fusion(bf16[384,1024]{1,0:T(8,128)(2,1)} %param.10, bf16[384,1024]{1,0:T(8,128)(2,1)} %param.11), kind=kLoop, calls=%fused_computation.15 | loop fusion | flops 1572864 | bytes 2359296 | tf_op jit(solution)/shard_map/convert_element_type | solution.py:46
  5.6 1.5 %copy.69 = bf16[8,8,2,3,16,128]{5,4,3,2,1,0:T(8,128)(2,1)} copy(bf16[8,8,2,3,16,128]{5,1,4,0,3,2:T(8,128)(2,1)S(1)} %maximum_bitcast_fusion) | data formatting | bytes 3145728 | tf_op jit(solution)/shard_map/transpose | solution.py:14
  7.2 15.2 %all-to-all-start = ((bf16[64,2,3,16,128]{4,3,2,1,0:T(8,128)(2,1)}), bf16[64,2,3,16,128]{4,3,2,1,0:T(8,128)(2,1)S(1)}, u32[]{:S(2)}, u32[]{:S(2)}) async-start(bf16[64,2,3,16,128]{4,3,2,1,0:T(8,128)(2,1)} %bitcast.4), calls=%async_computation | async-start | bytes 3145728 | tf_op jit(solution)/shard_map/all_to_all | solution.py:15
  23.0 1.8 %select_reduce_fusion = f32[3,16,64,64]{3,2,1,0:T(8,128)S(1)} fusion(f32[3,16,6]{2,1,0:T(8,128)S(1)} %get-tuple-element.22, f32[64,64,6]{1,0,2:T(8,128)S(1)} %and_select_fusion, f32[3,16,6]{2,1,0:T(8,128)S(1)} %get-tuple-element.21, pred[64,64,6]{1,0,2:T(8,128)(4,1)S(1)} %broadcast_compare_fusion), kind=kLoop, calls=%fused_computation | loop fusion | flops 3342336 | bytes 911616 | tf_op jit(solution)/shard_map/reduce_prod | solution.py:75
  24.8 35.6 %all-to-all-done = bf16[64,2,3,16,128]{4,3,2,1,0:T(8,128)(2,1)S(1)} async-done(((bf16[64,2,3,16,128]{4,3,2,1,0:T(8,128)(2,1)}), bf16[64,2,3,16,128]{4,3,2,1,0:T(8,128)(2,1)S(1)}, u32[]{:S(2)}, u32[]{:S(2)}) %all-to-all-start) | async-done | bytes 1572896 | tf_op jit(solution)/shard_map/all_to_all | solution.py:15
  60.7 1.0 fusion.17
  61.7 2.7 %fusion.15 = bf16[64,3,16,128]{3,0,2,1:T(8,128)(2,1)S(1)} fusion(f32[3,16,64,64]{3,2,1,0:T(8,128)S(1)} %select_reduce_fusion, f32[3,16,128,64]{2,3,1,0:T(8,128)S(1)} %fusion.17, bf16[64,1,3,16,128]{4,3,2,1,0:T(8,128)(2,1)S(1)} %get-tuple-element.19), kind=kOutput, calls=%fused_computation.23 | convolution fusion | flops 303169536 | bytes 3932160 | tf_op jit(solution)/shard_map/kied,ekic->dkic/dot_general | solution.py:79
  64.4 1.4 %copy.74 = bf16[64,3,16,128]{3,2,1,0:T(8,128)(2,1)} copy(bf16[64,3,16,128]{3,0,2,1:T(8,128)(2,1)S(1)} %fusion.15) | data formatting | bytes 1572864 | tf_op jit(solution)/shard_map/convert_element_type | solution.py:80
  65.8 8.9 %all-to-all-start.1 = ((bf16[64,3,16,128]{3,2,1,0:T(8,128)(2,1)}), bf16[64,3,16,128]{3,2,1,0:T(8,128)(2,1)S(1)}, u32[]{:S(2)}, u32[]{:S(2)}) async-start(bf16[64,3,16,128]{3,2,1,0:T(8,128)(2,1)} %copy.74), calls=%async_computation.1 | async-start | bytes 1572864 | tf_op jit(solution)/shard_map/all_to_all | solution.py:21
  75.0 20.9 %all-to-all-done.1 = bf16[64,3,16,128]{3,2,1,0:T(8,128)(2,1)S(1)} async-done(((bf16[64,3,16,128]{3,2,1,0:T(8,128)(2,1)}), bf16[64,3,16,128]{3,2,1,0:T(8,128)(2,1)S(1)}, u32[]{:S(2)}, u32[]{:S(2)}) %all-to-all-start.1) | async-done | bytes 786464 | tf_op jit(solution)/shard_map/all_to_all | solution.py:21
  98.7 2.9 %fusion.6 = f32[384,1024]{1,0:T(8,128)S(1)} fusion(bf16[384,1024]{1,0:T(8,128)(2,1)S(1)} %fusion.8, bf16[1024,4096]{1,0:T(8,128)(2,1)} %param.19), kind=kOutput, calls=%fused_computation.7 | convolution fusion | flops 805306368 | bytes 4456448 | tf_op jit(solution)/shard_map/dot_general | solution.py:111
  101.7 4.6 %collective-permute-start = (bf16[2,96,1024]{2,1,0:T(8,128)(2,1)S(1)}, bf16[2,96,1024]{2,1,0:T(8,128)(2,1)S(1)}, u32[]{:S(2)}, u32[]{:S(2)}) collective-permute-start(bf16[2,96,1024]{2,1,0:T(8,128)(2,1)S(1)} %fusion.20), channel_id=1, source_target_pairs={{0,1},{1,0},{2,3},{3,2},{4,5},{5,4},{6,7},{7,6},{8,9},{9,8},{10,11... | collective-permute-start | bytes 1179656 | tf_op jit(solution)/shard_map/ppermute | solution.py:93
  106.2 1.3 collective-permute-done
  108.4 2.6 %fusion.4 = f32[384,1024]{1,0:T(8,128)S(1)} fusion(bf16[384,1024]{1,0:T(8,128)(2,1)S(1)} %fusion.8, bf16[1024,4096]{1,0:T(8,128)(2,1)} %param.19), kind=kOutput, calls=%fused_computation.5 | convolution fusion | flops 805306368 | bytes 4456448 | tf_op jit(solution)/shard_map/dot_general | solution.py:111
  111.5 1.3 collective-permute-done.2
  113.7 2.6 %fusion.2 = f32[384,1024]{1,0:T(8,128)S(1)} fusion(bf16[384,1024]{1,0:T(8,128)(2,1)S(1)} %copy-done.5, bf16[1024,4096]{1,0:T(8,128)(2,1)} %param.19), kind=kOutput, calls=%fused_computation.3 | convolution fusion | flops 805306368 | bytes 4456448 | tf_op jit(solution)/shard_map/dot_general | solution.py:111
  117.9 1.1 collective-permute-start.3
  119.2 1.0 fusion.27
  120.2 2.9 %fusion = f32[384,1024]{1,0:T(8,128)S(1)} fusion(bf16[384,1024]{1,0:T(8,128)(2,1)} %copy-done.4, bf16[1024,4096]{1,0:T(8,128)(2,1)} %param.19), kind=kOutput, calls=%fused_computation.1 | convolution fusion | flops 805306368 | bytes 4456448 | tf_op jit(solution)/shard_map/dot_general | solution.py:111
  124.6 3.6 %collective-permute-done.3 = bf16[96,1024]{1,0:T(8,128)(2,1)S(1)} collective-permute-done((bf16[96,1024]{1,0:T(8,128)(2,1)S(1)}, bf16[96,1024]{1,0:T(8,128)(2,1)S(1)}, u32[]{:S(2)}, u32[]{:S(2)}) %collective-permute-start.3) | collective-permute-done | bytes 196640 | tf_op jit(solution)/shard_map/ppermute | solution.py:93
  128.2 1.1 fusion.32
  129.9 2.6 %collective-permute-done.5 = bf16[96,1024]{1,0:T(8,128)(2,1)S(1)} collective-permute-done((bf16[96,1024]{1,0:T(8,128)(2,1)S(1)}, bf16[96,1024]{1,0:T(8,128)(2,1)S(1)}, u32[]{:S(2)}, u32[]{:S(2)}) %collective-permute-start.5) | collective-permute-done | bytes 196640 | tf_op jit(solution)/shard_map/ppermute | solution.py:93
  132.4 1.0 fusion.29
  133.4 2.6 %collective-permute-done.7 = bf16[96,1024]{1,0:T(8,128)(2,1)S(1)} collective-permute-done((bf16[96,1024]{1,0:T(8,128)(2,1)S(1)}, bf16[96,1024]{1,0:T(8,128)(2,1)S(1)}, u32[]{:S(2)}, u32[]{:S(2)}) %collective-permute-start.7) | collective-permute-done | bytes 196640 | tf_op jit(solution)/shard_map/ppermute | solution.py:93
  (69 shorter events, 14.8 us)
Async XLA Ops:
  0.0 1.7 %copy-start = (bf16[3,128,128]{2,1,0:T(8,128)(2,1)S(1)}, bf16[3,128,128]{2,1,0:T(8,128)(2,1)}, u32[]{:S(2)}) copy-start(bf16[3,128,128]{2,1,0:T(8,128)(2,1)} %param.14) | copy-start | bytes 294916
  1.7 1.4 copy-start.12
  4.0 1.1 copy-start.2
  7.2 15.3 %copy-start.11 = (f32[6,384]{1,0:T(8,128)S(1)}, f32[6,384]{1,0:T(8,128)}, u32[]{:S(2)}) copy-start(f32[6,384]{1,0:T(8,128)} %param.18) | copy-start | bytes 27652
  7.2 53.2 %all-to-all-start = ((bf16[64,2,3,16,128]{4,3,2,1,0:T(8,128)(2,1)}), bf16[64,2,3,16,128]{4,3,2,1,0:T(8,128)(2,1)S(1)}, u32[]{:S(2)}, u32[]{:S(2)}) async-start(bf16[64,2,3,16,128]{4,3,2,1,0:T(8,128)(2,1)} %bitcast.4), calls=%async_computation | async-start | bytes 3145728 | tf_op jit(solution)/shard_map/all_to_all | solution.py:15
  64.4 10.4 %copy-start.13 = (bf16[128,3,3]{0,2,1:T(4,128)(2,1)S(1)}, bf16[128,3,3]{0,2,1:T(4,128)(2,1)}, u32[]{:S(2)}) copy-start(bf16[128,3,3]{0,2,1:T(4,128)(2,1)} %param.17) | copy-start | bytes 6916
  65.8 30.1 %all-to-all-start.1 = ((bf16[64,3,16,128]{3,2,1,0:T(8,128)(2,1)}), bf16[64,3,16,128]{3,2,1,0:T(8,128)(2,1)S(1)}, u32[]{:S(2)}, u32[]{:S(2)}) async-start(bf16[64,3,16,128]{3,2,1,0:T(8,128)(2,1)} %copy.74), calls=%async_computation.1 | async-start | bytes 1572864 | tf_op jit(solution)/shard_map/all_to_all | solution.py:21
  96.4 0.9 copy-start.10
  97.3 1.1 copy-start.3
  98.7 9.7 %copy-start.4 = (bf16[384,1024]{1,0:T(8,128)(2,1)}, bf16[384,1024]{1,0:T(8,128)(2,1)S(1)}, u32[]{:S(2)}) copy-start(bf16[384,1024]{1,0:T(8,128)(2,1)S(1)} %fusion.8) | copy-start | bytes 2359300
  101.7 5.9 %collective-permute-start = (bf16[2,96,1024]{2,1,0:T(8,128)(2,1)S(1)}, bf16[2,96,1024]{2,1,0:T(8,128)(2,1)S(1)}, u32[]{:S(2)}, u32[]{:S(2)}) collective-permute-start(bf16[2,96,1024]{2,1,0:T(8,128)(2,1)S(1)} %fusion.20), channel_id=1, source_target_pairs={{0,1},{1,0},{2,3},{3,2},{4,5},{5,4},{6,7},{7,6},{8,9},{9,8},{10,11... | collective-permute-start | bytes 1179656 | tf_op jit(solution)/shard_map/ppermute | solution.py:93
  107.6 3.4 %copy-start.6 = (bf16[2,96,1024]{2,1,0:T(8,128)(2,1)}, bf16[2,96,1024]{2,1,0:T(8,128)(2,1)S(1)}, u32[]{:S(2)}) copy-start(bf16[2,96,1024]{2,1,0:T(8,128)(2,1)S(1)} %collective-permute-done) | copy-start | bytes 1179652
  111.0 5.3 %copy-start.1 = (f32[384,1024]{1,0:T(8,128)}, f32[384,1024]{1,0:T(8,128)S(1)}, u32[]{:S(2)}) copy-start(f32[384,1024]{1,0:T(8,128)S(1)} %fusion.4) | copy-start | bytes 4718596
  111.0 2.7 %copy-start.5 = (bf16[384,1024]{1,0:T(8,128)(2,1)S(1)}, bf16[384,1024]{1,0:T(8,128)(2,1)}, u32[]{:S(2)}) copy-start(bf16[384,1024]{1,0:T(8,128)(2,1)} %copy-done.4) | copy-start | bytes 2359300
  111.1 1.8 %collective-permute-start.2 = (bf16[2,96,1024]{2,1,0:T(8,128)(2,1)S(1)}, bf16[2,96,1024]{2,1,0:T(8,128)(2,1)S(1)}, u32[]{:S(2)}, u32[]{:S(2)}) collective-permute-start(bf16[2,96,1024]{2,1,0:T(8,128)(2,1)S(1)} %fusion.21), channel_id=1, source_target_pairs={{0,1},{1,0},{2,3},{3,2},{4,5},{5,4},{6,7},{7,6},{8,9},{9,8},{10,11... | collective-permute-start | bytes 1179656 | tf_op jit(solution)/shard_map/ppermute | solution.py:93
  112.9 0.8 copy-start.8
  117.1 2.1 %collective-permute-start.4 = (bf16[2,96,1024]{2,1,0:T(8,128)(2,1)}, bf16[2,96,1024]{2,1,0:T(8,128)(2,1)}, u32[]{:S(2)}, u32[]{:S(2)}) collective-permute-start(bf16[2,96,1024]{2,1,0:T(8,128)(2,1)} %fusion.22), channel_id=1, source_target_pairs={{0,1},{1,0},{2,3},{3,2},{4,5},{5,4},{6,7},{7,6},{8,9},{9,8},{10,11... | collective-permute-start | bytes 1179656 | tf_op jit(solution)/shard_map/ppermute | solution.py:93
  117.5 6.5 %collective-permute-start.1 = (bf16[96,1024]{1,0:T(8,128)(2,1)}, bf16[96,1024]{1,0:T(8,128)(2,1)S(1)}, u32[]{:S(2)}, u32[]{:S(2)}) collective-permute-start(bf16[96,1024]{1,0:T(8,128)(2,1)} %fusion.33), channel_id=1, source_target_pairs={{0,2},{1,3},{2,0},{3,1},{4,6},{5,7},{6,4},{7,5},{8,10},{9,11},{10,... | collective-permute-start | bytes 589832 | tf_op jit(solution)/shard_map/ppermute | solution.py:93
  117.9 10.4 %collective-permute-start.3 = (bf16[96,1024]{1,0:T(8,128)(2,1)S(1)}, bf16[96,1024]{1,0:T(8,128)(2,1)S(1)}, u32[]{:S(2)}, u32[]{:S(2)}) collective-permute-start(bf16[96,1024]{1,0:T(8,128)(2,1)S(1)} %fusion.30), channel_id=1, source_target_pairs={{0,2},{1,3},{2,0},{3,1},{4,6},{5,7},{6,4},{7,5},{8,10},{9,11},{10,... | collective-permute-start | bytes 589832 | tf_op jit(solution)/shard_map/ppermute | solution.py:93
  120.1 3.9 %copy-start.7 = (bf16[2,96,1024]{2,1,0:T(8,128)(2,1)S(1)}, bf16[2,96,1024]{2,1,0:T(8,128)(2,1)}, u32[]{:S(2)}) copy-start(bf16[2,96,1024]{2,1,0:T(8,128)(2,1)} %copy-done.6) | copy-start | bytes 1179652
  123.0 5.2 %copy-start.9 = (bf16[2,96,1024]{2,1,0:T(8,128)(2,1)S(1)}, bf16[2,96,1024]{2,1,0:T(8,128)(2,1)}, u32[]{:S(2)}) copy-start(bf16[2,96,1024]{2,1,0:T(8,128)(2,1)} %copy-done.8) | copy-start | bytes 1179652
  123.1 6.2 %collective-permute-start.6 = (bf16[2,96,1024]{2,1,0:T(8,128)(2,1)S(1)}, bf16[2,96,1024]{2,1,0:T(8,128)(2,1)S(1)}, u32[]{:S(2)}, u32[]{:S(2)}) collective-permute-start(bf16[2,96,1024]{2,1,0:T(8,128)(2,1)S(1)} %fusion.23), channel_id=1, source_target_pairs={{0,1},{1,0},{2,3},{3,2},{4,5},{5,4},{6,7},{7,6},{8,9},{9,8},{10,11... | collective-permute-start | bytes 1179656 | tf_op jit(solution)/shard_map/ppermute | solution.py:93
  124.1 8.3 %collective-permute-start.5 = (bf16[96,1024]{1,0:T(8,128)(2,1)S(1)}, bf16[96,1024]{1,0:T(8,128)(2,1)S(1)}, u32[]{:S(2)}, u32[]{:S(2)}) collective-permute-start(bf16[96,1024]{1,0:T(8,128)(2,1)S(1)} %fusion.27), channel_id=1, source_target_pairs={{0,2},{1,3},{2,0},{3,1},{4,6},{5,7},{6,4},{7,5},{8,10},{9,11},{10,... | collective-permute-start | bytes 589832 | tf_op jit(solution)/shard_map/ppermute | solution.py:93
  129.4 6.7 %collective-permute-start.7 = (bf16[96,1024]{1,0:T(8,128)(2,1)S(1)}, bf16[96,1024]{1,0:T(8,128)(2,1)S(1)}, u32[]{:S(2)}, u32[]{:S(2)}) collective-permute-start(bf16[96,1024]{1,0:T(8,128)(2,1)S(1)} %fusion.24), channel_id=1, source_target_pairs={{0,2},{1,3},{2,0},{3,1},{4,6},{5,7},{6,4},{7,5},{8,10},{9,11},{10,... | collective-permute-start | bytes 589832 | tf_op jit(solution)/shard_map/ppermute | solution.py:93

commit v8 on v7

--- a/solution.py
+++ b/solution.py
@@ -93,7 +93,10 @@
     return lax.ppermute(value, "chan", pairs)
 
 
-def scatter_sum(gated, out_weight, blocks=4):
+BLOCKS = 8
+
+
+def scatter_sum(gated, out_weight, blocks=BLOCKS):
     me = lax.axis_index("chan")
     core = me % 2
     chip = me // 2
@@ -101,8 +104,7 @@
     pieces = []
     for block in range(blocks):
         pieces.append(scatter_block(gated, out_weight, block, width, core, chip))
-        gated = pieces[-1][1]
-    return jnp.concatenate([piece for piece, _ in pieces], axis=1)
+    return jnp.concatenate(pieces, axis=1)
 
 
 def scatter_block(gated, out_weight, block, width, core, chip):
@@ -115,11 +117,10 @@
     half = exchange(sent.astype(jnp.bfloat16), 1)
     other = lax.dynamic_index_in_dim(kept, 1 - chip, axis=0, keepdims=False)
     other = other + lax.dynamic_index_in_dim(half, 1 - chip, axis=0, keepdims=False).astype(jnp.float32)
-    gated, other = lax.optimization_barrier((gated, other.astype(jnp.bfloat16)))
-    quarter = exchange(other, 2)
+    quarter = exchange(other.astype(jnp.bfloat16), 2)
     mine = lax.dynamic_index_in_dim(kept, chip, axis=0, keepdims=False)
     mine = mine + lax.dynamic_index_in_dim(half, chip, axis=0, keepdims=False).astype(jnp.float32)
-    return (mine + quarter.astype(jnp.float32)).astype(jnp.bfloat16), gated
+    return (mine + quarter.astype(jnp.float32)).astype(jnp.bfloat16)
 
 
 def solution(mesh):

time: 138 us -> 135 us (0.978)
  other arithmetic: 9.41 us -> 4.1 us
  starting transfers between devices: 32.6 us -> 36.9 us
    ppermute x8 -> x16, starting transfers between devices: 8.4 us -> 12.7 us  [exchange(): return lax.ppermute(value, 'chan', pairs)]
    convert_element_type x8, other arithmetic: 4.12 us -> 0.21 us  [scatter_block(): quarter = exchange(other.astype(jnp.bfloat16), 2)]
    convert_element_type x1, other arithmetic: 1.71 us -> 0.3 us  [per_device(): mixed = (gate_in.astype(jnp.float32) * value_in.astype(jnp.float32)).asty...]
    dot_general x4 -> x8, matrix products: 10.9 us -> 9.65 us  [scatter_block(): product = jnp.dot(gated, weight, preferred_element_type=jnp.float32)]
    ppermute x8 -> x16, waiting for transfers between devices: 12.1 us -> 12.2 us  [exchange(): return lax.ppermute(value, 'chan', pairs)]
  transfers between devices with their start and end apart: 10 -> 18, of which waited for: 9 -> 9; matrix products, arithmetic and copies ran while one was open for 6% -> 2% of each run, Pallas kernels for 0% -> 0%
where the time goes in v8:
time: 135 us
  waiting for transfers between devices  68.7 us (51%)
  starting transfers between devices  36.9 us (27%)
  matrix products  16 us (12%)
  local copies, waits for them, and re-layouts  8.38 us (6%)
  other arithmetic  4.1 us (3%)
    all_to_all x1, waiting for transfers between devices, to_columns(): return lax.all_to_all(parts, 'seq', 0, 0, tiled=True)  35.6 us
    all_to_all x1, waiting for transfers between devices, from_columns(): back = lax.all_to_all(values, 'seq', 0, 0, tiled=True)  20.9 us
    all_to_all x1, starting transfers between devices, to_columns(): return lax.all_to_all(parts, 'seq', 0, 0, tiled=True)  15.2 us
    ppermute x16, starting transfers between devices, exchange(): return lax.ppermute(value, 'chan', pairs)  12.7 us
    ppermute x16, waiting for transfers between devices, exchange(): return lax.ppermute(value, 'chan', pairs)  12.2 us
    dot_general x8, matrix products, scatter_block(): product = jnp.dot(gated, weight, preferred_element_type=jnp.float32)  9.65 us
    all_to_all x1, starting transfers between devices, from_columns(): back = lax.all_to_all(values, 'seq', 0, 0, tiled=True)  8.92 us
    dot_general x1, matrix products, per_device(): work = jnp.einsum('kied,ekic->dkic', matrix, work, precision=hi)  2.72 us
  transfers between devices with their start and end apart: 18, of which 9 were waited for; matrix products, arithmetic and copies ran while one was open for 2% of the time, Pallas kernels for 0%

profile of v8, /device:TPU:1, one launch (start us, length us, event | category | flops | bytes accessed | tf_op | source)
XLA Modules:
  0.0 134.6 jit_solution(17017181841690408431)
XLA Ops:
  0.0 1.4 %copy.117 = bf16[48,8,8,128]{3,2,1,0:T(8,128)(2,1)S(1)} copy(bf16[48,8,8,128]{3,1,2,0:T(8,128)(2,1)} %bitcast.227) | data formatting | bytes 1572864
  5.2 1.5 %copy.85 = bf16[8,8,2,3,16,128]{5,4,3,2,1,0:T(8,128)(2,1)} copy(bf16[8,8,2,3,16,128]{5,1,4,0,3,2:T(8,128)(2,1)S(1)} %maximum_bitcast_fusion) | data formatting | bytes 3145728 | tf_op jit(solution)/shard_map/transpose | solution.py:14
  6.7 15.2 %all-to-all-start = ((bf16[64,2,3,16,128]{4,3,2,1,0:T(8,128)(2,1)}), bf16[64,2,3,16,128]{4,3,2,1,0:T(8,128)(2,1)S(1)}, u32[]{:S(2)}, u32[]{:S(2)}) async-start(bf16[64,2,3,16,128]{4,3,2,1,0:T(8,128)(2,1)} %bitcast.4), calls=%async_computation | async-start | bytes 3145728 | tf_op jit(solution)/shard_map/all_to_all | solution.py:15
  22.6 1.8 %select_reduce_fusion = f32[3,16,64,64]{3,2,1,0:T(8,128)S(1)} fusion(f32[3,16,6]{2,1,0:T(8,128)S(1)} %get-tuple-element.8, f32[64,64,6]{1,0,2:T(8,128)S(1)} %and_select_fusion, f32[3,16,6]{2,1,0:T(8,128)S(1)} %get-tuple-element.7, pred[64,64,6]{1,0,2:T(8,128)(4,1)S(1)} %broadcast_compare_fusion), kind=kLoop, calls=%fused_computation | loop fusion | flops 3342336 | bytes 911616 | tf_op jit(solution)/shard_map/reduce_prod | solution.py:75
  24.4 35.6 %all-to-all-done = bf16[64,2,3,16,128]{4,3,2,1,0:T(8,128)(2,1)S(1)} async-done(((bf16[64,2,3,16,128]{4,3,2,1,0:T(8,128)(2,1)}), bf16[64,2,3,16,128]{4,3,2,1,0:T(8,128)(2,1)S(1)}, u32[]{:S(2)}, u32[]{:S(2)}) %all-to-all-start) | async-done | bytes 1572896 | tf_op jit(solution)/shard_map/all_to_all | solution.py:15
  60.2 1.0 fusion.25
  61.2 2.7 %fusion.7 = bf16[64,3,16,128]{3,0,2,1:T(8,128)(2,1)S(1)} fusion(f32[3,16,64,64]{3,2,1,0:T(8,128)S(1)} %select_reduce_fusion, f32[3,16,128,64]{2,3,1,0:T(8,128)S(1)} %fusion.25, bf16[64,1,3,16,128]{4,3,2,1,0:T(8,128)(2,1)S(1)} %get-tuple-element.5), kind=kOutput, calls=%fused_computation.15 | convolution fusion | flops 303169536 | bytes 3932160 | tf_op jit(solution)/shard_map/kied,ekic->dkic/dot_general | solution.py:79
  64.0 1.4 %copy.90 = bf16[64,3,16,128]{3,2,1,0:T(8,128)(2,1)} copy(bf16[64,3,16,128]{3,0,2,1:T(8,128)(2,1)S(1)} %fusion.7) | data formatting | bytes 1572864 | tf_op jit(solution)/shard_map/convert_element_type | solution.py:80
  65.4 8.9 %all-to-all-start.1 = ((bf16[64,3,16,128]{3,2,1,0:T(8,128)(2,1)}), bf16[64,3,16,128]{3,2,1,0:T(8,128)(2,1)S(1)}, u32[]{:S(2)}, u32[]{:S(2)}) async-start(bf16[64,3,16,128]{3,2,1,0:T(8,128)(2,1)} %copy.90), calls=%async_computation.1 | async-start | bytes 1572864 | tf_op jit(solution)/shard_map/all_to_all | solution.py:21
  74.6 20.9 %all-to-all-done.1 = bf16[64,3,16,128]{3,2,1,0:T(8,128)(2,1)S(1)} async-done(((bf16[64,3,16,128]{3,2,1,0:T(8,128)(2,1)}), bf16[64,3,16,128]{3,2,1,0:T(8,128)(2,1)S(1)}, u32[]{:S(2)}, u32[]{:S(2)}) %all-to-all-start.1) | async-done | bytes 786464 | tf_op jit(solution)/shard_map/all_to_all | solution.py:21
  98.3 1.9 %fusion.23 = f32[384,512]{1,0:T(8,128)S(1)} fusion(bf16[384,1024]{1,0:T(8,128)(2,1)S(1)} %fusion, bf16[1024,4096]{1,0:T(8,128)(2,1)} %param.19), kind=kOutput, calls=%fused_computation.31 | convolution fusion | flops 402653184 | bytes 2621440 | tf_op jit(solution)/shard_map/dot_general | solution.py:113
  100.2 1.9 %fusion.21 = f32[384,512]{1,0:T(8,128)S(1)} fusion(bf16[384,1024]{1,0:T(8,128)(2,1)S(1)} %fusion, bf16[1024,4096]{1,0:T(8,128)(2,1)} %param.19), kind=kOutput, calls=%fused_computation.29 | convolution fusion | flops 402653184 | bytes 2621440 | tf_op jit(solution)/shard_map/dot_general | solution.py:113
  102.2 1.8 %fusion.19 = f32[384,512]{1,0:T(8,128)S(1)} fusion(bf16[384,1024]{1,0:T(8,128)(2,1)S(1)} %fusion, bf16[1024,4096]{1,0:T(8,128)(2,1)} %param.19), kind=kOutput, calls=%fused_computation.27 | convolution fusion | flops 402653184 | bytes 2621440 | tf_op jit(solution)/shard_map/dot_general | solution.py:113
  103.9 1.8 %fusion.17 = f32[384,512]{1,0:T(8,128)S(1)} fusion(bf16[384,1024]{1,0:T(8,128)(2,1)S(1)} %fusion, bf16[1024,4096]{1,0:T(8,128)(2,1)} %param.19), kind=kOutput, calls=%fused_computation.25 | convolution fusion | flops 402653184 | bytes 2621440 | tf_op jit(solution)/shard_map/dot_general | solution.py:113
  108.1 4.6 %collective-permute-start = (bf16[2,96,512]{2,1,0:T(8,128)(2,1)S(1)}, bf16[2,96,512]{2,1,0:T(8,128)(2,1)S(1)}, u32[]{:S(2)}, u32[]{:S(2)}) collective-permute-start(bf16[2,96,512]{2,1,0:T(8,128)(2,1)S(1)} %fusion.28), channel_id=1, source_target_pairs={{0,1},{1,0},{2,3},{3,2},{4,5},{5,4},{6,7},{7,6},{8,9},{9,8},{10,11... | collective-permute-start | bytes 589832 | tf_op jit(solution)/shard_map/ppermute | solution.py:93
  115.7 1.2 collective-permute-start.3
  117.5 1.4 %collective-permute-start.7 = (bf16[96,512]{1,0:T(8,128)(2,1)S(1)}, bf16[96,512]{1,0:T(8,128)(2,1)S(1)}, u32[]{:S(2)}, u32[]{:S(2)}) collective-permute-start(bf16[96,512]{1,0:T(8,128)(2,1)S(1)} %fusion.48), channel_id=1, source_target_pairs={{0,2},{1,3},{2,0},{3,1},{4,6},{5,7},{6,4},{7,5},{8,10},{9,11},{10,... | collective-permute-start | bytes 294920 | tf_op jit(solution)/shard_map/ppermute | solution.py:93
  119.4 1.2 collective-permute-start.11
  121.8 1.6 %collective-permute-done.5 = bf16[96,512]{1,0:T(8,128)(2,1)S(1)} collective-permute-done((bf16[96,512]{1,0:T(8,128)(2,1)S(1)}, bf16[96,512]{1,0:T(8,128)(2,1)S(1)}, u32[]{:S(2)}, u32[]{:S(2)}) %collective-permute-start.5) | collective-permute-done | bytes 98336 | tf_op jit(solution)/shard_map/ppermute | solution.py:93
  123.9 1.6 %collective-permute-done.7 = bf16[96,512]{1,0:T(8,128)(2,1)S(1)} collective-permute-done((bf16[96,512]{1,0:T(8,128)(2,1)S(1)}, bf16[96,512]{1,0:T(8,128)(2,1)S(1)}, u32[]{:S(2)}, u32[]{:S(2)}) %collective-permute-start.7) | collective-permute-done | bytes 98336 | tf_op jit(solution)/shard_map/ppermute | solution.py:93
  125.5 2.1 %collective-permute-done.9 = bf16[96,512]{1,0:T(8,128)(2,1)S(1)} collective-permute-done((bf16[96,512]{1,0:T(8,128)(2,1)S(1)}, bf16[96,512]{1,0:T(8,128)(2,1)S(1)}, u32[]{:S(2)}, u32[]{:S(2)}) %collective-permute-start.9) | collective-permute-done | bytes 98336 | tf_op jit(solution)/shard_map/ppermute | solution.py:93
  127.7 2.1 %collective-permute-done.11 = bf16[96,512]{1,0:T(8,128)(2,1)S(1)} collective-permute-done((bf16[96,512]{1,0:T(8,128)(2,1)S(1)}, bf16[96,512]{1,0:T(8,128)(2,1)S(1)}, u32[]{:S(2)}, u32[]{:S(2)}) %collective-permute-start.11) | collective-permute-done | bytes 98336 | tf_op jit(solution)/shard_map/ppermute | solution.py:93
  129.8 2.1 %collective-permute-done.13 = bf16[96,512]{1,0:T(8,128)(2,1)S(1)} collective-permute-done((bf16[96,512]{1,0:T(8,128)(2,1)S(1)}, bf16[96,512]{1,0:T(8,128)(2,1)S(1)}, u32[]{:S(2)}, u32[]{:S(2)}) %collective-permute-start.13) | collective-permute-done | bytes 98336 | tf_op jit(solution)/shard_map/ppermute | solution.py:93
  131.9 2.1 %collective-permute-done.15 = bf16[96,512]{1,0:T(8,128)(2,1)S(1)} collective-permute-done((bf16[96,512]{1,0:T(8,128)(2,1)S(1)}, bf16[96,512]{1,0:T(8,128)(2,1)S(1)}, u32[]{:S(2)}, u32[]{:S(2)}) %collective-permute-start.15) | collective-permute-done | bytes 98336 | tf_op jit(solution)/shard_map/ppermute | solution.py:93
  (95 shorter events, 16.4 us)
Async XLA Ops:
  0.0 2.0 %copy-start = (bf16[3,128,128]{2,1,0:T(8,128)(2,1)S(1)}, bf16[3,128,128]{2,1,0:T(8,128)(2,1)}, u32[]{:S(2)}) copy-start(bf16[3,128,128]{2,1,0:T(8,128)(2,1)} %param.14) | copy-start | bytes 294916
  6.7 15.3 %copy-start.6 = (f32[6,384]{1,0:T(8,128)S(1)}, f32[6,384]{1,0:T(8,128)}, u32[]{:S(2)}) copy-start(f32[6,384]{1,0:T(8,128)} %param.18) | copy-start | bytes 27652
  6.7 53.2 %all-to-all-start = ((bf16[64,2,3,16,128]{4,3,2,1,0:T(8,128)(2,1)}), bf16[64,2,3,16,128]{4,3,2,1,0:T(8,128)(2,1)S(1)}, u32[]{:S(2)}, u32[]{:S(2)}) async-start(bf16[64,2,3,16,128]{4,3,2,1,0:T(8,128)(2,1)} %bitcast.4), calls=%async_computation | async-start | bytes 3145728 | tf_op jit(solution)/shard_map/all_to_all | solution.py:15
  64.0 10.4 %copy-start.8 = (bf16[128,3,3]{0,2,1:T(4,128)(2,1)S(1)}, bf16[128,3,3]{0,2,1:T(4,128)(2,1)}, u32[]{:S(2)}) copy-start(bf16[128,3,3]{0,2,1:T(4,128)(2,1)} %param.17) | copy-start | bytes 6916
  65.4 30.1 %all-to-all-start.1 = ((bf16[64,3,16,128]{3,2,1,0:T(8,128)(2,1)}), bf16[64,3,16,128]{3,2,1,0:T(8,128)(2,1)S(1)}, u32[]{:S(2)}, u32[]{:S(2)}) async-start(bf16[64,3,16,128]{3,2,1,0:T(8,128)(2,1)} %copy.90), calls=%async_computation.1 | async-start | bytes 1572864 | tf_op jit(solution)/shard_map/all_to_all | solution.py:21
  96.9 8.8 %slice-start = ((s8[8388608]{0:T(1024)(128)(4,1)}), s8[4194304]{0:T(1024)(128)(4,1)S(1)}, s32[]{:S(2)}) async-start(s8[8388608]{0:T(1024)(128)(4,1)} %bitcast.252), calls=%async_computation.2 | async-start | bytes 8388608
  100.2 5.6 %slice-start.1 = ((s8[8388608]{0:T(1024)(128)(4,1)}), s8[4194304]{0:T(1024)(128)(4,1)S(1)}, s32[]{:S(2)}) async-start(s8[8388608]{0:T(1024)(128)(4,1)} %bitcast.252), calls=%async_computation.3 | async-start | bytes 8388608
  108.1 6.2 %collective-permute-start = (bf16[2,96,512]{2,1,0:T(8,128)(2,1)S(1)}, bf16[2,96,512]{2,1,0:T(8,128)(2,1)S(1)}, u32[]{:S(2)}, u32[]{:S(2)}) collective-permute-start(bf16[2,96,512]{2,1,0:T(8,128)(2,1)S(1)} %fusion.28), channel_id=1, source_target_pairs={{0,1},{1,0},{2,3},{3,2},{4,5},{5,4},{6,7},{7,6},{8,9},{9,8},{10,11... | collective-permute-start | bytes 589832 | tf_op jit(solution)/shard_map/ppermute | solution.py:93
  112.7 1.7 %collective-permute-start.2 = (bf16[2,96,512]{2,1,0:T(8,128)(2,1)S(1)}, bf16[2,96,512]{2,1,0:T(8,128)(2,1)S(1)}, u32[]{:S(2)}, u32[]{:S(2)}) collective-permute-start(bf16[2,96,512]{2,1,0:T(8,128)(2,1)S(1)} %fusion.29), channel_id=1, source_target_pairs={{0,1},{1,0},{2,3},{3,2},{4,5},{5,4},{6,7},{7,6},{8,9},{9,8},{10,11... | collective-permute-start | bytes 589832 | tf_op jit(solution)/shard_map/ppermute | solution.py:93
  112.9 2.2 %collective-permute-start.4 = (bf16[2,96,512]{2,1,0:T(8,128)(2,1)S(1)}, bf16[2,96,512]{2,1,0:T(8,128)(2,1)S(1)}, u32[]{:S(2)}, u32[]{:S(2)}) collective-permute-start(bf16[2,96,512]{2,1,0:T(8,128)(2,1)S(1)} %fusion.30), channel_id=1, source_target_pairs={{0,1},{1,0},{2,3},{3,2},{4,5},{5,4},{6,7},{7,6},{8,9},{9,8},{10,11... | collective-permute-start | bytes 589832 | tf_op jit(solution)/shard_map/ppermute | solution.py:93
  113.5 1.7 %collective-permute-start.6 = (bf16[2,96,512]{2,1,0:T(8,128)(2,1)S(1)}, bf16[2,96,512]{2,1,0:T(8,128)(2,1)S(1)}, u32[]{:S(2)}, u32[]{:S(2)}) collective-permute-start(bf16[2,96,512]{2,1,0:T(8,128)(2,1)S(1)} %fusion.31), channel_id=1, source_target_pairs={{0,1},{1,0},{2,3},{3,2},{4,5},{5,4},{6,7},{7,6},{8,9},{9,8},{10,11... | collective-permute-start | bytes 589832 | tf_op jit(solution)/shard_map/ppermute | solution.py:93
  113.6 2.1 %collective-permute-start.8 = (bf16[2,96,512]{2,1,0:T(8,128)(2,1)S(1)}, bf16[2,96,512]{2,1,0:T(8,128)(2,1)S(1)}, u32[]{:S(2)}, u32[]{:S(2)}) collective-permute-start(bf16[2,96,512]{2,1,0:T(8,128)(2,1)S(1)} %fusion.32), channel_id=1, source_target_pairs={{0,1},{1,0},{2,3},{3,2},{4,5},{5,4},{6,7},{7,6},{8,9},{9,8},{10,11... | collective-permute-start | bytes 589832 | tf_op jit(solution)/shard_map/ppermute | solution.py:93
  114.3 2.6 %collective-permute-start.10 = (bf16[2,96,512]{2,1,0:T(8,128)(2,1)S(1)}, bf16[2,96,512]{2,1,0:T(8,128)(2,1)S(1)}, u32[]{:S(2)}, u32[]{:S(2)}) collective-permute-start(bf16[2,96,512]{2,1,0:T(8,128)(2,1)S(1)} %fusion.33), channel_id=1, source_target_pairs={{0,1},{1,0},{2,3},{3,2},{4,5},{5,4},{6,7},{7,6},{8,9},{9,8},{10,11... | collective-permute-start | bytes 589832 | tf_op jit(solution)/shard_map/ppermute | solution.py:93
  114.5 3.0 %collective-permute-start.12 = (bf16[2,96,512]{2,1,0:T(8,128)(2,1)S(1)}, bf16[2,96,512]{2,1,0:T(8,128)(2,1)S(1)}, u32[]{:S(2)}, u32[]{:S(2)}) collective-permute-start(bf16[2,96,512]{2,1,0:T(8,128)(2,1)S(1)} %fusion.34), channel_id=1, source_target_pairs={{0,1},{1,0},{2,3},{3,2},{4,5},{5,4},{6,7},{7,6},{8,9},{9,8},{10,11... | collective-permute-start | bytes 589832 | tf_op jit(solution)/shard_map/ppermute | solution.py:93
  115.1 3.8 %collective-permute-start.14 = (bf16[2,96,512]{2,1,0:T(8,128)(2,1)S(1)}, bf16[2,96,512]{2,1,0:T(8,128)(2,1)S(1)}, u32[]{:S(2)}, u32[]{:S(2)}) collective-permute-start(bf16[2,96,512]{2,1,0:T(8,128)(2,1)S(1)} %fusion.35), channel_id=1, source_target_pairs={{0,1},{1,0},{2,3},{3,2},{4,5},{5,4},{6,7},{7,6},{8,9},{9,8},{10,11... | collective-permute-start | bytes 589832 | tf_op jit(solution)/shard_map/ppermute | solution.py:93
  115.2 4.2 %collective-permute-start.1 = (bf16[96,512]{1,0:T(8,128)(2,1)S(1)}, bf16[96,512]{1,0:T(8,128)(2,1)S(1)}, u32[]{:S(2)}, u32[]{:S(2)}) collective-permute-start(bf16[96,512]{1,0:T(8,128)(2,1)S(1)} %fusion.57), channel_id=1, source_target_pairs={{0,2},{1,3},{2,0},{3,1},{4,6},{5,7},{6,4},{7,5},{8,10},{9,11},{10,... | collective-permute-start | bytes 294920 | tf_op jit(solution)/shard_map/ppermute | solution.py:93
  115.7 5.5 %collective-permute-start.3 = (bf16[96,512]{1,0:T(8,128)(2,1)S(1)}, bf16[96,512]{1,0:T(8,128)(2,1)S(1)}, u32[]{:S(2)}, u32[]{:S(2)}) collective-permute-start(bf16[96,512]{1,0:T(8,128)(2,1)S(1)} %fusion.54), channel_id=1, source_target_pairs={{0,2},{1,3},{2,0},{3,1},{4,6},{5,7},{6,4},{7,5},{8,10},{9,11},{10,... | collective-permute-start | bytes 294920 | tf_op jit(solution)/shard_map/ppermute | solution.py:93
  116.9 6.5 %collective-permute-start.5 = (bf16[96,512]{1,0:T(8,128)(2,1)S(1)}, bf16[96,512]{1,0:T(8,128)(2,1)S(1)}, u32[]{:S(2)}, u32[]{:S(2)}) collective-permute-start(bf16[96,512]{1,0:T(8,128)(2,1)S(1)} %fusion.51), channel_id=1, source_target_pairs={{0,2},{1,3},{2,0},{3,1},{4,6},{5,7},{6,4},{7,5},{8,10},{9,11},{10,... | collective-permute-start | bytes 294920 | tf_op jit(solution)/shard_map/ppermute | solution.py:93
  117.5 8.0 %collective-permute-start.7 = (bf16[96,512]{1,0:T(8,128)(2,1)S(1)}, bf16[96,512]{1,0:T(8,128)(2,1)S(1)}, u32[]{:S(2)}, u32[]{:S(2)}) collective-permute-start(bf16[96,512]{1,0:T(8,128)(2,1)S(1)} %fusion.48), channel_id=1, source_target_pairs={{0,2},{1,3},{2,0},{3,1},{4,6},{5,7},{6,4},{7,5},{8,10},{9,11},{10,... | collective-permute-start | bytes 294920 | tf_op jit(solution)/shard_map/ppermute | solution.py:93
  118.9 8.7 %collective-permute-start.9 = (bf16[96,512]{1,0:T(8,128)(2,1)S(1)}, bf16[96,512]{1,0:T(8,128)(2,1)S(1)}, u32[]{:S(2)}, u32[]{:S(2)}) collective-permute-start(bf16[96,512]{1,0:T(8,128)(2,1)S(1)} %fusion.45), channel_id=1, source_target_pairs={{0,2},{1,3},{2,0},{3,1},{4,6},{5,7},{6,4},{7,5},{8,10},{9,11},{10,... | collective-permute-start | bytes 294920 | tf_op jit(solution)/shard_map/ppermute | solution.py:93
  119.4 10.3 %collective-permute-start.11 = (bf16[96,512]{1,0:T(8,128)(2,1)S(1)}, bf16[96,512]{1,0:T(8,128)(2,1)S(1)}, u32[]{:S(2)}, u32[]{:S(2)}) collective-permute-start(bf16[96,512]{1,0:T(8,128)(2,1)S(1)} %fusion.42), channel_id=1, source_target_pairs={{0,2},{1,3},{2,0},{3,1},{4,6},{5,7},{6,4},{7,5},{8,10},{9,11},{10,... | collective-permute-start | bytes 294920 | tf_op jit(solution)/shard_map/ppermute | solution.py:93
  121.3 10.5 %collective-permute-start.13 = (bf16[96,512]{1,0:T(8,128)(2,1)S(1)}, bf16[96,512]{1,0:T(8,128)(2,1)S(1)}, u32[]{:S(2)}, u32[]{:S(2)}) collective-permute-start(bf16[96,512]{1,0:T(8,128)(2,1)S(1)} %fusion.39), channel_id=1, source_target_pairs={{0,2},{1,3},{2,0},{3,1},{4,6},{5,7},{6,4},{7,5},{8,10},{9,11},{10,... | collective-permute-start | bytes 294920 | tf_op jit(solution)/shard_map/ppermute | solution.py:93
  123.4 10.5 %collective-permute-start.15 = (bf16[96,512]{1,0:T(8,128)(2,1)S(1)}, bf16[96,512]{1,0:T(8,128)(2,1)S(1)}, u32[]{:S(2)}, u32[]{:S(2)}) collective-permute-start(bf16[96,512]{1,0:T(8,128)(2,1)S(1)} %fusion.36), channel_id=1, source_target_pairs={{0,2},{1,3},{2,0},{3,1},{4,6},{5,7},{6,4},{7,5},{8,10},{9,11},{10,... | collective-permute-start | bytes 294920 | tf_op jit(solution)/shard_map/ppermute | solution.py:93
  131.9 2.1 %copy-start.5 = (bf16[96,4096]{1,0:T(8,128)(2,1)}, bf16[96,4096]{1,0:T(8,128)(2,1)S(1)}, u32[]{:S(2)}) copy-start(bf16[96,4096]{1,0:T(8,128)(2,1)S(1)} %fusion.66) | copy-start | bytes 2359300
  (5 other events, 6.5 us)

commit v9 on v8

--- a/solution.py
+++ b/solution.py
@@ -1,18 +1,55 @@
 import jax
 import jax.numpy as jnp
 from jax import lax
+from jax.experimental import pallas as pl
+from jax.experimental.pallas import tpu as pltpu
 from jax.sharding import PartitionSpec as P
 
 
 ROW_SPLIT = 8
 
 
-def to_columns(values, count):
-    n, nb, blk, chans = values.shape
+def prelude_kernel(gin_ref, vin_ref, filt_ref, blocks_ref, mix_ref, out_ref):
+    nb, blk = blocks_ref.shape[0], blocks_ref.shape[1]
+    count, rows, lanes = out_ref.shape[0], out_ref.shape[3], out_ref.shape[4]
+    cs = count // (blk // rows)
+    inner = []
+    for k in range(nb):
+        part = slice(k * blk, (k + 1) * blk)
+        mixed = gin_ref[part, :].astype(jnp.float32) * vin_ref[part, :].astype(jnp.float32)
+        inner.append(
+            jnp.dot(blocks_ref[k], mixed.astype(jnp.bfloat16), preferred_element_type=jnp.float32)
+            .astype(jnp.bfloat16)
+            .astype(jnp.float32)
+        )
+    for k in range(nb):
+        acc = mix_ref[:, k * nb : k * nb + 1] * inner[0]
+        for l in range(1, nb):
+            acc = acc + mix_ref[:, k * nb + l : k * nb + l + 1] * inner[l]
+        spec = acc.astype(jnp.bfloat16)
+        for a in range(blk // rows):
+            for b in range(cs):
+                cols = slice(b * lanes, (b + 1) * lanes)
+                out_ref[a * cs + b, 0, k] = spec[a * rows : (a + 1) * rows, cols]
+                out_ref[a * cs + b, 1, k] = filt_ref[k * blk + a * rows : k * blk + (a + 1) * rows, cols]
+
+
+def prelude(gate_in, value_in, spectral_filter, blocks, mix, count):
+    tokens, chans = gate_in.shape
+    nb, blk = blocks.shape[0], blocks.shape[1]
     cs = count // ROW_SPLIT
-    parts = values.reshape(n, nb, ROW_SPLIT, blk // ROW_SPLIT, cs, chans // cs)
-    parts = parts.transpose(2, 4, 0, 1, 3, 5).reshape(count, n, nb, blk // ROW_SPLIT, chans // cs)
-    return lax.all_to_all(parts, "seq", 0, 0, tiled=True)
+    vmem = pl.BlockSpec(memory_space=pltpu.VMEM)
+    return pl.pallas_call(
+        prelude_kernel,
+        out_shape=jax.ShapeDtypeStruct((count, 2, nb, blk // ROW_SPLIT, chans // cs), jnp.bfloat16),
+        in_specs=[vmem] * 5,
+        out_specs=vmem,
+        cost_estimate=pl.CostEstimate(
+            flops=2 * tokens * blk * chans + 6 * nb * tokens * chans,
+            bytes_accessed=2 * 5 * tokens * chans,
+            transcendentals=0,
+        ),
+    )(gate_in, value_in, spectral_filter, blocks, mix.astype(jnp.float32).reshape(blk, nb * nb))
 
 
 def from_columns(values, count, blk, chans):
@@ -41,20 +78,8 @@
     count = lax.axis_size("seq")
     sections = count.bit_length() - 1
     rank = lax.axis_index("seq")
-    mixed = (
-        (gate_in.astype(jnp.float32) * value_in.astype(jnp.float32))
-        .astype(jnp.bfloat16)
-        .reshape(nblocks, blk, chans)
-    )
-    inner = jnp.einsum(
-        "kij,kjc->kic", analysis_blocks, mixed, preferred_element_type=jnp.float32
-    ).astype(jnp.bfloat16)
-    spec = jnp.einsum(
-        "ikl,lic->kic", analysis_mix, inner, preferred_element_type=jnp.float32
-    ).astype(jnp.bfloat16)
-
-    both = jnp.stack([spec, spectral_filter.reshape(nblocks, blk, chans)])
-    both_cols = to_columns(both, count)
+    parts = prelude(gate_in, value_in, spectral_filter, analysis_blocks, analysis_mix, count)
+    both_cols = lax.all_to_all(parts, "seq", 0, 0, tiled=True)
     spec_cols = both_cols[:, 0]
     filt_cols = both_cols[:, 1]
     rows = blk // ROW_SPLIT
@@ -93,10 +118,7 @@
     return lax.ppermute(value, "chan", pairs)
 
 
-BLOCKS = 8
-
-
-def scatter_sum(gated, out_weight, blocks=BLOCKS):
+def scatter_sum(gated, out_weight, blocks=4):
     me = lax.axis_index("chan")
     core = me % 2
     chip = me // 2

time: 135 us -> 136 us (level)
  other arithmetic: 4.1 us -> 12.5 us
  starting transfers between devices: 36.9 us -> 32.5 us
  Pallas kernels: 0 us -> 3.56 us
  waiting for transfers between devices: 68.7 us -> 65.6 us
  matrix products: 16 us -> 13.4 us
    ppermute x16 -> x8, starting transfers between devices: 12.7 us -> 8.28 us  [exchange(): return lax.ppermute(value, 'chan', pairs)]
    convert_element_type x1 -> x4, other arithmetic: 0.3 us -> 4.23 us  [scatter_block(): return (mine + quarter.astype(jnp.float32)).astype(jnp.bfloat16)]
    convert_element_type x8 -> x4, other arithmetic: 0.21 us -> 4.1 us  [scatter_block(): quarter = exchange(other.astype(jnp.bfloat16), 2)]
    pallas_call x0 -> x1, Pallas kernels: none -> 3.56 us  [prelude(): pl.pallas_call(prelude_kernel, out_shape=jax.ShapeDtypeStruct((count, 2,...]
    ppermute x16 -> x8, waiting for transfers between devices: 12.2 us -> 9.13 us  [exchange(): return lax.ppermute(value, 'chan', pairs)]
    convert_element_type x8 -> x4, local copies, waits for them, and re-layouts: 0.22 us -> 3.23 us  [scatter_block(): half = exchange(sent.astype(jnp.bfloat16), 1)]
    unnamed x26 -> x18, local copies, waits for them, and re-layouts: 2.66 us -> 0.77 us
    dot_general x8 -> x4, matrix products: 9.65 us -> 7.91 us  [scatter_block(): product = jnp.dot(gated, weight, preferred_element_type=jnp.float32)]
  transfers between devices with their start and end apart: 18 -> 10, of which waited for: 9 -> 5; matrix products, arithmetic and copies ran while one was open for 2% -> 9% of each run, Pallas kernels for 0% -> 0%
where the time goes in v9:
time: 136 us
  waiting for transfers between devices  65.6 us (48%)
  starting transfers between devices  32.5 us (24%)
  matrix products  13.4 us (10%)
  other arithmetic  12.5 us (9%)
  local copies, waits for them, and re-layouts  7.69 us (6%)
  Pallas kernels  3.56 us (3%)
    all_to_all x1, waiting for transfers between devices, per_device(): both_cols = lax.all_to_all(parts, 'seq', 0, 0, tiled=True)  35.5 us
    all_to_all x1, waiting for transfers between devices, from_columns(): back = lax.all_to_all(values, 'seq', 0, 0, tiled=True)  20.9 us
    all_to_all x1, starting transfers between devices, per_device(): both_cols = lax.all_to_all(parts, 'seq', 0, 0, tiled=True)  15.2 us
    ppermute x8, waiting for transfers between devices, exchange(): return lax.ppermute(value, 'chan', pairs)  9.13 us
    all_to_all x1, starting transfers between devices, from_columns(): back = lax.all_to_all(values, 'seq', 0, 0, tiled=True)  8.97 us
    ppermute x8, starting transfers between devices, exchange(): return lax.ppermute(value, 'chan', pairs)  8.28 us
    dot_general x4, matrix products, scatter_block(): product = jnp.dot(gated, weight, preferred_element_type=jnp.float32)  7.91 us
    convert_element_type x4, other arithmetic, scatter_block(): return (mine + quarter.astype(jnp.float32)).astype(jnp.bfloat16)  4.23 us
  transfers between devices with their start and end apart: 10, of which 5 were waited for; matrix products, arithmetic and copies ran while one was open for 9% of the time, Pallas kernels for 0%

profile of v9, /device:TPU:1, one launch (start us, length us, event | category | flops | bytes accessed | tf_op | source)
XLA Modules:
  0.0 135.6 jit_solution(15580098373207248005)
XLA Ops:
  1.5 3.6 %shard_map.100 = bf16[64,2,3,16,128]{4,3,2,1,0:T(8,128)(2,1)} custom-call(bf16[384,1024]{1,0:T(8,128)(2,1)} %gin_ref.1, bf16[384,1024]{1,0:T(8,128)(2,1)} %vin_ref.1, bf16[384,1024]{1,0:T(8,128)(2,1)} %filt_ref.1, bf16[3,128,128]{2,1,0:T(8,128)(2,1)} %blocks_ref.1, f32[128,9]{1,0:T(8,128)} %copy.44.mix_ref), custom_call_target="tpu_custom_call" | custom-call | flops 107741184 | bytes 3932160 | tf_op jit(solution)/shard_map/pallas_call | solution.py:42
  5.0 15.2 %all-to-all-start = ((bf16[64,2,3,16,128]{4,3,2,1,0:T(8,128)(2,1)}), bf16[64,2,3,16,128]{4,3,2,1,0:T(8,128)(2,1)S(1)}, u32[]{:S(2)}, u32[]{:S(2)}) async-start(bf16[64,2,3,16,128]{4,3,2,1,0:T(8,128)(2,1)} %shard_map.100), calls=%async_computation | async-start | bytes 3145728 | tf_op jit(solution)/shard_map/all_to_all | solution.py:82
  20.9 1.8 %select_reduce_fusion = f32[3,16,64,64]{3,2,1,0:T(8,128)S(1)} fusion(f32[3,16,6]{2,1,0:T(8,128)S(1)} %get-tuple-element.6, f32[64,64,6]{1,0,2:T(8,128)S(1)} %and_select_fusion, f32[3,16,6]{2,1,0:T(8,128)S(1)} %get-tuple-element.5, pred[64,64,6]{1,0,2:T(8,128)(4,1)S(1)} %broadcast_compare_fusion), kind=kLoop, calls=%fused_computation | loop fusion | flops 3342336 | bytes 911616 | tf_op jit(solution)/shard_map/reduce_prod | solution.py:100
  22.7 35.5 %all-to-all-done = bf16[64,2,3,16,128]{4,3,2,1,0:T(8,128)(2,1)S(1)} async-done(((bf16[64,2,3,16,128]{4,3,2,1,0:T(8,128)(2,1)}), bf16[64,2,3,16,128]{4,3,2,1,0:T(8,128)(2,1)S(1)}, u32[]{:S(2)}, u32[]{:S(2)}) %all-to-all-start) | async-done | bytes 1572896 | tf_op jit(solution)/shard_map/all_to_all | solution.py:82
  58.3 1.0 fusion.21
  60.3 3.0 %fusion.15 = bf16[64,3,16,128]{3,0,2,1:T(8,128)(2,1)S(1)} fusion(f32[3,16,64,64]{3,2,1,0:T(8,128)S(1)} %select_reduce_fusion, f32[64,3,16,128]{3,2,1,0:T(8,128)S(1)} %convert_multiply_fusion), kind=kOutput, calls=%fused_computation.17 | convolution fusion | flops 302383104 | bytes 3145728 | tf_op jit(solution)/shard_map/kied,ekic->dkic/dot_general | solution.py:104
  63.3 1.4 %copy.50 = bf16[64,3,16,128]{3,2,1,0:T(8,128)(2,1)} copy(bf16[64,3,16,128]{3,0,2,1:T(8,128)(2,1)S(1)} %fusion.15) | data formatting | bytes 1572864 | tf_op jit(solution)/shard_map/convert_element_type | solution.py:105
  64.7 9.0 %all-to-all-start.1 = ((bf16[64,3,16,128]{3,2,1,0:T(8,128)(2,1)}), bf16[64,3,16,128]{3,2,1,0:T(8,128)(2,1)S(1)}, u32[]{:S(2)}, u32[]{:S(2)}) async-start(bf16[64,3,16,128]{3,2,1,0:T(8,128)(2,1)} %copy.50), calls=%async_computation.1 | async-start | bytes 1572864 | tf_op jit(solution)/shard_map/all_to_all | solution.py:58
  73.9 20.9 %all-to-all-done.1 = bf16[64,3,16,128]{3,2,1,0:T(8,128)(2,1)S(1)} async-done(((bf16[64,3,16,128]{3,2,1,0:T(8,128)(2,1)}), bf16[64,3,16,128]{3,2,1,0:T(8,128)(2,1)S(1)}, u32[]{:S(2)}, u32[]{:S(2)}) %all-to-all-start.1) | async-done | bytes 786464 | tf_op jit(solution)/shard_map/all_to_all | solution.py:58
  97.6 2.7 %fusion.6 = f32[384,1024]{1,0:T(8,128)S(1)} fusion(bf16[384,1024]{1,0:T(8,128)(2,1)S(1)} %fusion.8, bf16[1024,4096]{1,0:T(8,128)(2,1)} %param.19), kind=kOutput, calls=%fused_computation.7 | convolution fusion | flops 805306368 | bytes 4456448 | tf_op jit(solution)/shard_map/dot_general | solution.py:135
  100.4 3.2 %fusion.4 = f32[384,1024]{1,0:T(8,128)S(1)} fusion(bf16[384,1024]{1,0:T(8,128)(2,1)S(1)} %fusion.8, bf16[1024,4096]{1,0:T(8,128)(2,1)} %param.19), kind=kOutput, calls=%fused_computation.5 | convolution fusion | flops 805306368 | bytes 4456448 | tf_op jit(solution)/shard_map/dot_general | solution.py:135
  104.6 1.0 fusion
  106.4 4.5 %collective-permute-start = (bf16[2,96,1024]{2,1,0:T(8,128)(2,1)}, bf16[2,96,1024]{2,1,0:T(8,128)(2,1)}, u32[]{:S(2)}, u32[]{:S(2)}) collective-permute-start(bf16[2,96,1024]{2,1,0:T(8,128)(2,1)} %fusion.23), channel_id=1, source_target_pairs={{0,1},{1,0},{2,3},{3,2},{4,5},{5,4},{6,7},{7,6},{8,9},{9,8},{10,11... | collective-permute-start | bytes 1179656 | tf_op jit(solution)/shard_map/ppermute | solution.py:118
  113.9 1.1 fusion.36
  115.5 1.1 fusion.33
  116.5 1.2 collective-permute-start.3
  120.1 1.2 collective-permute-start.7
  121.3 1.1 fusion.38
  122.4 2.8 %collective-permute-done.3 = bf16[96,1024]{1,0:T(8,128)(2,1)S(1)} collective-permute-done((bf16[96,1024]{1,0:T(8,128)(2,1)S(1)}, bf16[96,1024]{1,0:T(8,128)(2,1)S(1)}, u32[]{:S(2)}, u32[]{:S(2)}) %collective-permute-start.3) | collective-permute-done | bytes 196640 | tf_op jit(solution)/shard_map/ppermute | solution.py:118
  125.2 1.1 fusion.35
  126.3 3.1 %collective-permute-done.5 = bf16[96,1024]{1,0:T(8,128)(2,1)S(1)} collective-permute-done((bf16[96,1024]{1,0:T(8,128)(2,1)S(1)}, bf16[96,1024]{1,0:T(8,128)(2,1)S(1)}, u32[]{:S(2)}, u32[]{:S(2)}) %collective-permute-start.5) | collective-permute-done | bytes 196640 | tf_op jit(solution)/shard_map/ppermute | solution.py:118
  129.4 1.0 fusion.32
  130.4 3.2 %collective-permute-done.7 = bf16[96,1024]{1,0:T(8,128)(2,1)S(1)} collective-permute-done((bf16[96,1024]{1,0:T(8,128)(2,1)S(1)}, bf16[96,1024]{1,0:T(8,128)(2,1)S(1)}, u32[]{:S(2)}, u32[]{:S(2)}) %collective-permute-start.7) | collective-permute-done | bytes 196640 | tf_op jit(solution)/shard_map/ppermute | solution.py:118
  133.6 1.0 fusion.29
  (53 shorter events, 14.6 us)
Async XLA Ops:
  0.0 96.2 %copy-start = (bf16[3,128,128]{2,1,0:T(8,128)(2,1)S(1)}, bf16[3,128,128]{2,1,0:T(8,128)(2,1)}, u32[]{:S(2)}) copy-start(bf16[3,128,128]{2,1,0:T(8,128)(2,1)} %param.16) | copy-start | bytes 294916
  5.0 15.3 %copy-start.4 = (f32[6,384]{1,0:T(8,128)S(1)}, f32[6,384]{1,0:T(8,128)}, u32[]{:S(2)}) copy-start(f32[6,384]{1,0:T(8,128)} %param.18) | copy-start | bytes 27652
  5.0 53.2 %all-to-all-start = ((bf16[64,2,3,16,128]{4,3,2,1,0:T(8,128)(2,1)}), bf16[64,2,3,16,128]{4,3,2,1,0:T(8,128)(2,1)S(1)}, u32[]{:S(2)}, u32[]{:S(2)}) async-start(bf16[64,2,3,16,128]{4,3,2,1,0:T(8,128)(2,1)} %shard_map.100), calls=%async_computation | async-start | bytes 3145728 | tf_op jit(solution)/shard_map/all_to_all | solution.py:82
  63.3 10.4 %copy-start.5 = (bf16[128,3,3]{0,2,1:T(4,128)(2,1)S(1)}, bf16[128,3,3]{0,2,1:T(4,128)(2,1)}, u32[]{:S(2)}) copy-start(bf16[128,3,3]{0,2,1:T(4,128)(2,1)} %param.17) | copy-start | bytes 6916
  64.7 30.1 %all-to-all-start.1 = ((bf16[64,3,16,128]{3,2,1,0:T(8,128)(2,1)}), bf16[64,3,16,128]{3,2,1,0:T(8,128)(2,1)S(1)}, u32[]{:S(2)}, u32[]{:S(2)}) async-start(bf16[64,3,16,128]{3,2,1,0:T(8,128)(2,1)} %copy.50), calls=%async_computation.1 | async-start | bytes 1572864 | tf_op jit(solution)/shard_map/all_to_all | solution.py:58
  96.2 1.1 copy-start.3
  97.4 6.2 %slice-start = ((s8[8388608]{0:T(1024)(128)(4,1)}), s8[4194304]{0:T(1024)(128)(4,1)S(1)}, s32[]{:S(2)}) async-start(s8[8388608]{0:T(1024)(128)(4,1)} %bitcast.125), calls=%async_computation.2 | async-start | bytes 8388608
  97.6 6.0 %slice-start.1 = ((s8[8388608]{0:T(1024)(128)(4,1)}), s8[4194304]{0:T(1024)(128)(4,1)S(1)}, s32[]{:S(2)}) async-start(s8[8388608]{0:T(1024)(128)(4,1)} %bitcast.125), calls=%async_computation.3 | async-start | bytes 8388608
  100.4 5.3 %copy-start.2 = (f32[384,1024]{1,0:T(8,128)}, f32[384,1024]{1,0:T(8,128)S(1)}, u32[]{:S(2)}) copy-start(f32[384,1024]{1,0:T(8,128)S(1)} %fusion.6) | copy-start | bytes 4718596
  103.6 7.3 %copy-start.1 = (f32[384,1024]{1,0:T(8,128)}, f32[384,1024]{1,0:T(8,128)S(1)}, u32[]{:S(2)}) copy-start(f32[384,1024]{1,0:T(8,128)S(1)} %fusion.4) | copy-start | bytes 4718596
  106.4 7.4 %collective-permute-start = (bf16[2,96,1024]{2,1,0:T(8,128)(2,1)}, bf16[2,96,1024]{2,1,0:T(8,128)(2,1)}, u32[]{:S(2)}, u32[]{:S(2)}) collective-permute-start(bf16[2,96,1024]{2,1,0:T(8,128)(2,1)} %fusion.23), channel_id=1, source_target_pairs={{0,1},{1,0},{2,3},{3,2},{4,5},{5,4},{6,7},{7,6},{8,9},{9,8},{10,11... | collective-permute-start | bytes 1179656 | tf_op jit(solution)/shard_map/ppermute | solution.py:118
  111.7 3.7 %collective-permute-start.2 = (bf16[2,96,1024]{2,1,0:T(8,128)(2,1)}, bf16[2,96,1024]{2,1,0:T(8,128)(2,1)}, u32[]{:S(2)}, u32[]{:S(2)}) collective-permute-start(bf16[2,96,1024]{2,1,0:T(8,128)(2,1)} %fusion.24), channel_id=1, source_target_pairs={{0,1},{1,0},{2,3},{3,2},{4,5},{5,4},{6,7},{7,6},{8,9},{9,8},{10,11... | collective-permute-start | bytes 1179656 | tf_op jit(solution)/shard_map/ppermute | solution.py:118
  112.6 5.1 %collective-permute-start.4 = (bf16[2,96,1024]{2,1,0:T(8,128)(2,1)}, bf16[2,96,1024]{2,1,0:T(8,128)(2,1)}, u32[]{:S(2)}, u32[]{:S(2)}) collective-permute-start(bf16[2,96,1024]{2,1,0:T(8,128)(2,1)} %fusion.25), channel_id=1, source_target_pairs={{0,1},{1,0},{2,3},{3,2},{4,5},{5,4},{6,7},{7,6},{8,9},{9,8},{10,11... | collective-permute-start | bytes 1179656 | tf_op jit(solution)/shard_map/ppermute | solution.py:118
  113.9 5.3 %collective-permute-start.6 = (bf16[2,96,1024]{2,1,0:T(8,128)(2,1)}, bf16[2,96,1024]{2,1,0:T(8,128)(2,1)}, u32[]{:S(2)}, u32[]{:S(2)}) collective-permute-start(bf16[2,96,1024]{2,1,0:T(8,128)(2,1)} %fusion.26), channel_id=1, source_target_pairs={{0,1},{1,0},{2,3},{3,2},{4,5},{5,4},{6,7},{7,6},{8,9},{9,8},{10,11... | collective-permute-start | bytes 1179656 | tf_op jit(solution)/shard_map/ppermute | solution.py:118
  115.0 6.3 %collective-permute-start.1 = (bf16[96,1024]{1,0:T(8,128)(2,1)S(1)}, bf16[96,1024]{1,0:T(8,128)(2,1)S(1)}, u32[]{:S(2)}, u32[]{:S(2)}) collective-permute-start(bf16[96,1024]{1,0:T(8,128)(2,1)S(1)} %fusion.36), channel_id=1, source_target_pairs={{0,2},{1,3},{2,0},{3,1},{4,6},{5,7},{6,4},{7,5},{8,10},{9,11},{10,... | collective-permute-start | bytes 589832 | tf_op jit(solution)/shard_map/ppermute | solution.py:118
  116.5 8.7 %collective-permute-start.3 = (bf16[96,1024]{1,0:T(8,128)(2,1)S(1)}, bf16[96,1024]{1,0:T(8,128)(2,1)S(1)}, u32[]{:S(2)}, u32[]{:S(2)}) collective-permute-start(bf16[96,1024]{1,0:T(8,128)(2,1)S(1)} %fusion.33), channel_id=1, source_target_pairs={{0,2},{1,3},{2,0},{3,1},{4,6},{5,7},{6,4},{7,5},{8,10},{9,11},{10,... | collective-permute-start | bytes 589832 | tf_op jit(solution)/shard_map/ppermute | solution.py:118
  118.7 10.8 %collective-permute-start.5 = (bf16[96,1024]{1,0:T(8,128)(2,1)S(1)}, bf16[96,1024]{1,0:T(8,128)(2,1)S(1)}, u32[]{:S(2)}, u32[]{:S(2)}) collective-permute-start(bf16[96,1024]{1,0:T(8,128)(2,1)S(1)} %fusion.30), channel_id=1, source_target_pairs={{0,2},{1,3},{2,0},{3,1},{4,6},{5,7},{6,4},{7,5},{8,10},{9,11},{10,... | collective-permute-start | bytes 589832 | tf_op jit(solution)/shard_map/ppermute | solution.py:118
  120.1 13.5 %collective-permute-start.7 = (bf16[96,1024]{1,0:T(8,128)(2,1)S(1)}, bf16[96,1024]{1,0:T(8,128)(2,1)S(1)}, u32[]{:S(2)}, u32[]{:S(2)}) collective-permute-start(bf16[96,1024]{1,0:T(8,128)(2,1)S(1)} %fusion.27), channel_id=1, source_target_pairs={{0,2},{1,3},{2,0},{3,1},{4,6},{5,7},{6,4},{7,5},{8,10},{9,11},{10,... | collective-permute-start | bytes 589832 | tf_op jit(solution)/shard_map/ppermute | solution.py:118

commit v10 on v9

--- a/solution.py
+++ b/solution.py
@@ -60,6 +60,15 @@
     return back.transpose(2, 0, 3, 1, 4).reshape(nb, blk, chans)
 
 
+def rotate_bit(values, cosine, sine, bit, sections, sign):
+    axis = sections - 1 - bit
+    lower = lax.index_in_dim(values, 0, axis, keepdims=True)
+    upper = lax.index_in_dim(values, 1, axis, keepdims=True)
+    new_lower = cosine * lower + sign * sine * upper
+    new_upper = cosine * upper - sign * sine * lower
+    return jnp.concatenate([new_lower, new_upper], axis=axis)
+
+
 def per_device(
     value_in,
     gate_in,
@@ -89,20 +98,14 @@
     cosines = jnp.cos(theta)[:, :, :, None]
     sines = jnp.sin(theta)[:, :, :, None]
 
-    bits = (jnp.arange(count)[:, None] >> jnp.arange(sections)[None, :]) & 1
-    same = bits[:, None, :] == bits[None, :, :]
-    below = (bits[:, None, :] == 0) & (bits[None, :, :] == 1)
-    factor = jnp.where(
-        same[None, None],
-        cosines[..., 0].transpose(1, 2, 0)[:, :, None, None, :],
-        jnp.where(below[None, None], 1.0, -1.0) * sines[..., 0].transpose(1, 2, 0)[:, :, None, None, :],
-    )
-    matrix = jnp.prod(factor, axis=-1)
-    hi = lax.Precision.HIGHEST
-    work = jnp.einsum("kide,ekic->dkic", matrix, spec_cols.astype(jnp.float32), precision=hi)
-    work = work * filt_cols.astype(jnp.float32)
-    work = jnp.einsum("kied,ekic->dkic", matrix, work, precision=hi)
-    work = work.astype(jnp.bfloat16)
+    shape = (2,) * sections + spec_cols.shape[1:]
+    work = spec_cols.astype(jnp.float32).reshape(shape)
+    for section in range(sections):
+        work = rotate_bit(work, cosines[section], sines[section], section, sections, 1.0)
+    work = work * filt_cols.astype(jnp.float32).reshape(shape)
+    for section in reversed(range(sections)):
+        work = rotate_bit(work, cosines[section], sines[section], section, sections, -1.0)
+    work = work.astype(jnp.bfloat16).reshape(spec_cols.shape)
 
     grid = from_columns(work, count, blk, chans)
     spread = jnp.einsum(

time: 136 us -> 135 us (level)
  matrix products: 13.4 us -> 9.26 us
  waiting for transfers between devices: 65.6 us -> 67.9 us
  other arithmetic: 12.5 us -> 14.5 us
  local copies, waits for them, and re-layouts: 7.69 us -> 6.3 us
    dot_general x2 -> x0, matrix products: 4.05 us -> none  [the longest x1 3.04 us: per_device(): work = jnp.einsum('kied,ekic->dkic', matrix, work, precision=hi)]
    add x0 -> x11, other arithmetic: none -> 3.31 us  [rotate_bit(): new_lower = cosine * lower + sign * sine * upper]
    all_to_all x1, waiting for transfers between devices: 35.5 us -> 37.6 us  [per_device(): both_cols = lax.all_to_all(parts, 'seq', 0, 0, tiled=True)]
    reduce_prod x1 -> x0, other arithmetic: 1.81 us -> none  [per_device(): matrix = jnp.prod(factor, axis=-1)]
    convert_element_type x1 -> x0, local copies, waits for them, and re-layouts: 1.39 us -> none  [per_device(): work = work.astype(jnp.bfloat16)]
  transfers between devices with their start and end apart: 10 -> 10, of which waited for: 5 -> 5; matrix products, arithmetic and copies ran while one was open for 9% -> 8% of each run, Pallas kernels for 0% -> 0%
where the time goes in v10:
time: 135 us; the launch traced here: 134 us
  waiting for transfers between devices  67.9 us (50%)
  starting transfers between devices  32.3 us (24%)
  other arithmetic  14.5 us (11%)
  matrix products  9.26 us (7%)
  local copies, waits for them, and re-layouts  6.3 us (5%)
  Pallas kernels  3.57 us (3%)
    all_to_all x1, waiting for transfers between devices, per_device(): both_cols = lax.all_to_all(parts, 'seq', 0, 0, tiled=True)  37.6 us
    all_to_all x1, waiting for transfers between devices, from_columns(): back = lax.all_to_all(values, 'seq', 0, 0, tiled=True)  21.1 us
    all_to_all x1, starting transfers between devices, per_device(): both_cols = lax.all_to_all(parts, 'seq', 0, 0, tiled=True)  15.2 us
    ppermute x8, waiting for transfers between devices, exchange(): return lax.ppermute(value, 'chan', pairs)  9.13 us
    all_to_all x1, starting transfers between devices, from_columns(): back = lax.all_to_all(values, 'seq', 0, 0, tiled=True)  8.79 us
    ppermute x8, starting transfers between devices, exchange(): return lax.ppermute(value, 'chan', pairs)  8.28 us
    dot_general x4, matrix products, scatter_block(): product = jnp.dot(gated, weight, preferred_element_type=jnp.float32)  7.91 us
    convert_element_type x4, other arithmetic, scatter_block(): return (mine + quarter.astype(jnp.float32)).astype(jnp.bfloat16)  4.23 us
  transfers between devices with their start and end apart: 10, of which 5 were waited for; matrix products, arithmetic and copies ran while one was open for 8% of the time, Pallas kernels for 0%

profile of v10, /device:TPU:1, one launch (start us, length us, event | category | flops | bytes accessed | tf_op | source)
XLA Modules:
  0.0 134.3 jit_solution(17416208964848775801)
XLA Ops:
  1.5 3.6 %shard_map.100 = bf16[64,2,3,16,128]{4,3,2,1,0:T(8,128)(2,1)} custom-call(bf16[384,1024]{1,0:T(8,128)(2,1)} %gin_ref.1, bf16[384,1024]{1,0:T(8,128)(2,1)} %vin_ref.1, bf16[384,1024]{1,0:T(8,128)(2,1)} %filt_ref.1, bf16[3,128,128]{2,1,0:T(8,128)(2,1)} %blocks_ref.1, f32[128,9]{1,0:T(8,128)} %copy.24.mix_ref), custom_call_target="tpu_custom_call" | custom-call | flops 107741184 | bytes 3932160 | tf_op jit(solution)/shard_map/pallas_call | solution.py:42
  5.0 15.2 %all-to-all-start = ((bf16[64,2,3,16,128]{4,3,2,1,0:T(8,128)(2,1)}), bf16[64,2,3,16,128]{4,3,2,1,0:T(8,128)(2,1)S(1)}, u32[]{:S(2)}, u32[]{:S(2)}) async-start(bf16[64,2,3,16,128]{4,3,2,1,0:T(8,128)(2,1)} %shard_map.100), calls=%async_computation | async-start | bytes 3145728 | tf_op jit(solution)/shard_map/all_to_all | solution.py:91
  20.6 37.6 %all-to-all-done = bf16[64,2,3,16,128]{4,3,2,1,0:T(8,128)(2,1)S(1)} async-done(((bf16[64,2,3,16,128]{4,3,2,1,0:T(8,128)(2,1)}), bf16[64,2,3,16,128]{4,3,2,1,0:T(8,128)(2,1)S(1)}, u32[]{:S(2)}, u32[]{:S(2)}) %all-to-all-start) | async-done | bytes 1572896 | tf_op jit(solution)/shard_map/all_to_all | solution.py:91
  62.7 0.9 pad_maximum_fusion.10
  63.6 8.8 %all-to-all-start.1 = ((bf16[64,3,16,128]{3,2,1,0:T(8,128)(2,1)}), bf16[64,3,16,128]{3,2,1,0:T(8,128)(2,1)S(1)}, u32[]{:S(2)}, u32[]{:S(2)}) async-start(bf16[64,3,16,128]{3,2,1,0:T(8,128)(2,1)} %bitcast.15), calls=%async_computation.1 | async-start | bytes 1572864 | tf_op jit(solution)/shard_map/all_to_all | solution.py:58
  72.6 21.1 %all-to-all-done.1 = bf16[64,3,16,128]{3,2,1,0:T(8,128)(2,1)S(1)} async-done(((bf16[64,3,16,128]{3,2,1,0:T(8,128)(2,1)}), bf16[64,3,16,128]{3,2,1,0:T(8,128)(2,1)S(1)}, u32[]{:S(2)}, u32[]{:S(2)}) %all-to-all-start.1) | async-done | bytes 786464 | tf_op jit(solution)/shard_map/all_to_all | solution.py:58
  96.3 2.7 %fusion = f32[384,1024]{1,0:T(8,128)S(1)} fusion(bf16[384,1024]{1,0:T(8,128)(2,1)S(1)} %fusion.8, bf16[1024,4096]{1,0:T(8,128)(2,1)} %param.19), kind=kOutput, calls=%fused_computation | convolution fusion | flops 805306368 | bytes 4456448 | tf_op jit(solution)/shard_map/dot_general | solution.py:138
  99.1 3.2 %fusion.2 = f32[384,1024]{1,0:T(8,128)S(1)} fusion(bf16[384,1024]{1,0:T(8,128)(2,1)S(1)} %fusion.8, bf16[1024,4096]{1,0:T(8,128)(2,1)} %param.19), kind=kOutput, calls=%fused_computation.2 | convolution fusion | flops 805306368 | bytes 4456448 | tf_op jit(solution)/shard_map/dot_general | solution.py:138
  102.4 1.0 fusion.4
  103.4 1.0 fusion.6
  105.2 4.5 %collective-permute-start.6 = (bf16[2,96,1024]{2,1,0:T(8,128)(2,1)}, bf16[2,96,1024]{2,1,0:T(8,128)(2,1)}, u32[]{:S(2)}, u32[]{:S(2)}) collective-permute-start(bf16[2,96,1024]{2,1,0:T(8,128)(2,1)} %fusion.25), channel_id=1, source_target_pairs={{0,1},{1,0},{2,3},{3,2},{4,5},{5,4},{6,7},{7,6},{8,9},{9,8},{10,11... | collective-permute-start | bytes 1179656 | tf_op jit(solution)/shard_map/ppermute | solution.py:121
  112.6 1.1 fusion.26
  114.2 1.1 fusion.29
  115.2 1.2 collective-permute-start.5
  116.4 1.0 fusion.32
  117.9 1.0 fusion.35
  118.8 1.2 collective-permute-start.1
  120.0 1.1 fusion.28
  121.1 2.8 %collective-permute-done.5 = bf16[96,1024]{1,0:T(8,128)(2,1)S(1)} collective-permute-done((bf16[96,1024]{1,0:T(8,128)(2,1)S(1)}, bf16[96,1024]{1,0:T(8,128)(2,1)S(1)}, u32[]{:S(2)}, u32[]{:S(2)}) %collective-permute-start.5) | collective-permute-done | bytes 196640 | tf_op jit(solution)/shard_map/ppermute | solution.py:121
  123.9 1.1 fusion.31
  125.0 3.1 %collective-permute-done.3 = bf16[96,1024]{1,0:T(8,128)(2,1)S(1)} collective-permute-done((bf16[96,1024]{1,0:T(8,128)(2,1)S(1)}, bf16[96,1024]{1,0:T(8,128)(2,1)S(1)}, u32[]{:S(2)}, u32[]{:S(2)}) %collective-permute-start.3) | collective-permute-done | bytes 196640 | tf_op jit(solution)/shard_map/ppermute | solution.py:121
  128.1 1.0 fusion.34
  129.1 3.2 %collective-permute-done.1 = bf16[96,1024]{1,0:T(8,128)(2,1)S(1)} collective-permute-done((bf16[96,1024]{1,0:T(8,128)(2,1)S(1)}, bf16[96,1024]{1,0:T(8,128)(2,1)S(1)}, u32[]{:S(2)}, u32[]{:S(2)}) %collective-permute-start.1) | collective-permute-done | bytes 196640 | tf_op jit(solution)/shard_map/ppermute | solution.py:121
  132.3 1.0 fusion.37
  (60 shorter events, 14.4 us)
Async XLA Ops:
  0.0 94.9 %copy-start = (bf16[3,128,128]{2,1,0:T(8,128)(2,1)S(1)}, bf16[3,128,128]{2,1,0:T(8,128)(2,1)}, u32[]{:S(2)}) copy-start(bf16[3,128,128]{2,1,0:T(8,128)(2,1)} %param.16) | copy-start | bytes 294916
  5.0 15.3 %copy-start.4 = (f32[6,384]{1,0:T(8,128)S(1)}, f32[6,384]{1,0:T(8,128)}, u32[]{:S(2)}) copy-start(f32[6,384]{1,0:T(8,128)} %param.18) | copy-start | bytes 27652
  5.0 53.2 %all-to-all-start = ((bf16[64,2,3,16,128]{4,3,2,1,0:T(8,128)(2,1)}), bf16[64,2,3,16,128]{4,3,2,1,0:T(8,128)(2,1)S(1)}, u32[]{:S(2)}, u32[]{:S(2)}) async-start(bf16[64,2,3,16,128]{4,3,2,1,0:T(8,128)(2,1)} %shard_map.100), calls=%async_computation | async-start | bytes 3145728 | tf_op jit(solution)/shard_map/all_to_all | solution.py:91
  62.7 9.8 %copy-start.5 = (bf16[128,3,3]{0,2,1:T(4,128)(2,1)S(1)}, bf16[128,3,3]{0,2,1:T(4,128)(2,1)}, u32[]{:S(2)}) copy-start(bf16[128,3,3]{0,2,1:T(4,128)(2,1)} %param.17) | copy-start | bytes 6916
  63.6 30.1 %all-to-all-start.1 = ((bf16[64,3,16,128]{3,2,1,0:T(8,128)(2,1)}), bf16[64,3,16,128]{3,2,1,0:T(8,128)(2,1)S(1)}, u32[]{:S(2)}, u32[]{:S(2)}) async-start(bf16[64,3,16,128]{3,2,1,0:T(8,128)(2,1)} %bitcast.15), calls=%async_computation.1 | async-start | bytes 1572864 | tf_op jit(solution)/shard_map/all_to_all | solution.py:58
  94.9 1.1 copy-start.3
  96.1 6.2 %slice-start = ((s8[8388608]{0:T(1024)(128)(4,1)}), s8[4194304]{0:T(1024)(128)(4,1)S(1)}, s32[]{:S(2)}) async-start(s8[8388608]{0:T(1024)(128)(4,1)} %bitcast.148), calls=%async_computation.2 | async-start | bytes 8388608
  96.3 6.0 %slice-start.1 = ((s8[8388608]{0:T(1024)(128)(4,1)}), s8[4194304]{0:T(1024)(128)(4,1)S(1)}, s32[]{:S(2)}) async-start(s8[8388608]{0:T(1024)(128)(4,1)} %bitcast.148), calls=%async_computation.3 | async-start | bytes 8388608
  99.1 5.3 %copy-start.2 = (f32[384,1024]{1,0:T(8,128)}, f32[384,1024]{1,0:T(8,128)S(1)}, u32[]{:S(2)}) copy-start(f32[384,1024]{1,0:T(8,128)S(1)} %fusion) | copy-start | bytes 4718596
  102.4 7.3 %copy-start.1 = (f32[384,1024]{1,0:T(8,128)}, f32[384,1024]{1,0:T(8,128)S(1)}, u32[]{:S(2)}) copy-start(f32[384,1024]{1,0:T(8,128)S(1)} %fusion.2) | copy-start | bytes 4718596
  105.2 7.4 %collective-permute-start.6 = (bf16[2,96,1024]{2,1,0:T(8,128)(2,1)}, bf16[2,96,1024]{2,1,0:T(8,128)(2,1)}, u32[]{:S(2)}, u32[]{:S(2)}) collective-permute-start(bf16[2,96,1024]{2,1,0:T(8,128)(2,1)} %fusion.25), channel_id=1, source_target_pairs={{0,1},{1,0},{2,3},{3,2},{4,5},{5,4},{6,7},{7,6},{8,9},{9,8},{10,11... | collective-permute-start | bytes 1179656 | tf_op jit(solution)/shard_map/ppermute | solution.py:121
  110.5 3.7 %collective-permute-start.4 = (bf16[2,96,1024]{2,1,0:T(8,128)(2,1)}, bf16[2,96,1024]{2,1,0:T(8,128)(2,1)}, u32[]{:S(2)}, u32[]{:S(2)}) collective-permute-start(bf16[2,96,1024]{2,1,0:T(8,128)(2,1)} %fusion.24), channel_id=1, source_target_pairs={{0,1},{1,0},{2,3},{3,2},{4,5},{5,4},{6,7},{7,6},{8,9},{9,8},{10,11... | collective-permute-start | bytes 1179656 | tf_op jit(solution)/shard_map/ppermute | solution.py:121
  111.3 5.1 %collective-permute-start.2 = (bf16[2,96,1024]{2,1,0:T(8,128)(2,1)}, bf16[2,96,1024]{2,1,0:T(8,128)(2,1)}, u32[]{:S(2)}, u32[]{:S(2)}) collective-permute-start(bf16[2,96,1024]{2,1,0:T(8,128)(2,1)} %fusion.23), channel_id=1, source_target_pairs={{0,1},{1,0},{2,3},{3,2},{4,5},{5,4},{6,7},{7,6},{8,9},{9,8},{10,11... | collective-permute-start | bytes 1179656 | tf_op jit(solution)/shard_map/ppermute | solution.py:121
  112.6 5.3 %collective-permute-start = (bf16[2,96,1024]{2,1,0:T(8,128)(2,1)}, bf16[2,96,1024]{2,1,0:T(8,128)(2,1)}, u32[]{:S(2)}, u32[]{:S(2)}) collective-permute-start(bf16[2,96,1024]{2,1,0:T(8,128)(2,1)} %fusion.22), channel_id=1, source_target_pairs={{0,1},{1,0},{2,3},{3,2},{4,5},{5,4},{6,7},{7,6},{8,9},{9,8},{10,11... | collective-permute-start | bytes 1179656 | tf_op jit(solution)/shard_map/ppermute | solution.py:121
  113.7 6.3 %collective-permute-start.7 = (bf16[96,1024]{1,0:T(8,128)(2,1)S(1)}, bf16[96,1024]{1,0:T(8,128)(2,1)S(1)}, u32[]{:S(2)}, u32[]{:S(2)}) collective-permute-start(bf16[96,1024]{1,0:T(8,128)(2,1)S(1)} %fusion.26), channel_id=1, source_target_pairs={{0,2},{1,3},{2,0},{3,1},{4,6},{5,7},{6,4},{7,5},{8,10},{9,11},{10,... | collective-permute-start | bytes 589832 | tf_op jit(solution)/shard_map/ppermute | solution.py:121
  115.2 8.7 %collective-permute-start.5 = (bf16[96,1024]{1,0:T(8,128)(2,1)S(1)}, bf16[96,1024]{1,0:T(8,128)(2,1)S(1)}, u32[]{:S(2)}, u32[]{:S(2)}) collective-permute-start(bf16[96,1024]{1,0:T(8,128)(2,1)S(1)} %fusion.29), channel_id=1, source_target_pairs={{0,2},{1,3},{2,0},{3,1},{4,6},{5,7},{6,4},{7,5},{8,10},{9,11},{10,... | collective-permute-start | bytes 589832 | tf_op jit(solution)/shard_map/ppermute | solution.py:121
  117.4 10.8 %collective-permute-start.3 = (bf16[96,1024]{1,0:T(8,128)(2,1)S(1)}, bf16[96,1024]{1,0:T(8,128)(2,1)S(1)}, u32[]{:S(2)}, u32[]{:S(2)}) collective-permute-start(bf16[96,1024]{1,0:T(8,128)(2,1)S(1)} %fusion.32), channel_id=1, source_target_pairs={{0,2},{1,3},{2,0},{3,1},{4,6},{5,7},{6,4},{7,5},{8,10},{9,11},{10,... | collective-permute-start | bytes 589832 | tf_op jit(solution)/shard_map/ppermute | solution.py:121
  118.8 13.5 %collective-permute-start.1 = (bf16[96,1024]{1,0:T(8,128)(2,1)S(1)}, bf16[96,1024]{1,0:T(8,128)(2,1)S(1)}, u32[]{:S(2)}, u32[]{:S(2)}) collective-permute-start(bf16[96,1024]{1,0:T(8,128)(2,1)S(1)} %fusion.35), channel_id=1, source_target_pairs={{0,2},{1,3},{2,0},{3,1},{4,6},{5,7},{6,4},{7,5},{8,10},{9,11},{10,... | collective-permute-start | bytes 589832 | tf_op jit(solution)/shard_map/ppermute | solution.py:121

commit v11 on v10

--- a/solution.py
+++ b/solution.py
@@ -125,11 +125,13 @@
     me = lax.axis_index("chan")
     core = me % 2
     chip = me // 2
+    rows, _ = gated.shape
     width = out_weight.shape[1] // blocks
-    pieces = []
+    out = jnp.zeros((rows // 4, out_weight.shape[1]), jnp.bfloat16)
     for block in range(blocks):
-        pieces.append(scatter_block(gated, out_weight, block, width, core, chip))
-    return jnp.concatenate(pieces, axis=1)
+        piece = scatter_block(gated, out_weight, block, width, core, chip)
+        out = lax.dynamic_update_slice_in_dim(out, piece, block * width, axis=1)
+    return out
 
 
 def scatter_block(gated, out_weight, block, width, core, chip):

time: 135 us -> 135 us (level)
    dynamic_update_slice x0 -> x3, other arithmetic: none -> 3.77 us  [scatter_sum(): out = lax.dynamic_update_slice_in_dim(out, piece, block * width, axis=1)]
    convert_element_type x4 -> x1, other arithmetic: 4.23 us -> 1.12 us  [scatter_block(): return (mine + quarter.astype(jnp.float32)).astype(jnp.bfloat16)]
where the time goes in v11:
time: 135 us; the launch traced here: 134 us
  waiting for transfers between devices  67.8 us (50%)
  starting transfers between devices  32.3 us (24%)
  other arithmetic  14.3 us (11%)
  matrix products  9.26 us (7%)
  local copies, waits for them, and re-layouts  6.4 us (5%)
  Pallas kernels  3.59 us (3%)
    all_to_all x1, waiting for transfers between devices, per_device(): both_cols = lax.all_to_all(parts, 'seq', 0, 0, tiled=True)  37.6 us
    all_to_all x1, waiting for transfers between devices, from_columns(): back = lax.all_to_all(values, 'seq', 0, 0, tiled=True)  21.1 us
    all_to_all x1, starting transfers between devices, per_device(): both_cols = lax.all_to_all(parts, 'seq', 0, 0, tiled=True)  15.2 us
    ppermute x8, waiting for transfers between devices, exchange(): return lax.ppermute(value, 'chan', pairs)  9.05 us
    all_to_all x1, starting transfers between devices, from_columns(): back = lax.all_to_all(values, 'seq', 0, 0, tiled=True)  8.79 us
    ppermute x8, starting transfers between devices, exchange(): return lax.ppermute(value, 'chan', pairs)  8.28 us
    dot_general x4, matrix products, scatter_block(): product = jnp.dot(gated, weight, preferred_element_type=jnp.float32)  7.91 us
    convert_element_type x4, other arithmetic, scatter_block(): quarter = exchange(other.astype(jnp.bfloat16), 2)  4.1 us
  transfers between devices with their start and end apart: 10, of which 5 were waited for; matrix products, arithmetic and copies ran while one was open for 8% of the time, Pallas kernels for 0%

profile of v11, /device:TPU:1, one launch (start us, length us, event | category | flops | bytes accessed | tf_op | source)
XLA Modules:
  0.0 134.1 jit_solution(15060370342797460062)
XLA Ops:
  1.5 3.6 %shard_map.100 = bf16[64,2,3,16,128]{4,3,2,1,0:T(8,128)(2,1)} custom-call(bf16[384,1024]{1,0:T(8,128)(2,1)} %gin_ref.1, bf16[384,1024]{1,0:T(8,128)(2,1)} %vin_ref.1, bf16[384,1024]{1,0:T(8,128)(2,1)} %filt_ref.1, bf16[3,128,128]{2,1,0:T(8,128)(2,1)} %blocks_ref.1, f32[128,9]{1,0:T(8,128)} %copy.24.mix_ref), custom_call_target="tpu_custom_call" | custom-call | flops 107741184 | bytes 3932160 | tf_op jit(solution)/shard_map/pallas_call | solution.py:42
  5.1 15.2 %all-to-all-start = ((bf16[64,2,3,16,128]{4,3,2,1,0:T(8,128)(2,1)}), bf16[64,2,3,16,128]{4,3,2,1,0:T(8,128)(2,1)S(1)}, u32[]{:S(2)}, u32[]{:S(2)}) async-start(bf16[64,2,3,16,128]{4,3,2,1,0:T(8,128)(2,1)} %shard_map.100), calls=%async_computation | async-start | bytes 3145728 | tf_op jit(solution)/shard_map/all_to_all | solution.py:91
  20.6 37.6 %all-to-all-done = bf16[64,2,3,16,128]{4,3,2,1,0:T(8,128)(2,1)S(1)} async-done(((bf16[64,2,3,16,128]{4,3,2,1,0:T(8,128)(2,1)}), bf16[64,2,3,16,128]{4,3,2,1,0:T(8,128)(2,1)S(1)}, u32[]{:S(2)}, u32[]{:S(2)}) %all-to-all-start) | async-done | bytes 1572896 | tf_op jit(solution)/shard_map/all_to_all | solution.py:91
  62.7 0.9 pad_maximum_fusion.10
  63.6 8.8 %all-to-all-start.1 = ((bf16[64,3,16,128]{3,2,1,0:T(8,128)(2,1)}), bf16[64,3,16,128]{3,2,1,0:T(8,128)(2,1)S(1)}, u32[]{:S(2)}, u32[]{:S(2)}) async-start(bf16[64,3,16,128]{3,2,1,0:T(8,128)(2,1)} %bitcast.15), calls=%async_computation.1 | async-start | bytes 1572864 | tf_op jit(solution)/shard_map/all_to_all | solution.py:58
  72.7 21.1 %all-to-all-done.1 = bf16[64,3,16,128]{3,2,1,0:T(8,128)(2,1)S(1)} async-done(((bf16[64,3,16,128]{3,2,1,0:T(8,128)(2,1)}), bf16[64,3,16,128]{3,2,1,0:T(8,128)(2,1)S(1)}, u32[]{:S(2)}, u32[]{:S(2)}) %all-to-all-start.1) | async-done | bytes 786464 | tf_op jit(solution)/shard_map/all_to_all | solution.py:58
  96.4 2.7 %fusion.6 = f32[384,1024]{1,0:T(8,128)S(1)} fusion(bf16[384,1024]{1,0:T(8,128)(2,1)S(1)} %fusion.8, bf16[1024,4096]{1,0:T(8,128)(2,1)} %param.19), kind=kOutput, calls=%fused_computation.6 | convolution fusion | flops 805306368 | bytes 4456448 | tf_op jit(solution)/shard_map/dot_general | solution.py:140
  99.1 3.2 %fusion.4 = f32[384,1024]{1,0:T(8,128)S(1)} fusion(bf16[384,1024]{1,0:T(8,128)(2,1)S(1)} %fusion.8, bf16[1024,4096]{1,0:T(8,128)(2,1)} %param.19), kind=kOutput, calls=%fused_computation.4 | convolution fusion | flops 805306368 | bytes 4456448 | tf_op jit(solution)/shard_map/dot_general | solution.py:140
  102.4 1.0 fusion.2
  103.4 1.0 fusion
  105.2 4.5 %collective-permute-start = (bf16[2,96,1024]{2,1,0:T(8,128)(2,1)}, bf16[2,96,1024]{2,1,0:T(8,128)(2,1)}, u32[]{:S(2)}, u32[]{:S(2)}) collective-permute-start(bf16[2,96,1024]{2,1,0:T(8,128)(2,1)} %fusion.22), channel_id=1, source_target_pairs={{0,1},{1,0},{2,3},{3,2},{4,5},{5,4},{6,7},{7,6},{8,9},{9,8},{10,11... | collective-permute-start | bytes 1179656 | tf_op jit(solution)/shard_map/ppermute | solution.py:121
  112.6 1.1 fusion.35
  114.2 1.1 fusion.32
  115.3 1.2 collective-permute-start.3
  116.4 1.0 fusion.29
  117.9 1.0 fusion.26
  118.9 1.2 collective-permute-start.7
  120.0 1.1 fusion.37
  121.2 2.7 %collective-permute-done.3 = bf16[96,1024]{1,0:T(8,128)(2,1)S(1)} collective-permute-done((bf16[96,1024]{1,0:T(8,128)(2,1)S(1)}, bf16[96,1024]{1,0:T(8,128)(2,1)S(1)}, u32[]{:S(2)}, u32[]{:S(2)}) %collective-permute-start.3) | collective-permute-done | bytes 196640 | tf_op jit(solution)/shard_map/ppermute | solution.py:121
  124.0 1.1 fusion.38
  125.1 3.1 %collective-permute-done.5 = bf16[96,1024]{1,0:T(8,128)(2,1)S(1)} collective-permute-done((bf16[96,1024]{1,0:T(8,128)(2,1)S(1)}, bf16[96,1024]{1,0:T(8,128)(2,1)S(1)}, u32[]{:S(2)}, u32[]{:S(2)}) %collective-permute-start.5) | collective-permute-done | bytes 196640 | tf_op jit(solution)/shard_map/ppermute | solution.py:121
  128.2 1.0 fusion.39
  129.2 3.2 %collective-permute-done.7 = bf16[96,1024]{1,0:T(8,128)(2,1)S(1)} collective-permute-done((bf16[96,1024]{1,0:T(8,128)(2,1)S(1)}, bf16[96,1024]{1,0:T(8,128)(2,1)S(1)}, u32[]{:S(2)}, u32[]{:S(2)}) %collective-permute-start.7) | collective-permute-done | bytes 196640 | tf_op jit(solution)/shard_map/ppermute | solution.py:121
  132.4 1.7 %fusion.40 = bf16[96,4096]{1,0:T(8,128)(2,1)} fusion(bf16[96,4096]{1,0:T(8,128)(2,1)} %copy-done.3, bf16[96,1024]{1,0:T(8,128)(2,1)S(1)} %collective-permute-done.7, f32[2,2,96,1024]{3,2,1,0:T(8,128)S(1)} %bitcast.144, s32[]{:T(128)S(6)} %select_n.63, s32[]{:T(128)S(6)} %select_n.66, bf16[2,96,1024]{2,1,0:T(8,128)(2,1)} %collective-permute-done.6, ...), kind=kLoop, calls=%fused_computation.110 | loop fusion | flops 491520 | bytes 983052 | tf_op jit(solution)/shard_map/dynamic_update_slice | solution.py:133
  (62 shorter events, 13.6 us)
Async XLA Ops:
  0.0 94.9 %copy-start = (bf16[3,128,128]{2,1,0:T(8,128)(2,1)S(1)}, bf16[3,128,128]{2,1,0:T(8,128)(2,1)}, u32[]{:S(2)}) copy-start(bf16[3,128,128]{2,1,0:T(8,128)(2,1)} %param.16) | copy-start | bytes 294916
  5.1 15.3 %copy-start.5 = (f32[6,384]{1,0:T(8,128)S(1)}, f32[6,384]{1,0:T(8,128)}, u32[]{:S(2)}) copy-start(f32[6,384]{1,0:T(8,128)} %param.18) | copy-start | bytes 27652
  5.1 53.2 %all-to-all-start = ((bf16[64,2,3,16,128]{4,3,2,1,0:T(8,128)(2,1)}), bf16[64,2,3,16,128]{4,3,2,1,0:T(8,128)(2,1)S(1)}, u32[]{:S(2)}, u32[]{:S(2)}) async-start(bf16[64,2,3,16,128]{4,3,2,1,0:T(8,128)(2,1)} %shard_map.100), calls=%async_computation | async-start | bytes 3145728 | tf_op jit(solution)/shard_map/all_to_all | solution.py:91
  62.7 9.8 %copy-start.6 = (bf16[128,3,3]{0,2,1:T(4,128)(2,1)S(1)}, bf16[128,3,3]{0,2,1:T(4,128)(2,1)}, u32[]{:S(2)}) copy-start(bf16[128,3,3]{0,2,1:T(4,128)(2,1)} %param.17) | copy-start | bytes 6916
  63.6 30.1 %all-to-all-start.1 = ((bf16[64,3,16,128]{3,2,1,0:T(8,128)(2,1)}), bf16[64,3,16,128]{3,2,1,0:T(8,128)(2,1)S(1)}, u32[]{:S(2)}, u32[]{:S(2)}) async-start(bf16[64,3,16,128]{3,2,1,0:T(8,128)(2,1)} %bitcast.15), calls=%async_computation.1 | async-start | bytes 1572864 | tf_op jit(solution)/shard_map/all_to_all | solution.py:58
  95.0 1.1 copy-start.4
  96.1 6.3 %slice-start = ((s8[8388608]{0:T(1024)(128)(4,1)}), s8[4194304]{0:T(1024)(128)(4,1)S(1)}, s32[]{:S(2)}) async-start(s8[8388608]{0:T(1024)(128)(4,1)} %bitcast.154), calls=%async_computation.2 | async-start | bytes 8388608
  96.4 6.0 %slice-start.1 = ((s8[8388608]{0:T(1024)(128)(4,1)}), s8[4194304]{0:T(1024)(128)(4,1)S(1)}, s32[]{:S(2)}) async-start(s8[8388608]{0:T(1024)(128)(4,1)} %bitcast.154), calls=%async_computation.3 | async-start | bytes 8388608
  99.1 5.3 %copy-start.2 = (f32[384,1024]{1,0:T(8,128)}, f32[384,1024]{1,0:T(8,128)S(1)}, u32[]{:S(2)}) copy-start(f32[384,1024]{1,0:T(8,128)S(1)} %fusion.6) | copy-start | bytes 4718596
  102.4 7.3 %copy-start.1 = (f32[384,1024]{1,0:T(8,128)}, f32[384,1024]{1,0:T(8,128)S(1)}, u32[]{:S(2)}) copy-start(f32[384,1024]{1,0:T(8,128)S(1)} %fusion.4) | copy-start | bytes 4718596
  105.2 7.5 %collective-permute-start = (bf16[2,96,1024]{2,1,0:T(8,128)(2,1)}, bf16[2,96,1024]{2,1,0:T(8,128)(2,1)}, u32[]{:S(2)}, u32[]{:S(2)}) collective-permute-start(bf16[2,96,1024]{2,1,0:T(8,128)(2,1)} %fusion.22), channel_id=1, source_target_pairs={{0,1},{1,0},{2,3},{3,2},{4,5},{5,4},{6,7},{7,6},{8,9},{9,8},{10,11... | collective-permute-start | bytes 1179656 | tf_op jit(solution)/shard_map/ppermute | solution.py:121
  110.5 3.7 %collective-permute-start.2 = (bf16[2,96,1024]{2,1,0:T(8,128)(2,1)}, bf16[2,96,1024]{2,1,0:T(8,128)(2,1)}, u32[]{:S(2)}, u32[]{:S(2)}) collective-permute-start(bf16[2,96,1024]{2,1,0:T(8,128)(2,1)} %fusion.23), channel_id=1, source_target_pairs={{0,1},{1,0},{2,3},{3,2},{4,5},{5,4},{6,7},{7,6},{8,9},{9,8},{10,11... | collective-permute-start | bytes 1179656 | tf_op jit(solution)/shard_map/ppermute | solution.py:121
  111.3 5.2 %collective-permute-start.4 = (bf16[2,96,1024]{2,1,0:T(8,128)(2,1)}, bf16[2,96,1024]{2,1,0:T(8,128)(2,1)}, u32[]{:S(2)}, u32[]{:S(2)}) collective-permute-start(bf16[2,96,1024]{2,1,0:T(8,128)(2,1)} %fusion.24), channel_id=1, source_target_pairs={{0,1},{1,0},{2,3},{3,2},{4,5},{5,4},{6,7},{7,6},{8,9},{9,8},{10,11... | collective-permute-start | bytes 1179656 | tf_op jit(solution)/shard_map/ppermute | solution.py:121
  112.6 5.3 %collective-permute-start.6 = (bf16[2,96,1024]{2,1,0:T(8,128)(2,1)}, bf16[2,96,1024]{2,1,0:T(8,128)(2,1)}, u32[]{:S(2)}, u32[]{:S(2)}) collective-permute-start(bf16[2,96,1024]{2,1,0:T(8,128)(2,1)} %fusion.25), channel_id=1, source_target_pairs={{0,1},{1,0},{2,3},{3,2},{4,5},{5,4},{6,7},{7,6},{8,9},{9,8},{10,11... | collective-permute-start | bytes 1179656 | tf_op jit(solution)/shard_map/ppermute | solution.py:121
  113.7 6.3 %collective-permute-start.1 = (bf16[96,1024]{1,0:T(8,128)(2,1)S(1)}, bf16[96,1024]{1,0:T(8,128)(2,1)S(1)}, u32[]{:S(2)}, u32[]{:S(2)}) collective-permute-start(bf16[96,1024]{1,0:T(8,128)(2,1)S(1)} %fusion.35), channel_id=1, source_target_pairs={{0,2},{1,3},{2,0},{3,1},{4,6},{5,7},{6,4},{7,5},{8,10},{9,11},{10,... | collective-permute-start | bytes 589832 | tf_op jit(solution)/shard_map/ppermute | solution.py:121
  115.3 8.7 %collective-permute-start.3 = (bf16[96,1024]{1,0:T(8,128)(2,1)S(1)}, bf16[96,1024]{1,0:T(8,128)(2,1)S(1)}, u32[]{:S(2)}, u32[]{:S(2)}) collective-permute-start(bf16[96,1024]{1,0:T(8,128)(2,1)S(1)} %fusion.32), channel_id=1, source_target_pairs={{0,2},{1,3},{2,0},{3,1},{4,6},{5,7},{6,4},{7,5},{8,10},{9,11},{10,... | collective-permute-start | bytes 589832 | tf_op jit(solution)/shard_map/ppermute | solution.py:121
  117.4 10.8 %collective-permute-start.5 = (bf16[96,1024]{1,0:T(8,128)(2,1)S(1)}, bf16[96,1024]{1,0:T(8,128)(2,1)S(1)}, u32[]{:S(2)}, u32[]{:S(2)}) collective-permute-start(bf16[96,1024]{1,0:T(8,128)(2,1)S(1)} %fusion.29), channel_id=1, source_target_pairs={{0,2},{1,3},{2,0},{3,1},{4,6},{5,7},{6,4},{7,5},{8,10},{9,11},{10,... | collective-permute-start | bytes 589832 | tf_op jit(solution)/shard_map/ppermute | solution.py:121
  118.9 13.5 %collective-permute-start.7 = (bf16[96,1024]{1,0:T(8,128)(2,1)S(1)}, bf16[96,1024]{1,0:T(8,128)(2,1)S(1)}, u32[]{:S(2)}, u32[]{:S(2)}) collective-permute-start(bf16[96,1024]{1,0:T(8,128)(2,1)S(1)} %fusion.26), channel_id=1, source_target_pairs={{0,2},{1,3},{2,0},{3,1},{4,6},{5,7},{6,4},{7,5},{8,10},{9,11},{10,... | collective-permute-start | bytes 589832 | tf_op jit(solution)/shard_map/ppermute | solution.py:121
  129.2 3.2 %copy-start.3 = (bf16[96,4096]{1,0:T(8,128)(2,1)}, bf16[96,4096]{1,0:T(8,128)(2,1)S(1)}, u32[]{:S(2)}) copy-start(bf16[96,4096]{1,0:T(8,128)(2,1)S(1)} %fusion.39) | copy-start | bytes 2359300

commit v12 on v10

--- a/solution.py
+++ b/solution.py
@@ -121,20 +121,27 @@
     return lax.ppermute(value, "chan", pairs)
 
 
-def scatter_sum(gated, out_weight, blocks=4):
+SHARES = (1.5, 1.5, 1.5, 1.5, 2)
+
+
+def scatter_sum(gated, out_weight, shares=SHARES):
     me = lax.axis_index("chan")
     core = me % 2
     chip = me // 2
-    width = out_weight.shape[1] // blocks
+    unit = out_weight.shape[1] // 8
+    bounds = [0]
+    for share in shares:
+        bounds.append(bounds[-1] + int(share * unit))
     pieces = []
-    for block in range(blocks):
-        pieces.append(scatter_block(gated, out_weight, block, width, core, chip))
+    for block in range(len(shares)):
+        pieces.append(scatter_block(gated, out_weight, bounds[block], bounds[block + 1], core, chip))
     return jnp.concatenate(pieces, axis=1)
 
 
-def scatter_block(gated, out_weight, block, width, core, chip):
+def scatter_block(gated, out_weight, start, stop, core, chip):
     rows = gated.shape[0]
-    weight = out_weight[:, block * width : (block + 1) * width]
+    width = stop - start
+    weight = out_weight[:, start:stop]
     product = jnp.dot(gated, weight, preferred_element_type=jnp.float32)
     quarters = product.reshape(2, 2, rows // 4, width)
     sent = lax.dynamic_index_in_dim(quarters, 1 - core, axis=1, keepdims=False)

time: 135 us -> 134 us (level)
  other arithmetic: 14.5 us -> 6.41 us
  waiting for transfers between devices: 67.9 us -> 73.7 us
  matrix products: 9.26 us -> 12.7 us
  local copies, waits for them, and re-layouts: 6.3 us -> 3.26 us
  starting transfers between devices: 32.3 us -> 33.9 us
    ppermute x8 -> x10, waiting for transfers between devices: 9.13 us -> 15 us  [exchange(): return lax.ppermute(value, 'chan', pairs)]
    convert_element_type x4 -> x0, other arithmetic: 4.23 us -> none  [scatter_block(): return (mine + quarter.astype(jnp.float32)).astype(jnp.bfloat16)]
    convert_element_type x4 -> x5, other arithmetic: 4.1 us -> 0.18 us  [scatter_block(): quarter = exchange(other.astype(jnp.bfloat16), 2)]
    dot_general x4 -> x5, matrix products: 7.91 us -> 11.3 us  [scatter_block(): product = jnp.dot(gated, weight, preferred_element_type=jnp.float32)]
    convert_element_type x4 -> x5, local copies, waits for them, and re-layouts: 3.22 us -> 0.18 us  [scatter_block(): half = exchange(sent.astype(jnp.bfloat16), 1)]
    ppermute x8 -> x10, starting transfers between devices: 8.28 us -> 9.89 us  [exchange(): return lax.ppermute(value, 'chan', pairs)]
  transfers between devices with their start and end apart: 10 -> 12, of which waited for: 5 -> 7; matrix products, arithmetic and copies ran while one was open for 8% -> 1% of each run, Pallas kernels for 0% -> 0%
where the time goes in v12:
time: 134 us
  waiting for transfers between devices  73.7 us (55%)
  starting transfers between devices  33.9 us (25%)
  matrix products  12.7 us (9%)
  other arithmetic  6.41 us (5%)
  Pallas kernels  3.57 us (3%)
  local copies, waits for them, and re-layouts  3.26 us (2%)
    all_to_all x1, waiting for transfers between devices, per_device(): both_cols = lax.all_to_all(parts, 'seq', 0, 0, tiled=True)  37.6 us
    all_to_all x1, waiting for transfers between devices, from_columns(): back = lax.all_to_all(values, 'seq', 0, 0, tiled=True)  21.1 us
    all_to_all x1, starting transfers between devices, per_device(): both_cols = lax.all_to_all(parts, 'seq', 0, 0, tiled=True)  15.2 us
    ppermute x10, waiting for transfers between devices, exchange(): return lax.ppermute(value, 'chan', pairs)  15 us
    dot_general x5, matrix products, scatter_block(): product = jnp.dot(gated, weight, preferred_element_type=jnp.float32)  11.3 us
    ppermute x10, starting transfers between devices, exchange(): return lax.ppermute(value, 'chan', pairs)  9.89 us
    all_to_all x1, starting transfers between devices, from_columns(): back = lax.all_to_all(values, 'seq', 0, 0, tiled=True)  8.79 us
    pallas_call x1, Pallas kernels, prelude(): pl.pallas_call(prelude_kernel, out_shape=jax.ShapeDtypeStruct((count, 2,...  3.57 us
  transfers between devices with their start and end apart: 12, of which 7 were waited for; matrix products, arithmetic and copies ran while one was open for 1% of the time, Pallas kernels for 0%

profile of v12, /device:TPU:1, one launch (start us, length us, event | category | flops | bytes accessed | tf_op | source)
XLA Modules:
  0.0 134.0 jit_solution(550134232546784221)
XLA Ops:
  0.0 0.7 reshape.252
  0.7 0.7 copy.26.mix_ref
  1.5 3.6 %shard_map.100 = bf16[64,2,3,16,128]{4,3,2,1,0:T(8,128)(2,1)} custom-call(bf16[384,1024]{1,0:T(8,128)(2,1)} %gin_ref.1, bf16[384,1024]{1,0:T(8,128)(2,1)} %vin_ref.1, bf16[384,1024]{1,0:T(8,128)(2,1)} %filt_ref.1, bf16[3,128,128]{2,1,0:T(8,128)(2,1)} %blocks_ref.1, f32[128,9]{1,0:T(8,128)} %copy.26.mix_ref), custom_call_target="tpu_custom_call" | custom-call | flops 107741184 | bytes 3932160 | tf_op jit(solution)/shard_map/pallas_call | solution.py:42
  5.0 15.2 %all-to-all-start = ((bf16[64,2,3,16,128]{4,3,2,1,0:T(8,128)(2,1)}), bf16[64,2,3,16,128]{4,3,2,1,0:T(8,128)(2,1)S(1)}, u32[]{:S(2)}, u32[]{:S(2)}) async-start(bf16[64,2,3,16,128]{4,3,2,1,0:T(8,128)(2,1)} %shard_map.100), calls=%async_computation | async-start | bytes 3145728 | tf_op jit(solution)/shard_map/all_to_all | solution.py:91
  20.6 37.6 %all-to-all-done = bf16[64,2,3,16,128]{4,3,2,1,0:T(8,128)(2,1)S(1)} async-done(((bf16[64,2,3,16,128]{4,3,2,1,0:T(8,128)(2,1)}), bf16[64,2,3,16,128]{4,3,2,1,0:T(8,128)(2,1)S(1)}, u32[]{:S(2)}, u32[]{:S(2)}) %all-to-all-start) | async-done | bytes 1572896 | tf_op jit(solution)/shard_map/all_to_all | solution.py:91
  62.7 0.9 pad_maximum_fusion.10
  63.6 8.8 %all-to-all-start.1 = ((bf16[64,3,16,128]{3,2,1,0:T(8,128)(2,1)}), bf16[64,3,16,128]{3,2,1,0:T(8,128)(2,1)S(1)}, u32[]{:S(2)}, u32[]{:S(2)}) async-start(bf16[64,3,16,128]{3,2,1,0:T(8,128)(2,1)} %bitcast.15), calls=%async_computation.1 | async-start | bytes 1572864 | tf_op jit(solution)/shard_map/all_to_all | solution.py:58
  72.7 21.1 %all-to-all-done.1 = bf16[64,3,16,128]{3,2,1,0:T(8,128)(2,1)S(1)} async-done(((bf16[64,3,16,128]{3,2,1,0:T(8,128)(2,1)}), bf16[64,3,16,128]{3,2,1,0:T(8,128)(2,1)S(1)}, u32[]{:S(2)}, u32[]{:S(2)}) %all-to-all-start.1) | async-done | bytes 786464 | tf_op jit(solution)/shard_map/all_to_all | solution.py:58
  94.2 0.7 fusion.11
  94.9 0.7 fusion.22
  96.3 2.2 %fusion.9 = f32[384,768]{1,0:T(8,128)S(1)} fusion(bf16[384,1024]{1,0:T(8,128)(2,1)S(1)} %fusion.2, bf16[1024,4096]{1,0:T(8,128)(2,1)} %param.19), kind=kOutput, calls=%fused_computation.31 | convolution fusion | flops 603979776 | bytes 3538944 | tf_op jit(solution)/shard_map/dot_general | solution.py:145
  98.5 2.2 %fusion.7 = f32[384,768]{1,0:T(8,128)S(1)} fusion(bf16[384,1024]{1,0:T(8,128)(2,1)S(1)} %fusion.2, bf16[1024,4096]{1,0:T(8,128)(2,1)} %param.19), kind=kOutput, calls=%fused_computation.29 | convolution fusion | flops 603979776 | bytes 3538944 | tf_op jit(solution)/shard_map/dot_general | solution.py:145
  100.7 2.2 %fusion.5 = f32[384,768]{1,0:T(8,128)S(1)} fusion(bf16[384,1024]{1,0:T(8,128)(2,1)S(1)} %fusion.2, bf16[1024,4096]{1,0:T(8,128)(2,1)} %param.19), kind=kOutput, calls=%fused_computation.27 | convolution fusion | flops 603979776 | bytes 3538944 | tf_op jit(solution)/shard_map/dot_general | solution.py:145
  102.9 2.2 %fusion.3 = f32[384,768]{1,0:T(8,128)S(1)} fusion(bf16[384,1024]{1,0:T(8,128)(2,1)S(1)} %fusion.2, bf16[1024,4096]{1,0:T(8,128)(2,1)} %param.19), kind=kOutput, calls=%fused_computation.25 | convolution fusion | flops 603979776 | bytes 3538944 | tf_op jit(solution)/shard_map/dot_general | solution.py:145
  105.1 2.6 %fusion = f32[384,1024]{1,0:T(8,128)S(1)} fusion(bf16[384,1024]{1,0:T(8,128)(2,1)S(1)} %fusion.2, bf16[1024,4096]{1,0:T(8,128)(2,1)} %param.19), kind=kOutput, calls=%fused_computation | convolution fusion | flops 805306368 | bytes 4456448 | tf_op jit(solution)/shard_map/dot_general | solution.py:145
  107.7 4.6 %collective-permute-start = (bf16[2,96,768]{2,1,0:T(8,128)(2,1)S(1)}, bf16[2,96,768]{2,1,0:T(8,128)(2,1)S(1)}, u32[]{:S(2)}, u32[]{:S(2)}) collective-permute-start(bf16[2,96,768]{2,1,0:T(8,128)(2,1)S(1)} %fusion.28), channel_id=1, source_target_pairs={{0,1},{1,0},{2,3},{3,2},{4,5},{5,4},{6,7},{7,6},{8,9},{9,8},{10,11... | collective-permute-start | bytes 884744 | tf_op jit(solution)/shard_map/ppermute | solution.py:121
  114.6 1.2 collective-permute-start.3
  116.3 1.2 collective-permute-start.7
  118.0 1.5 %collective-permute-done.1 = bf16[96,768]{1,0:T(8,128)(2,1)S(1)} collective-permute-done((bf16[96,768]{1,0:T(8,128)(2,1)S(1)}, bf16[96,768]{1,0:T(8,128)(2,1)S(1)}, u32[]{:S(2)}, u32[]{:S(2)}) %collective-permute-start.1) | collective-permute-done | bytes 147488 | tf_op jit(solution)/shard_map/ppermute | solution.py:121
  119.6 3.1 %collective-permute-done.3 = bf16[96,768]{1,0:T(8,128)(2,1)S(1)} collective-permute-done((bf16[96,768]{1,0:T(8,128)(2,1)S(1)}, bf16[96,768]{1,0:T(8,128)(2,1)S(1)}, u32[]{:S(2)}, u32[]{:S(2)}) %collective-permute-start.3) | collective-permute-done | bytes 147488 | tf_op jit(solution)/shard_map/ppermute | solution.py:121
  122.7 3.1 %collective-permute-done.5 = bf16[96,768]{1,0:T(8,128)(2,1)S(1)} collective-permute-done((bf16[96,768]{1,0:T(8,128)(2,1)S(1)}, bf16[96,768]{1,0:T(8,128)(2,1)S(1)}, u32[]{:S(2)}, u32[]{:S(2)}) %collective-permute-start.5) | collective-permute-done | bytes 147488 | tf_op jit(solution)/shard_map/ppermute | solution.py:121
  125.9 3.1 %collective-permute-done.7 = bf16[96,768]{1,0:T(8,128)(2,1)S(1)} collective-permute-done((bf16[96,768]{1,0:T(8,128)(2,1)S(1)}, bf16[96,768]{1,0:T(8,128)(2,1)S(1)}, u32[]{:S(2)}, u32[]{:S(2)}) %collective-permute-start.7) | collective-permute-done | bytes 147488 | tf_op jit(solution)/shard_map/ppermute | solution.py:121
  129.1 4.1 %collective-permute-done.9 = bf16[96,1024]{1,0:T(8,128)(2,1)S(1)} collective-permute-done((bf16[96,1024]{1,0:T(8,128)(2,1)S(1)}, bf16[96,1024]{1,0:T(8,128)(2,1)S(1)}, u32[]{:S(2)}, u32[]{:S(2)}) %collective-permute-start.9) | collective-permute-done | bytes 196640 | tf_op jit(solution)/shard_map/ppermute | solution.py:121
  133.2 0.8 fusion.44
  (60 shorter events, 9.5 us)
Async XLA Ops:
  0.0 94.9 %copy-start = (bf16[3,128,128]{2,1,0:T(8,128)(2,1)S(1)}, bf16[3,128,128]{2,1,0:T(8,128)(2,1)}, u32[]{:S(2)}) copy-start(bf16[3,128,128]{2,1,0:T(8,128)(2,1)} %param.16) | copy-start | bytes 294916
  5.0 15.3 %copy-start.3 = (f32[6,384]{1,0:T(8,128)S(1)}, f32[6,384]{1,0:T(8,128)}, u32[]{:S(2)}) copy-start(f32[6,384]{1,0:T(8,128)} %param.18) | copy-start | bytes 27652
  5.0 53.2 %all-to-all-start = ((bf16[64,2,3,16,128]{4,3,2,1,0:T(8,128)(2,1)}), bf16[64,2,3,16,128]{4,3,2,1,0:T(8,128)(2,1)S(1)}, u32[]{:S(2)}, u32[]{:S(2)}) async-start(bf16[64,2,3,16,128]{4,3,2,1,0:T(8,128)(2,1)} %shard_map.100), calls=%async_computation | async-start | bytes 3145728 | tf_op jit(solution)/shard_map/all_to_all | solution.py:91
  62.7 9.8 %copy-start.4 = (bf16[128,3,3]{0,2,1:T(4,128)(2,1)S(1)}, bf16[128,3,3]{0,2,1:T(4,128)(2,1)}, u32[]{:S(2)}) copy-start(bf16[128,3,3]{0,2,1:T(4,128)(2,1)} %param.17) | copy-start | bytes 6916
  63.6 30.1 %all-to-all-start.1 = ((bf16[64,3,16,128]{3,2,1,0:T(8,128)(2,1)}), bf16[64,3,16,128]{3,2,1,0:T(8,128)(2,1)S(1)}, u32[]{:S(2)}, u32[]{:S(2)}) async-start(bf16[64,3,16,128]{3,2,1,0:T(8,128)(2,1)} %bitcast.15), calls=%async_computation.1 | async-start | bytes 1572864 | tf_op jit(solution)/shard_map/all_to_all | solution.py:58
  94.9 1.1 copy-start.1
  107.7 6.3 %collective-permute-start = (bf16[2,96,768]{2,1,0:T(8,128)(2,1)S(1)}, bf16[2,96,768]{2,1,0:T(8,128)(2,1)S(1)}, u32[]{:S(2)}, u32[]{:S(2)}) collective-permute-start(bf16[2,96,768]{2,1,0:T(8,128)(2,1)S(1)} %fusion.28), channel_id=1, source_target_pairs={{0,1},{1,0},{2,3},{3,2},{4,5},{5,4},{6,7},{7,6},{8,9},{9,8},{10,11... | collective-permute-start | bytes 884744 | tf_op jit(solution)/shard_map/ppermute | solution.py:121
  112.3 2.2 %collective-permute-start.2 = (bf16[2,96,768]{2,1,0:T(8,128)(2,1)S(1)}, bf16[2,96,768]{2,1,0:T(8,128)(2,1)S(1)}, u32[]{:S(2)}, u32[]{:S(2)}) collective-permute-start(bf16[2,96,768]{2,1,0:T(8,128)(2,1)S(1)} %fusion.29), channel_id=1, source_target_pairs={{0,1},{1,0},{2,3},{3,2},{4,5},{5,4},{6,7},{7,6},{8,9},{9,8},{10,11... | collective-permute-start | bytes 884744 | tf_op jit(solution)/shard_map/ppermute | solution.py:121
  112.7 3.1 %collective-permute-start.4 = (bf16[2,96,768]{2,1,0:T(8,128)(2,1)S(1)}, bf16[2,96,768]{2,1,0:T(8,128)(2,1)S(1)}, u32[]{:S(2)}, u32[]{:S(2)}) collective-permute-start(bf16[2,96,768]{2,1,0:T(8,128)(2,1)S(1)} %fusion.30), channel_id=1, source_target_pairs={{0,1},{1,0},{2,3},{3,2},{4,5},{5,4},{6,7},{7,6},{8,9},{9,8},{10,11... | collective-permute-start | bytes 884744 | tf_op jit(solution)/shard_map/ppermute | solution.py:121
  113.3 3.0 %collective-permute-start.6 = (bf16[2,96,768]{2,1,0:T(8,128)(2,1)S(1)}, bf16[2,96,768]{2,1,0:T(8,128)(2,1)S(1)}, u32[]{:S(2)}, u32[]{:S(2)}) collective-permute-start(bf16[2,96,768]{2,1,0:T(8,128)(2,1)S(1)} %fusion.31), channel_id=1, source_target_pairs={{0,1},{1,0},{2,3},{3,2},{4,5},{5,4},{6,7},{7,6},{8,9},{9,8},{10,11... | collective-permute-start | bytes 884744 | tf_op jit(solution)/shard_map/ppermute | solution.py:121
  113.4 4.0 %collective-permute-start.8 = (bf16[2,96,1024]{2,1,0:T(8,128)(2,1)S(1)}, bf16[2,96,1024]{2,1,0:T(8,128)(2,1)S(1)}, u32[]{:S(2)}, u32[]{:S(2)}) collective-permute-start(bf16[2,96,1024]{2,1,0:T(8,128)(2,1)S(1)} %fusion.24), channel_id=1, source_target_pairs={{0,1},{1,0},{2,3},{3,2},{4,5},{5,4},{6,7},{7,6},{8,9},{9,8},{10,11... | collective-permute-start | bytes 1179656 | tf_op jit(solution)/shard_map/ppermute | solution.py:121
  114.0 5.5 %collective-permute-start.1 = (bf16[96,768]{1,0:T(8,128)(2,1)S(1)}, bf16[96,768]{1,0:T(8,128)(2,1)S(1)}, u32[]{:S(2)}, u32[]{:S(2)}) collective-permute-start(bf16[96,768]{1,0:T(8,128)(2,1)S(1)} %fusion.41), channel_id=1, source_target_pairs={{0,2},{1,3},{2,0},{3,1},{4,6},{5,7},{6,4},{7,5},{8,10},{9,11},{10,... | collective-permute-start | bytes 442376 | tf_op jit(solution)/shard_map/ppermute | solution.py:121
  114.6 8.1 %collective-permute-start.3 = (bf16[96,768]{1,0:T(8,128)(2,1)S(1)}, bf16[96,768]{1,0:T(8,128)(2,1)S(1)}, u32[]{:S(2)}, u32[]{:S(2)}) collective-permute-start(bf16[96,768]{1,0:T(8,128)(2,1)S(1)} %fusion.38), channel_id=1, source_target_pairs={{0,2},{1,3},{2,0},{3,1},{4,6},{5,7},{6,4},{7,5},{8,10},{9,11},{10,... | collective-permute-start | bytes 442376 | tf_op jit(solution)/shard_map/ppermute | solution.py:121
  115.8 10.1 %collective-permute-start.5 = (bf16[96,768]{1,0:T(8,128)(2,1)S(1)}, bf16[96,768]{1,0:T(8,128)(2,1)S(1)}, u32[]{:S(2)}, u32[]{:S(2)}) collective-permute-start(bf16[96,768]{1,0:T(8,128)(2,1)S(1)} %fusion.35), channel_id=1, source_target_pairs={{0,2},{1,3},{2,0},{3,1},{4,6},{5,7},{6,4},{7,5},{8,10},{9,11},{10,... | collective-permute-start | bytes 442376 | tf_op jit(solution)/shard_map/ppermute | solution.py:121
  116.3 12.7 %collective-permute-start.7 = (bf16[96,768]{1,0:T(8,128)(2,1)S(1)}, bf16[96,768]{1,0:T(8,128)(2,1)S(1)}, u32[]{:S(2)}, u32[]{:S(2)}) collective-permute-start(bf16[96,768]{1,0:T(8,128)(2,1)S(1)} %fusion.32), channel_id=1, source_target_pairs={{0,2},{1,3},{2,0},{3,1},{4,6},{5,7},{6,4},{7,5},{8,10},{9,11},{10,... | collective-permute-start | bytes 442376 | tf_op jit(solution)/shard_map/ppermute | solution.py:121
  117.5 15.7 %collective-permute-start.9 = (bf16[96,1024]{1,0:T(8,128)(2,1)S(1)}, bf16[96,1024]{1,0:T(8,128)(2,1)S(1)}, u32[]{:S(2)}, u32[]{:S(2)}) collective-permute-start(bf16[96,1024]{1,0:T(8,128)(2,1)S(1)} %fusion.25), channel_id=1, source_target_pairs={{0,2},{1,3},{2,0},{3,1},{4,6},{5,7},{6,4},{7,5},{8,10},{9,11},{10,... | collective-permute-start | bytes 589832 | tf_op jit(solution)/shard_map/ppermute | solution.py:121
  129.0 4.2 %copy-start.2 = (bf16[96,4096]{1,0:T(8,128)(2,1)}, bf16[96,4096]{1,0:T(8,128)(2,1)S(1)}, u32[]{:S(2)}) copy-start(bf16[96,4096]{1,0:T(8,128)(2,1)S(1)} %fusion.48) | copy-start | bytes 2359300
